TPU v7x, 128 devices: a whole 4x4x4 slice. The times are simulated.
128 devices in a mesh: req: 8 (over y, core), exp: 16 (over z, x).
Axes of the slice: x: 4, y: 4, z: 4, core: 2. Of those that a mesh axis runs over, the one named last changes fastest.
Arguments:
- queries: bfloat16 [128, 64, 2048], P('req', None, 'exp'), may hold values from -42 to 42
- new_keys: bfloat16 [128, 64, 2048], P('req', None, 'exp'), may hold values from -6 to 6
- new_values: bfloat16 [128, 64, 2048], P('req', None, 'exp'), may hold values from -6 to 6
- long_keys: bfloat16 [8, 16384, 2048], P('req', None, 'exp'), may hold values from -18 to 18
- long_values: bfloat16 [8, 16384, 2048], P('req', None, 'exp'), may hold values from -6 to 6
- long_lengths: int32 [8], P('req'), may hold values from 4096 to 16384
- short_keys: bfloat16 [120, 1024, 2048], P('req', None, 'exp'), may hold values from -18 to 18
- short_values: bfloat16 [120, 1024, 2048], P('req', None, 'exp'), may hold values from -6 to 6
- short_lengths: int32 [120], P('req'), may hold values from 256 to 1024
- parents: int32 [128, 64], P('req'), may hold values from 0 to 62, as said below
- accepted: int32 [128], P('req'), may hold values from 0 to 63
- residual: float32 [8192, 2048], P(('req', 'exp')), may hold values from -18 to 18
- out_weight: bfloat16 [2048, 2048], P('exp'), may hold values from -2 to 2
- norm_gain: float32 [2048], replicated, may hold values from 0.5 to 1.5
- routes: int32 [8192, 8], P(('req', 'exp')), may hold values from 0 to 63, all different within a row; in each aligned block of 64 rows (0 to 63, 64 to 127, ...) at most 16 rows name the same one
- route_weights: float32 [8192, 8], P(('req', 'exp')), may hold values from 0.05 to 0.4
- expert_gate: bfloat16 [128, 2048, 512], P(('req', 'exp')), may hold values from -0.125 to 0.125
- expert_up: bfloat16 [128, 2048, 512], P(('req', 'exp')), may hold values from -0.125 to 0.125
- expert_down: bfloat16 [128, 512, 2048], P(('req', 'exp')), may hold values from -0.1875 to 0.1875
Outputs:
- hidden_out: bfloat16 [8192, 2048], P(('req', 'exp'))
- accepted_keys: bfloat16 [128, 64, 2048], P('req', None, 'exp')
- accepted_values: bfloat16 [128, 64, 2048], P('req', None, 'exp')
Inputs may be any that keep to these rules, and one draw needn't show every extreme that they name: parents[r, 0] = 0 (the root); for t >= 1, parents[r, t] < t. `routes`: each row names 8 different experts; within the 64 rows of one device (aligned blocks) no expert is named by more than 16 rows.
All inputs are finite; a program needn't handle non-finite values.
Results may differ from a plain program's by a relative error of at most 0.02.
Values may be sent and summed in bfloat16 or wider, within the bound.
No kernel may reach another device: no remote copies, remote signals or barrier semaphores. Data moves between devices by JAX's collectives and lax.ppermute only.
A program may use at most 128 MiB of HBM per device.

v0:
```python
import jax
import jax.numpy as jnp
from jax import lax
from jax.sharding import PartitionSpec as P

HEAD = 128
EXPERTS = 64


def ancestors(parents):
    tokens_per = parents.shape[1]
    position = jnp.arange(tokens_per, dtype=jnp.int32)
    identity = (position[:, None] == position[None, :]).astype(jnp.float32)
    linked = (parents[:, :, None] == position[None, None, :]) & (position[None, :, None] > 0)
    reached = jnp.maximum(identity[None], linked.astype(jnp.float32))
    for rounds in range(tokens_per.bit_length()):
        reached = jnp.minimum(
            jnp.einsum("bij,bjk->bik", reached, reached, precision=lax.Precision.HIGHEST), 1.0
        )
    return reached


def compact_path(reached, accepted, stacked):
    tokens_per = reached.shape[1]
    position = jnp.arange(tokens_per, dtype=jnp.int32)
    levels = jnp.sum(reached, axis=2) - 1.0
    leaf_row = (accepted[:, None] == position[None, :]).astype(jnp.float32)
    on_path = jnp.einsum("bi,bij->bj", leaf_row, reached, precision=lax.Precision.HIGHEST)
    chooser = on_path[:, None, :] * (
        levels[:, None, :] == position[None, :, None].astype(jnp.float32)
    ).astype(jnp.float32)
    return jnp.einsum(
        "btj,bjc->btc", chooser.astype(jnp.bfloat16), stacked, preferred_element_type=jnp.float32
    ).astype(jnp.bfloat16)


def attend(queries, cache_keys, cache_values, lengths, new_keys, new_values, reached):
    batch, tokens_per, width = queries.shape
    heads = width // HEAD
    scale = HEAD ** (-0.5)
    shape_q = (batch, tokens_per, heads, HEAD)
    shape_c = (batch, cache_keys.shape[1], heads, HEAD)
    query_four = queries.reshape(shape_q)
    cache_scores = (
        jnp.einsum(
            "bthe,blhe->bhtl",
            query_four,
            cache_keys.reshape(shape_c),
            preferred_element_type=jnp.float32,
        )
        * scale
    )
    valid = jnp.arange(cache_keys.shape[1], dtype=jnp.int32)[None, :] < lengths[:, None]
    cache_scores = jnp.where(valid[:, None, None, :], cache_scores, -jnp.inf)
    draft_scores = (
        jnp.einsum(
            "bthe,bshe->bhts",
            query_four,
            new_keys.reshape(shape_q),
            preferred_element_type=jnp.float32,
        )
        * scale
    )
    draft_scores = jnp.where(reached[:, None] > 0.5, draft_scores, -jnp.inf)
    highest = jnp.maximum(jnp.max(cache_scores, axis=3), jnp.max(draft_scores, axis=3))
    cache_probs = jnp.exp(cache_scores - highest[..., None])
    draft_probs = jnp.exp(draft_scores - highest[..., None])
    totals = jnp.sum(cache_probs, axis=3) + jnp.sum(draft_probs, axis=3)
    mixed = jnp.einsum(
        "bhtl,blhe->bthe",
        cache_probs.astype(jnp.bfloat16),
        cache_values.reshape(shape_c),
        preferred_element_type=jnp.float32,
    )
    mixed = mixed + jnp.einsum(
        "bhts,bshe->bthe",
        draft_probs.astype(jnp.bfloat16),
        new_values.reshape(shape_q),
        preferred_element_type=jnp.float32,
    )
    mixed = mixed / jnp.transpose(totals, (0, 2, 1))[..., None]
    return mixed.reshape(batch, tokens_per, width).astype(jnp.bfloat16)


def expert_rows(rows, expert_gate, expert_up, expert_down):
    gate_part = jnp.dot(rows, expert_gate, preferred_element_type=jnp.float32)
    up_part = jnp.dot(rows, expert_up, preferred_element_type=jnp.float32)
    activation = (jax.nn.silu(gate_part) * up_part).astype(jnp.bfloat16)
    return jnp.dot(activation, expert_down, preferred_element_type=jnp.float32).astype(jnp.bfloat16)


def per_device(
    queries,
    new_keys,
    new_values,
    long_keys,
    long_values,
    long_lengths,
    short_keys,
    short_values,
    short_lengths,
    parents,
    accepted,
    residual,
    out_weight,
    norm_gain,
    routes,
    route_weights,
    expert_gate,
    expert_up,
    expert_down,
):
    reached = ancestors(parents)
    head_width = new_keys.shape[2]
    stacked = jnp.concatenate([new_keys, new_values], axis=2)
    compacted = compact_path(reached, accepted, stacked)
    accepted_keys = compacted[:, :, :head_width]
    accepted_values = compacted[:, :, head_width:]
    long_out = attend(
        queries[:1], long_keys, long_values, long_lengths, new_keys[:1], new_values[:1], reached[:1]
    )
    short_out = attend(
        queries[1:],
        short_keys,
        short_values,
        short_lengths,
        new_keys[1:],
        new_values[1:],
        reached[1:],
    )
    attended = jnp.concatenate([long_out, short_out], axis=0).reshape(-1, head_width)
    n_exp = lax.axis_size("exp")
    model_width = out_weight.shape[1]
    partial = jnp.dot(attended, out_weight, preferred_element_type=jnp.float32).astype(jnp.bfloat16)
    partial = partial.reshape(n_exp, -1, model_width)
    gathered = lax.all_to_all(partial, "exp", split_axis=0, concat_axis=0, tiled=True)
    attn_proj = jnp.sum(gathered.astype(jnp.float32), axis=0)
    middle = residual + attn_proj
    normed = (
        middle * lax.rsqrt(jnp.mean(middle * middle, axis=1, keepdims=True) + 1e-05) * norm_gain
    ).astype(jnp.bfloat16)
    tok_rows, top_count = routes.shape
    devices = lax.axis_size("req") * lax.axis_size("exp")
    pieces = max(1, devices // EXPERTS)
    capacity = 2 * tok_rows * top_count // EXPERTS
    flat_routes = routes.reshape(-1)
    flat_count = flat_routes.shape[0]
    expert_ids = jnp.arange(EXPERTS, dtype=jnp.int32)
    onehot = (flat_routes[:, None] == expert_ids[None, :]).astype(jnp.float32)
    flat_ids = jnp.arange(flat_count, dtype=jnp.int32)
    earlier = (flat_ids[:, None] > flat_ids[None, :]).astype(jnp.float32)
    before = jnp.dot(earlier, onehot, precision=lax.Precision.HIGHEST)
    slot_index = jnp.sum(before * onehot, axis=1).astype(jnp.int32).reshape(tok_rows, top_count)
    target = routes * capacity + slot_index
    columns = jnp.arange(EXPERTS * pieces * capacity, dtype=jnp.int32)
    column_target = (columns // (pieces * capacity)) * capacity + columns % capacity
    hits = target[:, :, None] == column_target[None, None, :]
    placement = jnp.any(hits, axis=1).astype(jnp.bfloat16)
    packed = jnp.einsum("tc,td->cd", placement, normed, preferred_element_type=jnp.float32).astype(
        jnp.bfloat16
    )
    outgoing = packed.reshape(devices, capacity, model_width)
    received = lax.all_to_all(outgoing, ("req", "exp"), split_axis=0, concat_axis=0, tiled=True)
    produced = expert_rows(
        received.reshape(-1, model_width), expert_gate[0], expert_up[0], expert_down[0]
    ).reshape(devices, capacity, model_width)
    returned = lax.all_to_all(produced, ("req", "exp"), split_axis=0, concat_axis=0, tiled=True)
    chooser = hits.reshape(tok_rows * top_count, -1).astype(jnp.bfloat16)
    expert_out = jnp.dot(
        chooser, returned.reshape(-1, model_width), preferred_element_type=jnp.float32
    ).reshape(tok_rows, top_count, model_width)
    moe = jnp.sum(route_weights[:, :, None] * expert_out, axis=1)
    hidden_out = (middle + moe).astype(jnp.bfloat16)
    return (hidden_out, accepted_keys, accepted_values)


def solution(mesh):
    in_specs = (
        P("req", None, "exp"),
        P("req", None, "exp"),
        P("req", None, "exp"),
        P("req", None, "exp"),
        P("req", None, "exp"),
        P("req"),
        P("req", None, "exp"),
        P("req", None, "exp"),
        P("req"),
        P("req", None),
        P("req"),
        P(("req", "exp"), None),
        P("exp", None),
        P(),
        P(("req", "exp"), None),
        P(("req", "exp"), None),
        P(("req", "exp"), None, None),
        P(("req", "exp"), None, None),
        P(("req", "exp"), None, None),
    )
    out_specs = (P(("req", "exp"), None), P("req", None, "exp"), P("req", None, "exp"))
    return jax.shard_map(
        per_device, mesh=mesh, in_specs=in_specs, out_specs=out_specs, check_vma=False
    )
```

profile of v0, /device:TPU:60, one launch (start us, length us, event | category | flops | bytes accessed | tf_op | source)
XLA Modules:
  0.0 345.7 jit_solution(8209755982448152997)
XLA Ops:
  0.7 1.7 convolution_minimum_fusion.6
  7.3 1.6 fusion.8
  8.9 1.0 fusion.11
  11.0 1.2 fusion.21
  13.2 1.7 fusion.94
  15.1 0.8 fusion.6
  15.9 1.2 copy-done.2
  17.1 1.1 fusion.3
  18.9 3.2 convolution_convert_fusion.2
  22.2 8.0 %all-to-all-start = ((bf16[16,64,2048]{2,1,0:T(8,128)(2,1)}), bf16[16,64,2048]{2,1,0:T(8,128)(2,1)}, u32[]{:S(2)}, u32[]{:S(2)}) async-start(bf16[16,64,2048]{2,1,0:T(8,128)(2,1)} %bitcast.105), calls=%async_computation | async-start | bytes 8388608 | tf_op jit(solution)/shard_map/all_to_all | solution.py:136
  30.9 1.9 compare_reduce_fusion
  32.8 54.4 %all-to-all-done = bf16[16,64,2048]{2,1,0:T(8,128)(2,1)} async-done(((bf16[16,64,2048]{2,1,0:T(8,128)(2,1)}), bf16[16,64,2048]{2,1,0:T(8,128)(2,1)}, u32[]{:S(2)}, u32[]{:S(2)}) %all-to-all-start) | async-done | bytes 4194336 | tf_op jit(solution)/shard_map/all_to_all | solution.py:136
  87.2 3.0 convert_reduce_fusion
  90.2 1.2 multiply_reduce_fusion.1
  91.5 2.4 convolution_convert_fusion.1
  93.9 106.0 %all_to_all.15 = bf16[128,16,2048]{2,1,0:T(8,128)(2,1)S(1)} all-to-all(bf16[128,16,2048]{2,1,0:T(8,128)(2,1)S(1)} %bitcast.104), channel_id=1, replica_groups=mesh['req'=8,'exp'=16] {'req','exp'}, dimensions={0} | all-to-all | bytes 16777216 | tf_op jit(solution)/shard_map/all_to_all | solution.py:163
  199.9 4.5 %fusion.16 = f32[2048,512]{1,0:T(8,128)S(1)} fusion(bf16[2048,2048]{1,0:T(8,128)(2,1)S(1)} %bitcast.107, bf16[1,2048,512]{2,1,0:T(8,128)(2,1)S(1)} %copy-done.14), kind=kOutput, calls=%fused_computation.24 | convolution fusion | flops 4294967296 | bytes 14680064 | tf_op jit(solution)/shard_map/dot_general | solution.py:86
  204.5 5.1 %multiply_convert_fusion = bf16[2048,512]{1,0:T(8,128)(2,1)S(1)} fusion(f32[2048,512]{1,0:T(8,128)S(1)} %fusion.16, bf16[2048,2048]{1,0:T(8,128)(2,1)S(1)} %bitcast.108, bf16[1,2048,512]{2,1,0:T(8,128)(2,1)S(1)} %copy-done.15), kind=kOutput, calls=%fused_computation.12 | convolution fusion | flops 4301258752 | bytes 16777216 | tf_op jit(solution)/shard_map/dot_general | solution.py:87
  209.6 6.7 %convolution_convert_fusion = bf16[2048,2048]{1,0:T(8,128)(2,1)} fusion(bf16[2048,512]{1,0:T(8,128)(2,1)S(1)} %multiply_convert_fusion, bf16[1,512,2048]{2,1,0:T(8,128)(2,1)S(1)} %copy-done), kind=kOutput, calls=%fused_computation.3 | convolution fusion | flops 4299161600 | bytes 12582912 | tf_op jit(solution)/shard_map/dot_general | solution.py:89
  216.4 9.0 %all-to-all-start.2 = ((bf16[128,16,2048]{2,1,0:T(8,128)(2,1)}), bf16[128,16,2048]{2,1,0:T(8,128)(2,1)}, u32[]{:S(2)}, u32[]{:S(2)}) async-start(bf16[128,16,2048]{2,1,0:T(8,128)(2,1)} %bitcast.106), calls=%async_computation.2 | async-start | bytes 16777216 | tf_op jit(solution)/shard_map/all_to_all | solution.py:167
  225.9 1.3 convolution_convert_fusion.3
  227.2 0.9 fusion.92
  228.2 107.7 %all-to-all-done.2 = bf16[128,16,2048]{2,1,0:T(8,128)(2,1)} async-done(((bf16[128,16,2048]{2,1,0:T(8,128)(2,1)}), bf16[128,16,2048]{2,1,0:T(8,128)(2,1)}, u32[]{:S(2)}, u32[]{:S(2)}) %all-to-all-start.2) | async-done | bytes 8388640 | tf_op jit(solution)/shard_map/all_to_all | solution.py:167
  335.9 9.0 %multiply_reduce_fusion = f32[64,2048]{1,0:T(8,128)S(1)} fusion(bf16[2048,2048,1]{1,0,2:T(8,128)(2,1)} %bitcast.24, s32[2048]{0:T(1024)S(1)} %fusion.82, s32[64,8]{1,0:T(8,128)S(1)} %copy.39, f32[64,8]{1,0:T(8,128)S(1)} %copy.36), kind=kOutput, calls=%fused_computation.11 | convolution fusion | flops 4297981952 | bytes 8925184 | tf_op jit(solution)/shard_map/dot_general | solution.py:169
  (70 shorter events, 9.1 us)
Async XLA Ops:
  0.6 209.0 %copy-start = (bf16[1,512,2048]{2,1,0:T(8,128)(2,1)S(1)}, bf16[1,512,2048]{2,1,0:T(8,128)(2,1)}, u32[]{:S(2)}) copy-start(bf16[1,512,2048]{2,1,0:T(8,128)(2,1)} %param.37) | copy-start | bytes 6291460
  3.1 3.5 %copy-start.6 = (bf16[16,64,128]{2,1,0:T(8,128)(2,1)S(1)}, bf16[16,64,128]{2,1,0:T(8,128)(2,1)}, u32[]{:S(2)}) copy-start(bf16[16,64,128]{2,1,0:T(8,128)(2,1)} %param.19) | copy-start | bytes 786436
  3.1 3.5 %copy-start.8 = (bf16[16,64,128]{2,1,0:T(8,128)(2,1)S(1)}, bf16[16,64,128]{2,1,0:T(8,128)(2,1)}, u32[]{:S(2)}) copy-start(bf16[16,64,128]{2,1,0:T(8,128)(2,1)} %param.20) | copy-start | bytes 786436
  4.4 2.8 copy-start.10
  4.4 2.8 copy-start.12
  8.9 2.1 copy-start.13
  11.0 2.2 copy-start.1
  14.9 2.2 copy-start.2
  17.0 1.1 copy-start.16
  17.1 1.9 copy-start.3
  22.2 8.0 %copy-start.4 = (s32[64,8]{0,1:T(8,128)S(1)}, s32[64,8]{0,1:T(8,128)}, u32[]{:S(2)}) copy-start(s32[64,8]{0,1:T(8,128)} %param.33) | copy-start | bytes 6148
  22.2 65.0 %all-to-all-start = ((bf16[16,64,2048]{2,1,0:T(8,128)(2,1)}), bf16[16,64,2048]{2,1,0:T(8,128)(2,1)}, u32[]{:S(2)}, u32[]{:S(2)}) async-start(bf16[16,64,2048]{2,1,0:T(8,128)(2,1)} %bitcast.105), calls=%async_computation | async-start | bytes 8388608 | tf_op jit(solution)/shard_map/all_to_all | solution.py:136
  30.1 61.3 %copy-start.5 = (f32[2048]{0:T(1024)S(1)}, f32[2048]{0:T(1024)}, u32[]{:S(2)}) copy-start(f32[2048]{0:T(1024)} %param.32) | copy-start | bytes 24580
  93.9 106.0 %copy-start.14 = (bf16[1,2048,512]{2,1,0:T(8,128)(2,1)S(1)}, bf16[1,2048,512]{2,1,0:T(8,128)(2,1)}, u32[]{:S(2)}) copy-start(bf16[1,2048,512]{2,1,0:T(8,128)(2,1)} %param.35) | copy-start | bytes 6291460
  199.9 4.5 %copy-start.15 = (bf16[1,2048,512]{2,1,0:T(8,128)(2,1)S(1)}, bf16[1,2048,512]{2,1,0:T(8,128)(2,1)}, u32[]{:S(2)}) copy-start(bf16[1,2048,512]{2,1,0:T(8,128)(2,1)} %param.36) | copy-start | bytes 6291460
  216.3 9.0 %copy-start.7 = (f32[64,8]{0,1:T(8,128)S(1)}, f32[64,8]{0,1:T(8,128)}, u32[]{:S(2)}) copy-start(f32[64,8]{0,1:T(8,128)} %param.34) | copy-start | bytes 6148
  216.4 9.1 %copy-start.11 = (s32[16]{0:T(128)S(1)}, s32[16]{0:T(128)}, u32[]{:S(2)}) copy-start(s32[16]{0:T(128)} %param.29) | copy-start | bytes 196
  216.4 9.6 %copy-start.9 = (bf16[16,64,128]{2,1,0:T(8,128)(2,1)S(1)}, bf16[16,64,128]{2,1,0:T(8,128)(2,1)}, u32[]{:S(2)}) copy-start(bf16[16,64,128]{2,1,0:T(8,128)(2,1)} %param.20) | copy-start | bytes 786436
  216.4 119.6 %all-to-all-start.2 = ((bf16[128,16,2048]{2,1,0:T(8,128)(2,1)}), bf16[128,16,2048]{2,1,0:T(8,128)(2,1)}, u32[]{:S(2)}, u32[]{:S(2)}) async-start(bf16[128,16,2048]{2,1,0:T(8,128)(2,1)} %bitcast.106), calls=%async_computation.2 | async-start | bytes 16777216 | tf_op jit(solution)/shard_map/all_to_all | solution.py:167
where the time goes:
time: 346 us
  waiting for transfers between devices  162 us (47%)
  blocking collectives  106 us (31%)
  matrix products  45.5 us (13%)
  starting transfers between devices  17 us (5%)
  other arithmetic  9.55 us (3%)
  local copies, waits for them, and re-layouts  3.61 us (1%)
    all_to_all x1, waiting for transfers between devices, per_device(): lax.all_to_all(produced, ('req', 'exp'), split_axis=0, concat_axis=0, til...  108 us
    all_to_all x1, blocking collectives, per_device(): lax.all_to_all(outgoing, ('req', 'exp'), split_axis=0, concat_axis=0, til...  106 us
    all_to_all x1, waiting for transfers between devices, per_device(): lax.all_to_all(partial, 'exp', split_axis=0, concat_axis=0, tiled=True)  54.4 us
    all_to_all x1, starting transfers between devices, per_device(): lax.all_to_all(produced, ('req', 'exp'), split_axis=0, concat_axis=0, til...  9.02 us
    dot_general x1, matrix products, per_device(): jnp.dot(chooser, returned.reshape(-1, model_width), preferred_element_typ...  8.99 us
    all_to_all x1, starting transfers between devices, per_device(): lax.all_to_all(partial, 'exp', split_axis=0, concat_axis=0, tiled=True)  7.98 us
  transfers between devices with their start and end apart: 2, of which 2 were waited for; matrix products, arithmetic and copies ran while one was open for 2% of the time, Pallas kernels for 0%

commit v1 on v0

--- a/solution.py
+++ b/solution.py
@@ -14,8 +14,9 @@
     linked = (parents[:, :, None] == position[None, None, :]) & (position[None, :, None] > 0)
     reached = jnp.maximum(identity[None], linked.astype(jnp.float32))
     for rounds in range(tokens_per.bit_length()):
+        squared = reached.astype(jnp.bfloat16)
         reached = jnp.minimum(
-            jnp.einsum("bij,bjk->bik", reached, reached, precision=lax.Precision.HIGHEST), 1.0
+            jnp.einsum("bij,bjk->bik", squared, squared, preferred_element_type=jnp.float32), 1.0
         )
     return reached
 
@@ -25,7 +26,12 @@
     position = jnp.arange(tokens_per, dtype=jnp.int32)
     levels = jnp.sum(reached, axis=2) - 1.0
     leaf_row = (accepted[:, None] == position[None, :]).astype(jnp.float32)
-    on_path = jnp.einsum("bi,bij->bj", leaf_row, reached, precision=lax.Precision.HIGHEST)
+    on_path = jnp.einsum(
+        "bi,bij->bj",
+        leaf_row.astype(jnp.bfloat16),
+        reached.astype(jnp.bfloat16),
+        preferred_element_type=jnp.float32,
+    )
     chooser = on_path[:, None, :] * (
         levels[:, None, :] == position[None, :, None].astype(jnp.float32)
     ).astype(jnp.float32)
@@ -131,10 +137,17 @@
     attended = jnp.concatenate([long_out, short_out], axis=0).reshape(-1, head_width)
     n_exp = lax.axis_size("exp")
     model_width = out_weight.shape[1]
-    partial = jnp.dot(attended, out_weight, preferred_element_type=jnp.float32).astype(jnp.bfloat16)
-    partial = partial.reshape(n_exp, -1, model_width)
-    gathered = lax.all_to_all(partial, "exp", split_axis=0, concat_axis=0, tiled=True)
-    attn_proj = jnp.sum(gathered.astype(jnp.float32), axis=0)
+    split = model_width // 2
+    swapped = jnp.dot(attended, out_weight[:, :split], preferred_element_type=jnp.float32)
+    reduced = jnp.dot(attended, out_weight[:, split:], preferred_element_type=jnp.float32)
+    reduced = lax.psum_scatter(
+        reduced.astype(jnp.bfloat16), "exp", scatter_dimension=0, tiled=True
+    )
+    swapped = swapped.astype(jnp.bfloat16).reshape(n_exp, -1, split)
+    gathered = lax.all_to_all(swapped, "exp", split_axis=0, concat_axis=0, tiled=True)
+    attn_proj = jnp.concatenate(
+        [jnp.sum(gathered.astype(jnp.float32), axis=0), reduced.astype(jnp.float32)], axis=1
+    )
     middle = residual + attn_proj
     normed = (
         middle * lax.rsqrt(jnp.mean(middle * middle, axis=1, keepdims=True) + 1e-05) * norm_gain
@@ -165,11 +178,15 @@
         received.reshape(-1, model_width), expert_gate[0], expert_up[0], expert_down[0]
     ).reshape(devices, capacity, model_width)
     returned = lax.all_to_all(produced, ("req", "exp"), split_axis=0, concat_axis=0, tiled=True)
-    chooser = hits.reshape(tok_rows * top_count, -1).astype(jnp.bfloat16)
-    expert_out = jnp.dot(
-        chooser, returned.reshape(-1, model_width), preferred_element_type=jnp.float32
-    ).reshape(tok_rows, top_count, model_width)
-    moe = jnp.sum(route_weights[:, :, None] * expert_out, axis=1)
+    weighing = jnp.sum(jnp.where(hits, route_weights[:, :, None], 0.0), axis=1)
+    terms = []
+    for _ in range(3):
+        term = weighing.astype(jnp.bfloat16)
+        terms.append(term)
+        weighing = weighing - term.astype(jnp.float32)
+    terms = jnp.concatenate(terms, axis=0)
+    moe = jnp.dot(terms, returned.reshape(-1, model_width), preferred_element_type=jnp.float32)
+    moe = jnp.sum(moe.reshape(3, tok_rows, model_width), axis=0)
     hidden_out = (middle + moe).astype(jnp.bfloat16)
     return (hidden_out, accepted_keys, accepted_values)
 

time: 346 us -> 373 us (1.078)
  waiting for transfers between devices: 162 us -> 181 us
  between operations: 1.79 us -> 15.2 us
  matrix products: 45.5 us -> 40.9 us
    reduce_scatter x0 -> x1, waiting for transfers between devices: none -> 48.3 us  [per_device(): lax.psum_scatter(reduced.astype(jnp.bfloat16), 'exp', scatter_dimension=0...]
    all_to_all x1, waiting for transfers between devices: 54.4 us -> 27.9 us  [per_device(): lax.all_to_all(swapped, 'exp', split_axis=0, concat_axis=0, tiled=True)]
    dot_general x10 -> x8, matrix products: 18.4 us -> 13.8 us  [the longest x1 5.48 us: per_device(): jnp.dot(terms, returned.reshape(-1, model_width), preferred_element_type=...]
  transfers between devices with their start and end apart: 2 -> 3, of which waited for: 2 -> 3; matrix products, arithmetic and copies ran while one was open for 2% -> 3% of each run, Pallas kernels for 0% -> 0%
where the time goes in v1:
time: 373 us; the launch traced here: 372 us
  waiting for transfers between devices  181 us (49%)
  blocking collectives  103 us (28%)
  matrix products  40.9 us (11%)
  starting transfers between devices  17 us (5%)
  between operations  15.2 us (4%)
  other arithmetic  10.8 us (3%)
  local copies, waits for them, and re-layouts  4.84 us (1%)
    all_to_all x1, waiting for transfers between devices, per_device(): lax.all_to_all(produced, ('req', 'exp'), split_axis=0, concat_axis=0, til...  104 us
    all_to_all x1, blocking collectives, per_device(): lax.all_to_all(outgoing, ('req', 'exp'), split_axis=0, concat_axis=0, til...  103 us
    reduce_scatter x1, waiting for transfers between devices, per_device(): lax.psum_scatter(reduced.astype(jnp.bfloat16), 'exp', scatter_dimension=0...  48.3 us
    all_to_all x1, waiting for transfers between devices, per_device(): lax.all_to_all(swapped, 'exp', split_axis=0, concat_axis=0, tiled=True)  27.9 us
    all_to_all x1, starting transfers between devices, per_device(): lax.all_to_all(produced, ('req', 'exp'), split_axis=0, concat_axis=0, til...  9.02 us
    all_to_all x1, starting transfers between devices, per_device(): lax.all_to_all(swapped, 'exp', split_axis=0, concat_axis=0, tiled=True)  7.97 us
  transfers between devices with their start and end apart: 3, of which 3 were waited for; matrix products, arithmetic and copies ran while one was open for 3% of the time, Pallas kernels for 0%

profile of v1, /device:TPU:60, one launch (start us, length us, event | category | flops | bytes accessed | tf_op | source)
XLA Modules:
  0.0 372.0 jit_solution(1849595228844362474)
XLA Ops:
  7.3 1.8 fusion.25
  12.3 1.6 fusion.7
  16.0 1.2 fusion.16
  18.2 1.7 fusion.106
  20.9 1.2 copy-done.3
  22.1 1.1 fusion.2
  23.8 2.0 convolution_convert_fusion.2
  25.8 2.0 convolution_convert_fusion.3
  27.9 8.0 %all-to-all-start = ((bf16[16,64,1024]{2,1,0:T(8,128)(2,1)}), bf16[16,64,1024]{2,1,0:T(8,128)(2,1)}, u32[]{:S(2)}, u32[]{:S(2)}) async-start(bf16[16,64,1024]{2,1,0:T(8,128)(2,1)} %bitcast.100), calls=%async_computation | async-start | bytes 4194304 | tf_op jit(solution)/shard_map/all_to_all | solution.py:147
  36.6 1.9 compare_reduce_fusion
  38.5 27.9 %all-to-all-done = bf16[16,64,1024]{2,1,0:T(8,128)(2,1)} async-done(((bf16[16,64,1024]{2,1,0:T(8,128)(2,1)}), bf16[16,64,1024]{2,1,0:T(8,128)(2,1)}, u32[]{:S(2)}, u32[]{:S(2)}) %all-to-all-start) | async-done | bytes 2097184 | tf_op jit(solution)/shard_map/all_to_all | solution.py:147
  66.4 2.0 convert_reduce_fusion
  68.4 48.3 %reduce-scatter.2.cloned.1.call-done = bf16[64,1024]{1,0:T(8,128)(2,1)} async-done(((bf16[1024,1024]{1,0:T(8,128)(2,1)}), bf16[64,1024]{1,0:T(8,128)(2,1)}) %reduce-scatter.2.cloned.1.call-update) | async-done | bytes 131088 | tf_op jit(solution)/shard_map/reduce_scatter | solution.py:143
  117.8 2.4 convolution_convert_fusion.1
  120.3 102.5 %all_to_all.15 = bf16[128,16,2048]{2,1,0:T(8,128)(2,1)S(1)} all-to-all(bf16[128,16,2048]{2,1,0:T(8,128)(2,1)S(1)} %bitcast.99), channel_id=1, replica_groups=mesh['req'=8,'exp'=16] {'req','exp'}, dimensions={0} | all-to-all | bytes 16777216 | tf_op jit(solution)/shard_map/all_to_all | solution.py:176
  222.8 4.5 %fusion.13 = f32[2048,512]{1,0:T(8,128)S(1)} fusion(bf16[2048,2048]{1,0:T(8,128)(2,1)S(1)} %bitcast.102, bf16[1,2048,512]{2,1,0:T(8,128)(2,1)S(1)} %copy-done.15), kind=kOutput, calls=%fused_computation.22 | convolution fusion | flops 4294967296 | bytes 14680064 | tf_op jit(solution)/shard_map/dot_general | solution.py:92
  227.3 5.2 %multiply_convert_fusion = bf16[2048,512]{1,0:T(8,128)(2,1)S(1)} fusion(f32[2048,512]{1,0:T(8,128)S(1)} %fusion.13, bf16[2048,2048]{1,0:T(8,128)(2,1)S(1)} %bitcast.103, bf16[1,2048,512]{2,1,0:T(8,128)(2,1)S(1)} %copy-done.16), kind=kOutput, calls=%fused_computation.10 | convolution fusion | flops 4301258752 | bytes 16777216 | tf_op jit(solution)/shard_map/dot_general | solution.py:93
  232.5 6.7 %convolution_convert_fusion = bf16[2048,2048]{1,0:T(8,128)(2,1)} fusion(bf16[2048,512]{1,0:T(8,128)(2,1)S(1)} %multiply_convert_fusion, bf16[1,512,2048]{2,1,0:T(8,128)(2,1)S(1)} %copy-done), kind=kOutput, calls=%fused_computation.2 | convolution fusion | flops 4299161600 | bytes 12582912 | tf_op jit(solution)/shard_map/dot_general | solution.py:95
  239.3 9.0 %all-to-all-start.2 = ((bf16[128,16,2048]{2,1,0:T(8,128)(2,1)}), bf16[128,16,2048]{2,1,0:T(8,128)(2,1)}, u32[]{:S(2)}, u32[]{:S(2)}) async-start(bf16[128,16,2048]{2,1,0:T(8,128)(2,1)} %bitcast.101), calls=%async_computation.3 | async-start | bytes 16777216 | tf_op jit(solution)/shard_map/all_to_all | solution.py:180
  248.4 1.3 fusion.1
  249.8 1.2 fusion.48
  251.0 1.4 convolution_convert_fusion.4
  254.4 104.4 %all-to-all-done.2 = bf16[128,16,2048]{2,1,0:T(8,128)(2,1)} async-done(((bf16[128,16,2048]{2,1,0:T(8,128)(2,1)}), bf16[128,16,2048]{2,1,0:T(8,128)(2,1)}, u32[]{:S(2)}, u32[]{:S(2)}) %all-to-all-start.2) | async-done | bytes 8388640 | tf_op jit(solution)/shard_map/all_to_all | solution.py:180
  358.8 5.5 %convolution_reduce_fusion = f32[64,2048]{1,0:T(8,128)S(1)} fusion(bf16[3,64,2048]{2,1,0:T(8,128)(2,1)} %bitcast.106, bf16[2048,2048,1]{1,0,2:T(8,128)(2,1)} %bitcast.25), kind=kOutput, calls=%fused_computation.32 | convolution fusion | flops 1610874880 | bytes 9699328 | tf_op jit(solution)/shard_map/dot_general | solution.py:188
  (77 shorter events, 12.0 us)
Async XLA Ops:
  7.2 225.3 %copy-start = (bf16[1,512,2048]{2,1,0:T(8,128)(2,1)S(1)}, bf16[1,512,2048]{2,1,0:T(8,128)(2,1)}, u32[]{:S(2)}) copy-start(bf16[1,512,2048]{2,1,0:T(8,128)(2,1)} %param.37) | copy-start | bytes 6291460
  7.2 3.2 copy-start.8
  7.2 3.2 copy-start.10
  7.2 4.0 %copy-start.11 = (s32[15]{0:T(128)S(1)}, s32[15]{0:T(128)}, u32[]{:S(2)}) copy-start(s32[15]{0:T(128)} %param.27) | copy-start | bytes 184
  7.2 109.5 %reduce-scatter.2.cloned.1.call-start = ((), (), s32[]{:S(2)}) async-start(), calls=%async_computation.4 | async-start | bytes 2228224 | tf_op jit(solution)/shard_map/reduce_scatter | solution.py:143
  10.0 2.3 copy-start.13
  10.4 0.8 copy-start.4
  13.9 2.1 copy-start.14
  16.0 2.2 copy-start.2
  19.9 2.2 copy-start.3
  22.1 1.1 copy-start.17
  22.1 1.7 copy-start.5
  25.8 10.0 %copy-start.6 = (s32[64,8]{0,1:T(8,128)S(1)}, s32[64,8]{0,1:T(8,128)}, u32[]{:S(2)}) copy-start(s32[64,8]{0,1:T(8,128)} %param.33) | copy-start | bytes 6148
  27.9 89.8 %copy-start.1 = (f32[64,2048]{1,0:T(8,128)S(1)}, f32[64,2048]{1,0:T(8,128)}, u32[]{:S(2)}) copy-start(f32[64,2048]{1,0:T(8,128)} %param.30) | copy-start | bytes 1572868
  27.9 90.0 %copy-start.7 = (f32[2048]{0:T(1024)S(1)}, f32[2048]{0:T(1024)}, u32[]{:S(2)}) copy-start(f32[2048]{0:T(1024)} %param.32) | copy-start | bytes 24580
  27.9 38.5 %all-to-all-start = ((bf16[16,64,1024]{2,1,0:T(8,128)(2,1)}), bf16[16,64,1024]{2,1,0:T(8,128)(2,1)}, u32[]{:S(2)}, u32[]{:S(2)}) async-start(bf16[16,64,1024]{2,1,0:T(8,128)(2,1)} %bitcast.100), calls=%async_computation | async-start | bytes 4194304 | tf_op jit(solution)/shard_map/all_to_all | solution.py:147
  120.3 102.5 %copy-start.15 = (bf16[1,2048,512]{2,1,0:T(8,128)(2,1)S(1)}, bf16[1,2048,512]{2,1,0:T(8,128)(2,1)}, u32[]{:S(2)}) copy-start(bf16[1,2048,512]{2,1,0:T(8,128)(2,1)} %param.35) | copy-start | bytes 6291460
  222.8 4.5 %copy-start.16 = (bf16[1,2048,512]{2,1,0:T(8,128)(2,1)S(1)}, bf16[1,2048,512]{2,1,0:T(8,128)(2,1)}, u32[]{:S(2)}) copy-start(bf16[1,2048,512]{2,1,0:T(8,128)(2,1)} %param.36) | copy-start | bytes 6291460
  239.2 9.0 %copy-start.9 = (f32[64,8]{0,1:T(8,128)S(1)}, f32[64,8]{0,1:T(8,128)}, u32[]{:S(2)}) copy-start(f32[64,8]{0,1:T(8,128)} %param.34) | copy-start | bytes 6148
  239.2 10.5 %copy-start.12 = (s32[16]{0:T(128)S(1)}, s32[16]{0:T(128)}, u32[]{:S(2)}) copy-start(s32[16]{0:T(128)} %param.29) | copy-start | bytes 196
  239.3 119.5 %all-to-all-start.2 = ((bf16[128,16,2048]{2,1,0:T(8,128)(2,1)}), bf16[128,16,2048]{2,1,0:T(8,128)(2,1)}, u32[]{:S(2)}, u32[]{:S(2)}) async-start(bf16[128,16,2048]{2,1,0:T(8,128)(2,1)} %bitcast.101), calls=%async_computation.3 | async-start | bytes 16777216 | tf_op jit(solution)/shard_map/all_to_all | solution.py:180
Sparse Core Ops, SparseCore 0:
  25.9 90.7 reduce-scatter.1

commit v2 on v1

--- a/solution.py
+++ b/solution.py
@@ -93,6 +93,53 @@
     up_part = jnp.dot(rows, expert_up, preferred_element_type=jnp.float32)
     activation = (jax.nn.silu(gate_part) * up_part).astype(jnp.bfloat16)
     return jnp.dot(activation, expert_down, preferred_element_type=jnp.float32).astype(jnp.bfloat16)
+
+
+def ring_exchange(blocks, axis, forward, backward, own):
+    ring = blocks.shape[0]
+    rows = blocks.shape[1]
+    half = rows // 2
+    pick = lambda step: lax.dynamic_index_in_dim(blocks, (own + step) % ring, 0, keepdims=False)
+    across = pick(2)
+    to_right = jnp.concatenate([pick(1), across[:half]], axis=0)
+    to_left = jnp.concatenate([pick(3), across[half:]], axis=0)
+    from_left = lax.ppermute(to_right, axis, forward)
+    from_right = lax.ppermute(to_left, axis, backward)
+    far_left = lax.ppermute(from_left[rows:], axis, forward)
+    far_right = lax.ppermute(from_right[rows:], axis, backward)
+    total = pick(0).astype(jnp.float32) + from_left[:rows].astype(jnp.float32)
+    total = total + from_right[:rows].astype(jnp.float32)
+    return total + jnp.concatenate([far_left, far_right], axis=0).astype(jnp.float32)
+
+
+def ring_reduce_scatter(attended, out_weight, n_exp):
+    side = 4
+    assert n_exp == side * side
+    index = lax.axis_index("exp")
+    z_pos, x_pos = index // side, index % side
+    cells = [(z, x) for z in range(side) for x in range(side)]
+    x_next = [(z * side + x, z * side + (x + 1) % side) for z, x in cells]
+    x_prev = [(z * side + x, z * side + (x - 1) % side) for z, x in cells]
+    z_next = [(z * side + x, ((z + 1) % side) * side + x) for z, x in cells]
+    z_prev = [(z * side + x, ((z - 1) % side) * side + x) for z, x in cells]
+    rows = attended.shape[0] // n_exp
+    width = out_weight.shape[1]
+    split = width // 2
+    grid = attended.reshape(side, side, rows, -1)
+    by_x = jnp.swapaxes(grid, 0, 1).reshape(n_exp * rows, -1)
+    first = jnp.dot(by_x, out_weight[:, :split], preferred_element_type=jnp.float32)
+    first = first.astype(jnp.bfloat16).reshape(side, side * rows, split)
+    second = jnp.dot(attended, out_weight[:, split:], preferred_element_type=jnp.float32)
+    second = second.astype(jnp.bfloat16).reshape(side, side * rows, split)
+    first = ring_exchange(first, "exp", x_next, x_prev, x_pos)
+    second = ring_exchange(second, "exp", z_next, z_prev, z_pos)
+    first = ring_exchange(
+        first.astype(jnp.bfloat16).reshape(side, rows, split), "exp", z_next, z_prev, z_pos
+    )
+    second = ring_exchange(
+        second.astype(jnp.bfloat16).reshape(side, rows, split), "exp", x_next, x_prev, x_pos
+    )
+    return jnp.concatenate([first, second], axis=1)
 
 
 def per_device(
@@ -137,17 +184,7 @@
     attended = jnp.concatenate([long_out, short_out], axis=0).reshape(-1, head_width)
     n_exp = lax.axis_size("exp")
     model_width = out_weight.shape[1]
-    split = model_width // 2
-    swapped = jnp.dot(attended, out_weight[:, :split], preferred_element_type=jnp.float32)
-    reduced = jnp.dot(attended, out_weight[:, split:], preferred_element_type=jnp.float32)
-    reduced = lax.psum_scatter(
-        reduced.astype(jnp.bfloat16), "exp", scatter_dimension=0, tiled=True
-    )
-    swapped = swapped.astype(jnp.bfloat16).reshape(n_exp, -1, split)
-    gathered = lax.all_to_all(swapped, "exp", split_axis=0, concat_axis=0, tiled=True)
-    attn_proj = jnp.concatenate(
-        [jnp.sum(gathered.astype(jnp.float32), axis=0), reduced.astype(jnp.float32)], axis=1
-    )
+    attn_proj = ring_reduce_scatter(attended, out_weight, n_exp)
     middle = residual + attn_proj
     normed = (
         middle * lax.rsqrt(jnp.mean(middle * middle, axis=1, keepdims=True) + 1e-05) * norm_gain

time: 373 us -> 336 us (0.901)
  waiting for transfers between devices: 181 us -> 124 us
  between operations: 15.2 us -> 2.04 us
  local copies, waits for them, and re-layouts: 4.84 us -> 15.5 us
  starting transfers between devices: 17 us -> 26.1 us
  other arithmetic: 10.8 us -> 19.4 us
    reduce_scatter x1 -> x0, waiting for transfers between devices: 48.3 us -> none  [per_device(): lax.psum_scatter(reduced.astype(jnp.bfloat16), 'exp', scatter_dimension=0...]
    all_to_all x1 -> x0, waiting for transfers between devices: 27.9 us -> none  [per_device(): lax.all_to_all(swapped, 'exp', split_axis=0, concat_axis=0, tiled=True)]
    ppermute x0 -> x16, waiting for transfers between devices: none -> 20 us  [the longest x4 11.9 us: ring_exchange(): from_left = lax.ppermute(to_right, axis, forward)]
    ppermute x0 -> x16, starting transfers between devices: none -> 17 us  [the longest x4 6.75 us: ring_exchange(): far_left = lax.ppermute(from_left[rows:], axis, forward)]
    all_to_all x1 -> x0, starting transfers between devices: 7.97 us -> none  [per_device(): lax.all_to_all(swapped, 'exp', split_axis=0, concat_axis=0, tiled=True)]
    slice x0 -> x11, local copies, waits for them, and re-layouts: none -> 7.72 us  [the longest x4 3.64 us: ring_exchange(): far_left = lax.ppermute(from_left[rows:], axis, forward)]
    concatenate x0 -> x8, other arithmetic: none -> 5.75 us  [the longest x4 3.3 us: ring_exchange(): to_left = jnp.concatenate([pick(3), across[half:]], axis=0)]
  transfers between devices with their start and end apart: 3 -> 17, of which waited for: 3 -> 7; matrix products, arithmetic and copies ran while one was open for 3% -> 7% of each run, Pallas kernels for 0% -> 0%
where the time goes in v2:
time: 336 us; the launch traced here: 335 us
  waiting for transfers between devices  124 us (37%)
  blocking collectives  104 us (31%)
  matrix products  43 us (13%)
  starting transfers between devices  26.1 us (8%)
  other arithmetic  19.4 us (6%)
  local copies, waits for them, and re-layouts  15.5 us (5%)
    all_to_all x1, blocking collectives, per_device(): lax.all_to_all(outgoing, ('req', 'exp'), split_axis=0, concat_axis=0, til...  104 us
    all_to_all x1, waiting for transfers between devices, per_device(): lax.all_to_all(produced, ('req', 'exp'), split_axis=0, concat_axis=0, til...  104 us
    ppermute x4, waiting for transfers between devices, ring_exchange(): from_left = lax.ppermute(to_right, axis, forward)  11.9 us
    all_to_all x1, starting transfers between devices, per_device(): lax.all_to_all(produced, ('req', 'exp'), split_axis=0, concat_axis=0, til...  9.05 us
    ppermute x4, waiting for transfers between devices, ring_exchange(): far_right = lax.ppermute(from_right[rows:], axis, backward)  7.38 us
    ppermute x4, starting transfers between devices, ring_exchange(): far_left = lax.ppermute(from_left[rows:], axis, forward)  6.75 us
    dot_general x1, matrix products, expert_rows(): jnp.dot(activation, expert_down, preferred_element_type=jnp.float32)  6.72 us
  transfers between devices with their start and end apart: 17, of which 7 were waited for; matrix products, arithmetic and copies ran while one was open for 7% of the time, Pallas kernels for 0%

profile of v2, /device:TPU:60, one launch (start us, length us, event | category | flops | bytes accessed | tf_op | source)
XLA Modules:
  0.0 334.9 jit_solution(17973405052995412515)
XLA Ops:
  0.8 1.8 fusion.25
  5.0 3.7 %fusion.7 = (f32[15,64]{1,0:T(8,128)S(1)}, f32[15,64,1024]{2,1,0:T(8,128)S(1)}) fusion(pred[15,1024]{1,0:T(8,128)(4,1)S(1)} %iota_compare_fusion.5, bf16[16,64,128]{2,1,0:T(8,128)(2,1)S(1)} %copy-done.10, bf16[15,1024,128]{2,1,0:T(8,128)(2,1)} %param.25), kind=kOutput, calls=%fused_computation.16 | convolution fusion | flops 254606400 | bytes 8145664 | tf_op jit(solution)/shard_map/bthe,blhe->bhtl/dot_general | solution.py:51
  13.0 1.7 fusion.116
  18.6 2.0 convolution_convert_fusion.3
  20.6 2.0 convolution_convert_fusion.2
  30.5 2.2 collective-permute-start.8
  34.0 11.9 %collective-permute-done = bf16[384,1024]{1,0:T(8,128)(2,1)} collective-permute-done((bf16[384,1024]{1,0:T(8,128)(2,1)}, bf16[384,1024]{1,0:T(8,128)(2,1)}, u32[]{:S(2)}, u32[]{:S(2)}) %collective-permute-start) | collective-permute-done | bytes 786464 | tf_op jit(solution)/shard_map/ppermute | solution.py:106
  51.4 2.0 collective-permute-start.10
  56.1 1.9 fusion.41
  58.2 2.7 collective-permute-done.11
  60.8 1.7 fusion.38
  64.1 1.6 collective-permute-start.4
  71.1 1.6 collective-permute-start.6
  74.2 1.9 compare_reduce_fusion
  77.0 1.8 collective-permute-start.14
  81.2 3.1 collective-permute-done.15
  85.7 2.4 convolution_convert_fusion.1
  88.1 104.4 %all_to_all.10 = bf16[128,16,2048]{2,1,0:T(8,128)(2,1)S(1)} all-to-all(bf16[128,16,2048]{2,1,0:T(8,128)(2,1)S(1)} %bitcast.150), channel_id=1, replica_groups=mesh['req'=8,'exp'=16] {'req','exp'}, dimensions={0} | all-to-all | bytes 16777216 | tf_op jit(solution)/shard_map/all_to_all | solution.py:213
  192.5 4.5 %fusion.13 = f32[2048,512]{1,0:T(8,128)S(1)} fusion(bf16[2048,2048]{1,0:T(8,128)(2,1)S(1)} %bitcast.152, bf16[1,2048,512]{2,1,0:T(8,128)(2,1)S(1)} %copy-done.16), kind=kOutput, calls=%fused_computation.21 | convolution fusion | flops 4294967296 | bytes 14680064 | tf_op jit(solution)/shard_map/dot_general | solution.py:92
  197.1 5.2 %multiply_convert_fusion = bf16[2048,512]{1,0:T(8,128)(2,1)S(1)} fusion(f32[2048,512]{1,0:T(8,128)S(1)} %fusion.13, bf16[2048,2048]{1,0:T(8,128)(2,1)S(1)} %bitcast.153, bf16[1,2048,512]{2,1,0:T(8,128)(2,1)S(1)} %copy-done.17), kind=kOutput, calls=%fused_computation.10 | convolution fusion | flops 4301258752 | bytes 16777216 | tf_op jit(solution)/shard_map/dot_general | solution.py:93
  202.3 6.7 %convolution_convert_fusion = bf16[2048,2048]{1,0:T(8,128)(2,1)} fusion(bf16[2048,512]{1,0:T(8,128)(2,1)S(1)} %multiply_convert_fusion, bf16[1,512,2048]{2,1,0:T(8,128)(2,1)S(1)} %copy-done), kind=kOutput, calls=%fused_computation.2 | convolution fusion | flops 4299161600 | bytes 12582912 | tf_op jit(solution)/shard_map/dot_general | solution.py:95
  209.0 9.1 %all-to-all-start.1 = ((bf16[128,16,2048]{2,1,0:T(8,128)(2,1)}), bf16[128,16,2048]{2,1,0:T(8,128)(2,1)}, u32[]{:S(2)}, u32[]{:S(2)}) async-start(bf16[128,16,2048]{2,1,0:T(8,128)(2,1)} %bitcast.151), calls=%async_computation.1 | async-start | bytes 16777216 | tf_op jit(solution)/shard_map/all_to_all | solution.py:217
  224.2 104.4 %all-to-all-done.1 = bf16[128,16,2048]{2,1,0:T(8,128)(2,1)} async-done(((bf16[128,16,2048]{2,1,0:T(8,128)(2,1)}), bf16[128,16,2048]{2,1,0:T(8,128)(2,1)}, u32[]{:S(2)}, u32[]{:S(2)}) %all-to-all-start.1) | async-done | bytes 8388640 | tf_op jit(solution)/shard_map/all_to_all | solution.py:217
  328.6 5.5 %convolution_reduce_fusion = f32[64,2048]{1,0:T(8,128)S(1)} fusion(bf16[3,64,2048]{2,1,0:T(8,128)(2,1)} %bitcast.169, bf16[2048,2048,1]{1,0,2:T(8,128)(2,1)} %bitcast.51), kind=kOutput, calls=%fused_computation.31 | convolution fusion | flops 1610874880 | bytes 9699328 | tf_op jit(solution)/shard_map/dot_general | solution.py:225
  (132 shorter events, 47.0 us)
Async XLA Ops:
  0.6 201.6 %copy-start = (bf16[1,512,2048]{2,1,0:T(8,128)(2,1)S(1)}, bf16[1,512,2048]{2,1,0:T(8,128)(2,1)}, u32[]{:S(2)}) copy-start(bf16[1,512,2048]{2,1,0:T(8,128)(2,1)} %param.37) | copy-start | bytes 6291460
  25.2 8.6 %copy-start.8 = (s32[64,8]{0,1:T(8,128)S(1)}, s32[64,8]{0,1:T(8,128)}, u32[]{:S(2)}) copy-start(s32[64,8]{0,1:T(8,128)} %param.33) | copy-start | bytes 6148
  26.2 19.6 %collective-permute-start = (bf16[384,1024]{1,0:T(8,128)(2,1)}, bf16[384,1024]{1,0:T(8,128)(2,1)}, u32[]{:S(2)}, u32[]{:S(2)}) collective-permute-start(bf16[384,1024]{1,0:T(8,128)(2,1)} %pad_maximum_fusion), channel_id=1, source_target_pairs={{0,1},{1,2},{2,3},{3,0},{4,5},{5,6},{6,7},{7,4},{8,9},{9,10},{10,1... | collective-permute-start | bytes 2359304 | tf_op jit(solution)/shard_map/ppermute | solution.py:106
  28.4 19.7 %collective-permute-start.1 = (bf16[384,1024]{1,0:T(8,128)(2,1)}, bf16[384,1024]{1,0:T(8,128)(2,1)}, u32[]{:S(2)}, u32[]{:S(2)}) collective-permute-start(bf16[384,1024]{1,0:T(8,128)(2,1)} %pad_maximum_fusion.1), channel_id=1, source_target_pairs={{0,3},{1,0},{2,1},{3,2},{4,7},{5,4},{6,5},{7,6},{8,11},{9,8},{10,9... | collective-permute-start | bytes 2359304 | tf_op jit(solution)/shard_map/ppermute | solution.py:107
  30.5 19.9 %collective-permute-start.8 = (bf16[384,1024]{1,0:T(8,128)(2,1)S(1)}, bf16[384,1024]{1,0:T(8,128)(2,1)}, u32[]{:S(2)}, u32[]{:S(2)}) collective-permute-start(bf16[384,1024]{1,0:T(8,128)(2,1)S(1)} %pad_maximum_fusion.2), channel_id=1, source_target_pairs={{0,4},{1,5},{2,6},{3,7},{4,8},{5,9},{6,10},{7,11},{8,12},{9,13},{1... | collective-permute-start | bytes 2359304 | tf_op jit(solution)/shard_map/ppermute | solution.py:106
  33.7 19.7 %collective-permute-start.9 = (bf16[384,1024]{1,0:T(8,128)(2,1)}, bf16[384,1024]{1,0:T(8,128)(2,1)}, u32[]{:S(2)}, u32[]{:S(2)}) collective-permute-start(bf16[384,1024]{1,0:T(8,128)(2,1)} %pad_maximum_fusion.3), channel_id=1, source_target_pairs={{0,12},{1,13},{2,14},{3,15},{4,0},{5,1},{6,2},{7,3},{8,4},{9,5},{1... | collective-permute-start | bytes 2359304 | tf_op jit(solution)/shard_map/ppermute | solution.py:107
  46.8 7.8 %collective-permute-start.2 = (bf16[128,1024]{1,0:T(8,128)(2,1)S(1)}, bf16[128,1024]{1,0:T(8,128)(2,1)}, u32[]{:S(2)}, u32[]{:S(2)}) collective-permute-start(bf16[128,1024]{1,0:T(8,128)(2,1)S(1)} %slice.180), channel_id=1, source_target_pairs={{0,1},{1,2},{2,3},{3,0},{4,5},{5,6},{6,7},{7,4},{8,9},{9,10},{10,1... | collective-permute-start | bytes 786440 | tf_op jit(solution)/shard_map/ppermute | solution.py:108
  49.0 7.1 %collective-permute-start.3 = (bf16[128,1024]{1,0:T(8,128)(2,1)S(1)}, bf16[128,1024]{1,0:T(8,128)(2,1)}, u32[]{:S(2)}, u32[]{:S(2)}) collective-permute-start(bf16[128,1024]{1,0:T(8,128)(2,1)S(1)} %slice.181), channel_id=1, source_target_pairs={{0,3},{1,0},{2,1},{3,2},{4,7},{5,4},{6,5},{7,6},{8,11},{9,8},{10,9... | collective-permute-start | bytes 786440 | tf_op jit(solution)/shard_map/ppermute | solution.py:109
  51.4 6.7 %collective-permute-start.10 = (bf16[128,1024]{1,0:T(8,128)(2,1)S(1)}, bf16[128,1024]{1,0:T(8,128)(2,1)S(1)}, u32[]{:S(2)}, u32[]{:S(2)}) collective-permute-start(bf16[128,1024]{1,0:T(8,128)(2,1)S(1)} %slice.188), channel_id=1, source_target_pairs={{0,4},{1,5},{2,6},{3,7},{4,8},{5,9},{6,10},{7,11},{8,12},{9,13},{1... | collective-permute-start | bytes 786440 | tf_op jit(solution)/shard_map/ppermute | solution.py:108
  54.4 6.4 %collective-permute-start.11 = (bf16[128,1024]{1,0:T(8,128)(2,1)S(1)}, bf16[128,1024]{1,0:T(8,128)(2,1)S(1)}, u32[]{:S(2)}, u32[]{:S(2)}) collective-permute-start(bf16[128,1024]{1,0:T(8,128)(2,1)S(1)} %slice.189), channel_id=1, source_target_pairs={{0,12},{1,13},{2,14},{3,15},{4,0},{5,1},{6,2},{7,3},{8,4},{9,5},{1... | collective-permute-start | bytes 786440 | tf_op jit(solution)/shard_map/ppermute | solution.py:109
  58.0 27.5 %copy-start.1 = (f32[64,2048]{1,0:T(8,128)S(1)}, f32[64,2048]{1,0:T(8,128)}, u32[]{:S(2)}) copy-start(f32[64,2048]{1,0:T(8,128)} %param.30) | copy-start | bytes 1572868
  58.1 27.6 %copy-start.9 = (f32[2048]{0:T(1024)S(1)}, f32[2048]{0:T(1024)}, u32[]{:S(2)}) copy-start(f32[2048]{0:T(1024)} %param.32) | copy-start | bytes 24580
  64.1 6.2 %collective-permute-start.4 = (bf16[96,1024]{1,0:T(8,128)(2,1)}, bf16[96,1024]{1,0:T(8,128)(2,1)}, u32[]{:S(2)}, u32[]{:S(2)}) collective-permute-start(bf16[96,1024]{1,0:T(8,128)(2,1)} %pad_maximum_fusion.6), channel_id=1, source_target_pairs={{0,4},{1,5},{2,6},{3,7},{4,8},{5,9},{6,10},{7,11},{8,12},{9,13},{1... | collective-permute-start | bytes 589832 | tf_op jit(solution)/shard_map/ppermute | solution.py:106
  66.4 6.4 %collective-permute-start.5 = (bf16[96,1024]{1,0:T(8,128)(2,1)}, bf16[96,1024]{1,0:T(8,128)(2,1)}, u32[]{:S(2)}, u32[]{:S(2)}) collective-permute-start(bf16[96,1024]{1,0:T(8,128)(2,1)} %pad_maximum_fusion.7), channel_id=1, source_target_pairs={{0,12},{1,13},{2,14},{3,15},{4,0},{5,1},{6,2},{7,3},{8,4},{9,5},{1... | collective-permute-start | bytes 589832 | tf_op jit(solution)/shard_map/ppermute | solution.py:107
  67.5 8.6 %collective-permute-start.12 = (bf16[96,1024]{1,0:T(8,128)(2,1)}, bf16[96,1024]{1,0:T(8,128)(2,1)}, u32[]{:S(2)}, u32[]{:S(2)}) collective-permute-start(bf16[96,1024]{1,0:T(8,128)(2,1)} %pad_maximum_fusion.8), channel_id=1, source_target_pairs={{0,1},{1,2},{2,3},{3,0},{4,5},{5,6},{6,7},{7,4},{8,9},{9,10},{10,1... | collective-permute-start | bytes 589832 | tf_op jit(solution)/shard_map/ppermute | solution.py:106
  69.4 9.4 %collective-permute-start.13 = (bf16[96,1024]{1,0:T(8,128)(2,1)}, bf16[96,1024]{1,0:T(8,128)(2,1)S(1)}, u32[]{:S(2)}, u32[]{:S(2)}) collective-permute-start(bf16[96,1024]{1,0:T(8,128)(2,1)} %pad_maximum_fusion.9), channel_id=1, source_target_pairs={{0,3},{1,0},{2,1},{3,2},{4,7},{5,4},{6,5},{7,6},{8,11},{9,8},{10,9... | collective-permute-start | bytes 589832 | tf_op jit(solution)/shard_map/ppermute | solution.py:107
  71.1 7.9 %collective-permute-start.6 = (bf16[32,1024]{1,0:T(8,128)(2,1)S(1)}, bf16[32,1024]{1,0:T(8,128)(2,1)S(1)}, u32[]{:S(2)}, u32[]{:S(2)}) collective-permute-start(bf16[32,1024]{1,0:T(8,128)(2,1)S(1)} %slice.184), channel_id=1, source_target_pairs={{0,4},{1,5},{2,6},{3,7},{4,8},{5,9},{6,10},{7,11},{8,12},{9,13},{1... | collective-permute-start | bytes 196616 | tf_op jit(solution)/shard_map/ppermute | solution.py:108
  73.6 5.9 %collective-permute-start.7 = (bf16[32,1024]{1,0:T(8,128)(2,1)S(1)}, bf16[32,1024]{1,0:T(8,128)(2,1)S(1)}, u32[]{:S(2)}, u32[]{:S(2)}) collective-permute-start(bf16[32,1024]{1,0:T(8,128)(2,1)S(1)} %slice.185), channel_id=1, source_target_pairs={{0,12},{1,13},{2,14},{3,15},{4,0},{5,1},{6,2},{7,3},{8,4},{9,5},{1... | collective-permute-start | bytes 196616 | tf_op jit(solution)/shard_map/ppermute | solution.py:109
  77.0 4.3 %collective-permute-start.14 = (bf16[32,1024]{1,0:T(8,128)(2,1)S(1)}, bf16[32,1024]{1,0:T(8,128)(2,1)S(1)}, u32[]{:S(2)}, u32[]{:S(2)}) collective-permute-start(bf16[32,1024]{1,0:T(8,128)(2,1)S(1)} %slice.192), channel_id=1, source_target_pairs={{0,1},{1,2},{2,3},{3,0},{4,5},{5,6},{6,7},{7,4},{8,9},{9,10},{10,1... | collective-permute-start | bytes 196616 | tf_op jit(solution)/shard_map/ppermute | solution.py:108
  78.8 5.5 %collective-permute-start.15 = (bf16[32,1024]{1,0:T(8,128)(2,1)S(1)}, bf16[32,1024]{1,0:T(8,128)(2,1)S(1)}, u32[]{:S(2)}, u32[]{:S(2)}) collective-permute-start(bf16[32,1024]{1,0:T(8,128)(2,1)S(1)} %slice.193), channel_id=1, source_target_pairs={{0,3},{1,0},{2,1},{3,2},{4,7},{5,4},{6,5},{7,6},{8,11},{9,8},{10,9... | collective-permute-start | bytes 196616 | tf_op jit(solution)/shard_map/ppermute | solution.py:109
  88.1 104.5 %copy-start.16 = (bf16[1,2048,512]{2,1,0:T(8,128)(2,1)S(1)}, bf16[1,2048,512]{2,1,0:T(8,128)(2,1)}, u32[]{:S(2)}) copy-start(bf16[1,2048,512]{2,1,0:T(8,128)(2,1)} %param.35) | copy-start | bytes 6291460
  209.0 9.1 %copy-start.11 = (f32[64,8]{0,1:T(8,128)S(1)}, f32[64,8]{0,1:T(8,128)}, u32[]{:S(2)}) copy-start(f32[64,8]{0,1:T(8,128)} %param.34) | copy-start | bytes 6148
  209.0 10.5 %copy-start.14 = (s32[16]{0:T(128)S(1)}, s32[16]{0:T(128)}, u32[]{:S(2)}) copy-start(s32[16]{0:T(128)} %param.29) | copy-start | bytes 196
  209.0 119.6 %all-to-all-start.1 = ((bf16[128,16,2048]{2,1,0:T(8,128)(2,1)}), bf16[128,16,2048]{2,1,0:T(8,128)(2,1)}, u32[]{:S(2)}, u32[]{:S(2)}) async-start(bf16[128,16,2048]{2,1,0:T(8,128)(2,1)} %bitcast.151), calls=%async_computation.1 | async-start | bytes 16777216 | tf_op jit(solution)/shard_map/all_to_all | solution.py:217
  (12 other events, 26.7 us)

commit v3 on v1

--- a/solution.py
+++ b/solution.py
@@ -93,6 +93,43 @@
     up_part = jnp.dot(rows, expert_up, preferred_element_type=jnp.float32)
     activation = (jax.nn.silu(gate_part) * up_part).astype(jnp.bfloat16)
     return jnp.dot(activation, expert_down, preferred_element_type=jnp.float32).astype(jnp.bfloat16)
+
+
+def ring_sum(blocks, shifts):
+    total = blocks[0].astype(jnp.float32)
+    for step, pairs in enumerate(shifts, start=1):
+        total = total + lax.ppermute(blocks[step], "exp", pairs).astype(jnp.float32)
+    return total
+
+
+def ring_reduce_scatter(attended, out_weight, n_exp):
+    side = 4
+    assert n_exp == side * side
+    index = lax.axis_index("exp")
+    z_pos, x_pos = index // side, index % side
+    cells = [(z, x) for z in range(side) for x in range(side)]
+    x_shifts = [[(z * side + x, z * side + (x + k) % side) for z, x in cells] for k in range(1, side)]
+    z_shifts = [[(z * side + x, ((z + k) % side) * side + x) for z, x in cells] for k in range(1, side)]
+    rows = attended.shape[0] // n_exp
+    width = out_weight.shape[1]
+    split = width // 2
+    blocks = attended.reshape(n_exp, rows, -1)
+    near = jnp.arange(side, dtype=jnp.int32)
+    z_of = (z_pos + near) % side
+    x_of = (x_pos + near) % side
+    x_major = (x_of[:, None] + z_of[None, :] * side).reshape(-1)
+    z_major = (z_of[:, None] * side + x_of[None, :]).reshape(-1)
+    first = jnp.take(blocks, x_major, axis=0).reshape(n_exp * rows, -1)
+    first = jnp.dot(first, out_weight[:, :split], preferred_element_type=jnp.float32)
+    first = first.astype(jnp.bfloat16).reshape(side, side * rows, split)
+    second = jnp.take(blocks, z_major, axis=0).reshape(n_exp * rows, -1)
+    second = jnp.dot(second, out_weight[:, split:], preferred_element_type=jnp.float32)
+    second = second.astype(jnp.bfloat16).reshape(side, side * rows, split)
+    first = ring_sum(first, x_shifts)
+    second = ring_sum(second, z_shifts)
+    first = ring_sum(first.astype(jnp.bfloat16).reshape(side, rows, split), z_shifts)
+    second = ring_sum(second.astype(jnp.bfloat16).reshape(side, rows, split), x_shifts)
+    return jnp.concatenate([first, second], axis=1)
 
 
 def per_device(
@@ -137,17 +174,7 @@
     attended = jnp.concatenate([long_out, short_out], axis=0).reshape(-1, head_width)
     n_exp = lax.axis_size("exp")
     model_width = out_weight.shape[1]
-    split = model_width // 2
-    swapped = jnp.dot(attended, out_weight[:, :split], preferred_element_type=jnp.float32)
-    reduced = jnp.dot(attended, out_weight[:, split:], preferred_element_type=jnp.float32)
-    reduced = lax.psum_scatter(
-        reduced.astype(jnp.bfloat16), "exp", scatter_dimension=0, tiled=True
-    )
-    swapped = swapped.astype(jnp.bfloat16).reshape(n_exp, -1, split)
-    gathered = lax.all_to_all(swapped, "exp", split_axis=0, concat_axis=0, tiled=True)
-    attn_proj = jnp.concatenate(
-        [jnp.sum(gathered.astype(jnp.float32), axis=0), reduced.astype(jnp.float32)], axis=1
-    )
+    attn_proj = ring_reduce_scatter(attended, out_weight, n_exp)
     middle = residual + attn_proj
     normed = (
         middle * lax.rsqrt(jnp.mean(middle * middle, axis=1, keepdims=True) + 1e-05) * norm_gain

time: 373 us -> 318 us (0.85)
  waiting for transfers between devices: 181 us -> 125 us
  between operations: 15.2 us -> 1.95 us
  starting transfers between devices: 17 us -> 26.6 us
  local copies, waits for them, and re-layouts: 4.84 us -> 10.5 us
    reduce_scatter x1 -> x0, waiting for transfers between devices: 48.3 us -> none  [per_device(): lax.psum_scatter(reduced.astype(jnp.bfloat16), 'exp', scatter_dimension=0...]
    all_to_all x1 -> x0, waiting for transfers between devices: 27.9 us -> none  [per_device(): lax.all_to_all(swapped, 'exp', split_axis=0, concat_axis=0, tiled=True)]
    ppermute x0 -> x12, waiting for transfers between devices: none -> 20.3 us  [ring_sum(): total = total + lax.ppermute(blocks[step], 'exp', pairs).astype(jnp.float32)]
    ppermute x0 -> x12, starting transfers between devices: none -> 17.6 us  [ring_sum(): total = total + lax.ppermute(blocks[step], 'exp', pairs).astype(jnp.float32)]
    all_to_all x1 -> x0, starting transfers between devices: 7.97 us -> none  [per_device(): lax.all_to_all(swapped, 'exp', split_axis=0, concat_axis=0, tiled=True)]
  transfers between devices with their start and end apart: 3 -> 13, of which waited for: 3 -> 7; matrix products, arithmetic and copies ran while one was open for 3% -> 5% of each run, Pallas kernels for 0% -> 0%
where the time goes in v3:
time: 318 us; the launch traced here: 317 us
  waiting for transfers between devices  125 us (39%)
  blocking collectives  101 us (32%)
  matrix products  40.3 us (13%)
  starting transfers between devices  26.6 us (8%)
  other arithmetic  11.8 us (4%)
  local copies, waits for them, and re-layouts  10.5 us (3%)
    all_to_all x1, waiting for transfers between devices, per_device(): lax.all_to_all(produced, ('req', 'exp'), split_axis=0, concat_axis=0, til...  104 us
    all_to_all x1, blocking collectives, per_device(): lax.all_to_all(outgoing, ('req', 'exp'), split_axis=0, concat_axis=0, til...  101 us
    ppermute x12, waiting for transfers between devices, ring_sum(): total = total + lax.ppermute(blocks[step], 'exp', pairs).astype(jnp.float32)  20.3 us
    ppermute x12, starting transfers between devices, ring_sum(): total = total + lax.ppermute(blocks[step], 'exp', pairs).astype(jnp.float32)  17.6 us
    all_to_all x1, starting transfers between devices, per_device(): lax.all_to_all(produced, ('req', 'exp'), split_axis=0, concat_axis=0, til...  9.02 us
    dot_general x1, matrix products, expert_rows(): jnp.dot(activation, expert_down, preferred_element_type=jnp.float32)  6.73 us
  transfers between devices with their start and end apart: 13, of which 7 were waited for; matrix products, arithmetic and copies ran while one was open for 5% of the time, Pallas kernels for 0%

profile of v3, /device:TPU:60, one launch (start us, length us, event | category | flops | bytes accessed | tf_op | source)
XLA Modules:
  0.0 317.3 jit_solution(17782310575599661772)
XLA Ops:
  0.7 1.8 fusion.25
  5.1 3.7 %fusion.7 = (f32[15,64]{1,0:T(8,128)S(1)}, f32[15,64,1024]{2,1,0:T(8,128)S(1)}) fusion(pred[15,1024]{1,0:T(8,128)(4,1)S(1)} %iota_compare_fusion.5, bf16[16,64,128]{2,1,0:T(8,128)(2,1)S(1)} %copy-done.10, bf16[15,1024,128]{2,1,0:T(8,128)(2,1)} %param.27), kind=kOutput, calls=%fused_computation.18 | convolution fusion | flops 254606400 | bytes 8145664 | tf_op jit(solution)/shard_map/bthe,blhe->bhtl/dot_general | solution.py:51
  13.2 1.7 fusion.113
  29.9 1.9 collective-permute-start.6
  33.6 1.9 compare_reduce_fusion
  35.5 2.3 collective-permute-done
  38.2 9.7 %collective-permute-done.1 = bf16[256,1024]{1,0:T(8,128)(2,1)} collective-permute-done((bf16[256,1024]{1,0:T(8,128)(2,1)}, bf16[256,1024]{1,0:T(8,128)(2,1)}, u32[]{:S(2)}, u32[]{:S(2)}) %collective-permute-start.1) | collective-permute-done | bytes 524320 | tf_op jit(solution)/shard_map/ppermute | solution.py:101
  47.9 1.8 collective-permute-done.2
  49.7 1.9 add_convert_fusion.1
  51.7 2.0 collective-permute-start.3
  54.8 2.5 collective-permute-start.5
  58.4 1.6 add_convert_fusion
  60.0 3.4 %collective-permute-start.10 = (bf16[64,1024]{1,0:T(8,128)(2,1)S(1)}, bf16[64,1024]{1,0:T(8,128)(2,1)S(1)}, u32[]{:S(2)}, u32[]{:S(2)}) collective-permute-start(bf16[64,1024]{1,0:T(8,128)(2,1)S(1)} %get-tuple-element.17), channel_id=1, source_target_pairs={{0,2},{1,3},{2,0},{3,1},{4,6},{5,7},{6,4},{7,5},{8,10},{9,11},{10,... | collective-permute-start | bytes 393224 | tf_op jit(solution)/shard_map/ppermute | solution.py:101
  63.5 2.0 collective-permute-start.9
  65.6 1.8 collective-permute-done.10
  67.4 3.5 %collective-permute-done.11 = bf16[64,1024]{1,0:T(8,128)(2,1)S(1)} collective-permute-done((bf16[64,1024]{1,0:T(8,128)(2,1)S(1)}, bf16[64,1024]{1,0:T(8,128)(2,1)S(1)}, u32[]{:S(2)}, u32[]{:S(2)}) %collective-permute-start.11) | collective-permute-done | bytes 131104 | tf_op jit(solution)/shard_map/ppermute | solution.py:101
  71.1 2.4 convolution_convert_fusion.1
  73.5 101.5 %all_to_all.10 = bf16[128,16,2048]{2,1,0:T(8,128)(2,1)S(1)} all-to-all(bf16[128,16,2048]{2,1,0:T(8,128)(2,1)S(1)} %bitcast.99), channel_id=1, replica_groups=mesh['req'=8,'exp'=16] {'req','exp'}, dimensions={0} | all-to-all | bytes 16777216 | tf_op jit(solution)/shard_map/all_to_all | solution.py:203
  175.0 4.5 %fusion.13 = f32[2048,512]{1,0:T(8,128)S(1)} fusion(bf16[2048,2048]{1,0:T(8,128)(2,1)S(1)} %bitcast.101, bf16[1,2048,512]{2,1,0:T(8,128)(2,1)S(1)} %copy-done.16), kind=kOutput, calls=%fused_computation.23 | convolution fusion | flops 4294967296 | bytes 14680064 | tf_op jit(solution)/shard_map/dot_general | solution.py:92
  179.5 5.2 %multiply_convert_fusion = bf16[2048,512]{1,0:T(8,128)(2,1)S(1)} fusion(f32[2048,512]{1,0:T(8,128)S(1)} %fusion.13, bf16[2048,2048]{1,0:T(8,128)(2,1)S(1)} %bitcast.102, bf16[1,2048,512]{2,1,0:T(8,128)(2,1)S(1)} %copy-done.17), kind=kOutput, calls=%fused_computation.12 | convolution fusion | flops 4301258752 | bytes 16777216 | tf_op jit(solution)/shard_map/dot_general | solution.py:93
  184.7 6.7 %convolution_convert_fusion = bf16[2048,2048]{1,0:T(8,128)(2,1)} fusion(bf16[2048,512]{1,0:T(8,128)(2,1)S(1)} %multiply_convert_fusion, bf16[1,512,2048]{2,1,0:T(8,128)(2,1)S(1)} %copy-done), kind=kOutput, calls=%fused_computation.4 | convolution fusion | flops 4299161600 | bytes 12582912 | tf_op jit(solution)/shard_map/dot_general | solution.py:95
  191.4 9.0 %all-to-all-start.1 = ((bf16[128,16,2048]{2,1,0:T(8,128)(2,1)}), bf16[128,16,2048]{2,1,0:T(8,128)(2,1)}, u32[]{:S(2)}, u32[]{:S(2)}) async-start(bf16[128,16,2048]{2,1,0:T(8,128)(2,1)} %bitcast.100), calls=%async_computation.1 | async-start | bytes 16777216 | tf_op jit(solution)/shard_map/all_to_all | solution.py:207
  206.5 104.5 %all-to-all-done.1 = bf16[128,16,2048]{2,1,0:T(8,128)(2,1)} async-done(((bf16[128,16,2048]{2,1,0:T(8,128)(2,1)}), bf16[128,16,2048]{2,1,0:T(8,128)(2,1)}, u32[]{:S(2)}, u32[]{:S(2)}) %all-to-all-start.1) | async-done | bytes 8388640 | tf_op jit(solution)/shard_map/all_to_all | solution.py:207
  311.0 5.5 %convolution_reduce_fusion = f32[64,2048]{1,0:T(8,128)S(1)} fusion(bf16[3,64,2048]{2,1,0:T(8,128)(2,1)} %bitcast.105, bf16[2048,2048,1]{1,0,2:T(8,128)(2,1)} %bitcast.25), kind=kOutput, calls=%fused_computation.33 | convolution fusion | flops 1610874880 | bytes 9699328 | tf_op jit(solution)/shard_map/dot_general | solution.py:215
  (118 shorter events, 32.6 us)
Async XLA Ops:
  0.6 184.1 %copy-start = (bf16[1,512,2048]{2,1,0:T(8,128)(2,1)S(1)}, bf16[1,512,2048]{2,1,0:T(8,128)(2,1)}, u32[]{:S(2)}) copy-start(bf16[1,512,2048]{2,1,0:T(8,128)(2,1)} %param.39) | copy-start | bytes 6291460
  0.6 3.1 copy-start.10
  0.7 3.1 copy-start.12
  0.7 4.4 %copy-start.13 = (s32[15]{0:T(128)S(1)}, s32[15]{0:T(128)}, u32[]{:S(2)}) copy-start(s32[15]{0:T(128)} %param.29) | copy-start | bytes 184
  22.7 10.2 %copy-start.8 = (s32[64,8]{0,1:T(8,128)S(1)}, s32[64,8]{0,1:T(8,128)}, u32[]{:S(2)}) copy-start(s32[64,8]{0,1:T(8,128)} %param.35) | copy-start | bytes 6148
  22.7 15.1 %collective-permute-start = (bf16[256,1024]{1,0:T(8,128)(2,1)}, bf16[256,1024]{1,0:T(8,128)(2,1)}, u32[]{:S(2)}, u32[]{:S(2)}) collective-permute-start(bf16[256,1024]{1,0:T(8,128)(2,1)} %get-tuple-element.4), channel_id=1, source_target_pairs={{0,1},{1,2},{2,3},{3,0},{4,5},{5,6},{6,7},{7,4},{8,9},{9,10},{10,1... | collective-permute-start | bytes 1572872 | tf_op jit(solution)/shard_map/ppermute | solution.py:101
  23.9 24.0 %collective-permute-start.1 = (bf16[256,1024]{1,0:T(8,128)(2,1)}, bf16[256,1024]{1,0:T(8,128)(2,1)}, u32[]{:S(2)}, u32[]{:S(2)}) collective-permute-start(bf16[256,1024]{1,0:T(8,128)(2,1)} %get-tuple-element.6), channel_id=1, source_target_pairs={{0,2},{1,3},{2,0},{3,1},{4,6},{5,7},{6,4},{7,5},{8,10},{9,11},{10,... | collective-permute-start | bytes 1572872 | tf_op jit(solution)/shard_map/ppermute | solution.py:101
  24.7 25.0 %collective-permute-start.2 = (bf16[256,1024]{1,0:T(8,128)(2,1)}, bf16[256,1024]{1,0:T(8,128)(2,1)}, u32[]{:S(2)}, u32[]{:S(2)}) collective-permute-start(bf16[256,1024]{1,0:T(8,128)(2,1)} %get-tuple-element.5), channel_id=1, source_target_pairs={{0,3},{1,0},{2,1},{3,2},{4,7},{5,4},{6,5},{7,6},{8,11},{9,8},{10,9... | collective-permute-start | bytes 1572872 | tf_op jit(solution)/shard_map/ppermute | solution.py:101
  29.9 24.9 %collective-permute-start.6 = (bf16[256,1024]{1,0:T(8,128)(2,1)}, bf16[256,1024]{1,0:T(8,128)(2,1)S(1)}, u32[]{:S(2)}, u32[]{:S(2)}) collective-permute-start(bf16[256,1024]{1,0:T(8,128)(2,1)} %get-tuple-element.7), channel_id=1, source_target_pairs={{0,4},{1,5},{2,6},{3,7},{4,8},{5,9},{6,10},{7,11},{8,12},{9,13},{1... | collective-permute-start | bytes 1572872 | tf_op jit(solution)/shard_map/ppermute | solution.py:101
  31.8 25.6 %collective-permute-start.7 = (bf16[256,1024]{1,0:T(8,128)(2,1)}, bf16[256,1024]{1,0:T(8,128)(2,1)}, u32[]{:S(2)}, u32[]{:S(2)}) collective-permute-start(bf16[256,1024]{1,0:T(8,128)(2,1)} %get-tuple-element.9), channel_id=1, source_target_pairs={{0,8},{1,9},{2,10},{3,11},{4,12},{5,13},{6,14},{7,15},{8,0},{9,1},... | collective-permute-start | bytes 1572872 | tf_op jit(solution)/shard_map/ppermute | solution.py:101
  37.8 33.1 %copy-start.3 = (f32[64,2048]{1,0:T(8,128)S(1)}, f32[64,2048]{1,0:T(8,128)}, u32[]{:S(2)}) copy-start(f32[64,2048]{1,0:T(8,128)} %param.32) | copy-start | bytes 1572868
  37.8 20.6 %collective-permute-start.8 = (bf16[256,1024]{1,0:T(8,128)(2,1)}, bf16[256,1024]{1,0:T(8,128)(2,1)S(1)}, u32[]{:S(2)}, u32[]{:S(2)}) collective-permute-start(bf16[256,1024]{1,0:T(8,128)(2,1)} %get-tuple-element.8), channel_id=1, source_target_pairs={{0,12},{1,13},{2,14},{3,15},{4,0},{5,1},{6,2},{7,3},{8,4},{9,5},{1... | collective-permute-start | bytes 1572872 | tf_op jit(solution)/shard_map/ppermute | solution.py:101
  51.6 19.5 %copy-start.9 = (f32[2048]{0:T(1024)S(1)}, f32[2048]{0:T(1024)}, u32[]{:S(2)}) copy-start(f32[2048]{0:T(1024)} %param.34) | copy-start | bytes 24580
  51.7 11.8 %collective-permute-start.3 = (bf16[64,1024]{1,0:T(8,128)(2,1)S(1)}, bf16[64,1024]{1,0:T(8,128)(2,1)S(1)}, u32[]{:S(2)}, u32[]{:S(2)}) collective-permute-start(bf16[64,1024]{1,0:T(8,128)(2,1)S(1)} %get-tuple-element.12), channel_id=1, source_target_pairs={{0,4},{1,5},{2,6},{3,7},{4,8},{5,9},{6,10},{7,11},{8,12},{9,13},{1... | collective-permute-start | bytes 393224 | tf_op jit(solution)/shard_map/ppermute | solution.py:101
  53.6 11.9 %collective-permute-start.4 = (bf16[64,1024]{1,0:T(8,128)(2,1)S(1)}, bf16[64,1024]{1,0:T(8,128)(2,1)S(1)}, u32[]{:S(2)}, u32[]{:S(2)}) collective-permute-start(bf16[64,1024]{1,0:T(8,128)(2,1)S(1)} %get-tuple-element.14), channel_id=1, source_target_pairs={{0,8},{1,9},{2,10},{3,11},{4,12},{5,13},{6,14},{7,15},{8,0},{9,1},... | collective-permute-start | bytes 393224 | tf_op jit(solution)/shard_map/ppermute | solution.py:101
  54.8 10.7 %collective-permute-start.5 = (bf16[64,1024]{1,0:T(8,128)(2,1)S(1)}, bf16[64,1024]{1,0:T(8,128)(2,1)S(1)}, u32[]{:S(2)}, u32[]{:S(2)}) collective-permute-start(bf16[64,1024]{1,0:T(8,128)(2,1)S(1)} %get-tuple-element.13), channel_id=1, source_target_pairs={{0,12},{1,13},{2,14},{3,15},{4,0},{5,1},{6,2},{7,3},{8,4},{9,5},{1... | collective-permute-start | bytes 393224 | tf_op jit(solution)/shard_map/ppermute | solution.py:101
  60.0 7.3 %collective-permute-start.10 = (bf16[64,1024]{1,0:T(8,128)(2,1)S(1)}, bf16[64,1024]{1,0:T(8,128)(2,1)S(1)}, u32[]{:S(2)}, u32[]{:S(2)}) collective-permute-start(bf16[64,1024]{1,0:T(8,128)(2,1)S(1)} %get-tuple-element.17), channel_id=1, source_target_pairs={{0,2},{1,3},{2,0},{3,1},{4,6},{5,7},{6,4},{7,5},{8,10},{9,11},{10,... | collective-permute-start | bytes 393224 | tf_op jit(solution)/shard_map/ppermute | solution.py:101
  63.5 7.3 %collective-permute-start.11 = (bf16[64,1024]{1,0:T(8,128)(2,1)S(1)}, bf16[64,1024]{1,0:T(8,128)(2,1)S(1)}, u32[]{:S(2)}, u32[]{:S(2)}) collective-permute-start(bf16[64,1024]{1,0:T(8,128)(2,1)S(1)} %get-tuple-element.16), channel_id=1, source_target_pairs={{0,3},{1,0},{2,1},{3,2},{4,7},{5,4},{6,5},{7,6},{8,11},{9,8},{10,9... | collective-permute-start | bytes 393224 | tf_op jit(solution)/shard_map/ppermute | solution.py:101
  63.5 7.3 %collective-permute-start.9 = (bf16[64,1024]{1,0:T(8,128)(2,1)S(1)}, bf16[64,1024]{1,0:T(8,128)(2,1)S(1)}, u32[]{:S(2)}, u32[]{:S(2)}) collective-permute-start(bf16[64,1024]{1,0:T(8,128)(2,1)S(1)} %get-tuple-element.15), channel_id=1, source_target_pairs={{0,1},{1,2},{2,3},{3,0},{4,5},{5,6},{6,7},{7,4},{8,9},{9,10},{10,1... | collective-permute-start | bytes 393224 | tf_op jit(solution)/shard_map/ppermute | solution.py:101
  73.5 101.5 %copy-start.16 = (bf16[1,2048,512]{2,1,0:T(8,128)(2,1)S(1)}, bf16[1,2048,512]{2,1,0:T(8,128)(2,1)}, u32[]{:S(2)}) copy-start(bf16[1,2048,512]{2,1,0:T(8,128)(2,1)} %param.37) | copy-start | bytes 6291460
  175.0 4.5 %copy-start.17 = (bf16[1,2048,512]{2,1,0:T(8,128)(2,1)S(1)}, bf16[1,2048,512]{2,1,0:T(8,128)(2,1)}, u32[]{:S(2)}) copy-start(bf16[1,2048,512]{2,1,0:T(8,128)(2,1)} %param.38) | copy-start | bytes 6291460
  191.4 9.0 %copy-start.11 = (f32[64,8]{0,1:T(8,128)S(1)}, f32[64,8]{0,1:T(8,128)}, u32[]{:S(2)}) copy-start(f32[64,8]{0,1:T(8,128)} %param.36) | copy-start | bytes 6148
  191.4 10.5 %copy-start.14 = (s32[16]{0:T(128)S(1)}, s32[16]{0:T(128)}, u32[]{:S(2)}) copy-start(s32[16]{0:T(128)} %param.31) | copy-start | bytes 196
  191.4 119.6 %all-to-all-start.1 = ((bf16[128,16,2048]{2,1,0:T(8,128)(2,1)}), bf16[128,16,2048]{2,1,0:T(8,128)(2,1)}, u32[]{:S(2)}, u32[]{:S(2)}) async-start(bf16[128,16,2048]{2,1,0:T(8,128)(2,1)} %bitcast.100), calls=%async_computation.1 | async-start | bytes 16777216 | tf_op jit(solution)/shard_map/all_to_all | solution.py:207
  (8 other events, 12.4 us)

commit v4 on v1

--- a/solution.py
+++ b/solution.py
@@ -93,6 +93,56 @@
     up_part = jnp.dot(rows, expert_up, preferred_element_type=jnp.float32)
     activation = (jax.nn.silu(gate_part) * up_part).astype(jnp.bfloat16)
     return jnp.dot(activation, expert_down, preferred_element_type=jnp.float32).astype(jnp.bfloat16)
+
+
+def ring_gather(shard, shifts):
+    parts = [shard] + [lax.ppermute(shard, "exp", pairs) for pairs in shifts]
+    return jnp.stack(parts, axis=0)
+
+
+def gathered_projection(attended, out_weight, n_exp):
+    side = 4
+    assert n_exp == side * side
+    index = lax.axis_index("exp")
+    z_pos, x_pos = index // side, index % side
+    cells = [(z, x) for z in range(side) for x in range(side)]
+    x_shifts = [[(z * side + x, z * side + (x - k) % side) for z, x in cells] for k in range(1, side)]
+    z_shifts = [[(z * side + x, ((z - k) % side) * side + x) for z, x in cells] for k in range(1, side)]
+    n_req = lax.axis_size("req")
+    sibling = [(i, i ^ 1) for i in range(n_req)]
+    core = lax.axis_index("req") % 2
+    width = out_weight.shape[1]
+    half = width // 2
+    quarter = half // 2
+    mine = lax.dynamic_slice_in_dim(out_weight, core * half, half, axis=1)
+    weight_a = ring_gather(ring_gather(mine[:, :quarter], x_shifts), z_shifts)
+    weight_b = ring_gather(ring_gather(mine[:, quarter:], z_shifts), x_shifts)
+    weight_a = weight_a.reshape(-1, quarter)
+    weight_b = weight_b.reshape(-1, quarter)
+    rows = attended.shape[0] // n_exp
+    heads = lax.all_to_all(
+        attended.reshape(n_exp, rows, -1), "exp", split_axis=0, concat_axis=0, tiled=True
+    )
+    near = jnp.arange(side, dtype=jnp.int32)
+    z_of = (z_pos + near) % side
+    x_of = (x_pos + near) % side
+    z_major = (z_of[:, None] * side + x_of[None, :]).reshape(-1)
+    x_major = (x_of[:, None] + z_of[None, :] * side).reshape(-1)
+    own_a = jnp.swapaxes(jnp.take(heads, z_major, axis=0), 0, 1).reshape(rows, -1)
+    own_b = jnp.swapaxes(jnp.take(heads, x_major, axis=0), 0, 1).reshape(rows, -1)
+    own = jnp.stack([own_a, own_b], axis=0)
+    other = lax.ppermute(own, "req", sibling)
+
+    def project(pair):
+        left = jnp.dot(pair[0], weight_a, preferred_element_type=jnp.float32)
+        right = jnp.dot(pair[1], weight_b, preferred_element_type=jnp.float32)
+        return jnp.concatenate([left, right], axis=1)
+
+    kept = project(own)
+    returned = lax.ppermute(project(other), "req", sibling)
+    low = jnp.where(core == 0, kept, returned)
+    high = jnp.where(core == 0, returned, kept)
+    return jnp.concatenate([low, high], axis=1)
 
 
 def per_device(
@@ -137,17 +187,7 @@
     attended = jnp.concatenate([long_out, short_out], axis=0).reshape(-1, head_width)
     n_exp = lax.axis_size("exp")
     model_width = out_weight.shape[1]
-    split = model_width // 2
-    swapped = jnp.dot(attended, out_weight[:, :split], preferred_element_type=jnp.float32)
-    reduced = jnp.dot(attended, out_weight[:, split:], preferred_element_type=jnp.float32)
-    reduced = lax.psum_scatter(
-        reduced.astype(jnp.bfloat16), "exp", scatter_dimension=0, tiled=True
-    )
-    swapped = swapped.astype(jnp.bfloat16).reshape(n_exp, -1, split)
-    gathered = lax.all_to_all(swapped, "exp", split_axis=0, concat_axis=0, tiled=True)
-    attn_proj = jnp.concatenate(
-        [jnp.sum(gathered.astype(jnp.float32), axis=0), reduced.astype(jnp.float32)], axis=1
-    )
+    attn_proj = gathered_projection(attended, out_weight, n_exp)
     middle = residual + attn_proj
     normed = (
         middle * lax.rsqrt(jnp.mean(middle * middle, axis=1, keepdims=True) + 1e-05) * norm_gain

time: 373 us -> 333 us (0.89)
  waiting for transfers between devices: 181 us -> 112 us
  starting transfers between devices: 17 us -> 33.7 us
  between operations: 15.2 us -> 2.05 us
  other arithmetic: 10.8 us -> 22.5 us
  local copies, waits for them, and re-layouts: 4.84 us -> 12.3 us
    reduce_scatter x1 -> x0, waiting for transfers between devices: 48.3 us -> none  [per_device(): lax.psum_scatter(reduced.astype(jnp.bfloat16), 'exp', scatter_dimension=0...]
    all_to_all x1, waiting for transfers between devices: 27.9 us -> 0.01 us  [gathered_projection(): lax.all_to_all(attended.reshape(n_exp, rows, -1), 'exp', split_axis=0, co...]
    ppermute x0 -> x14, starting transfers between devices: none -> 16.2 us  [the longest x12 16.1 us: ring_gather(): parts = [shard] + [lax.ppermute(shard, 'exp', pairs) for pairs in shifts]]
    another operation x0 -> x5, other arithmetic: none -> 8.27 us  [the longest x4 7.19 us: ring_gather(): return jnp.stack(parts, axis=0)]
    ppermute x0 -> x14, waiting for transfers between devices: none -> 7.75 us  [the longest x12 6.71 us: ring_gather(): parts = [shard] + [lax.ppermute(shard, 'exp', pairs) for pairs in shifts]]
  transfers between devices with their start and end apart: 3 -> 16, of which waited for: 3 -> 5; matrix products, arithmetic and copies ran while one was open for 3% -> 15% of each run, Pallas kernels for 0% -> 0%
where the time goes in v4:
time: 333 us; the launch traced here: 332 us
  waiting for transfers between devices  112 us (34%)
  blocking collectives  104 us (31%)
  matrix products  44.5 us (13%)
  starting transfers between devices  33.7 us (10%)
  other arithmetic  22.5 us (7%)
  local copies, waits for them, and re-layouts  12.3 us (4%)
    all_to_all x1, blocking collectives, per_device(): lax.all_to_all(outgoing, ('req', 'exp'), split_axis=0, concat_axis=0, til...  104 us
    all_to_all x1, waiting for transfers between devices, per_device(): lax.all_to_all(produced, ('req', 'exp'), split_axis=0, concat_axis=0, til...  104 us
    ppermute x12, starting transfers between devices, ring_gather(): parts = [shard] + [lax.ppermute(shard, 'exp', pairs) for pairs in shifts]  16.1 us
    all_to_all x1, starting transfers between devices, per_device(): lax.all_to_all(produced, ('req', 'exp'), split_axis=0, concat_axis=0, til...  9.03 us
    all_to_all x1, starting transfers between devices, gathered_projection(): lax.all_to_all(attended.reshape(n_exp, rows, -1), 'exp', split_axis=0, co...  8.49 us
    another operation x4, other arithmetic, ring_gather(): return jnp.stack(parts, axis=0)  7.19 us
    ppermute x12, waiting for transfers between devices, ring_gather(): parts = [shard] + [lax.ppermute(shard, 'exp', pairs) for pairs in shifts]  6.71 us
    dot_general x1, matrix products, expert_rows(): jnp.dot(activation, expert_down, preferred_element_type=jnp.float32)  6.7 us
  transfers between devices with their start and end apart: 16, of which 5 were waited for; matrix products, arithmetic and copies ran while one was open for 15% of the time, Pallas kernels for 0%

profile of v4, /device:TPU:60, one launch (start us, length us, event | category | flops | bytes accessed | tf_op | source)
XLA Modules:
  0.0 331.7 jit_solution(17632334728568048958)
XLA Ops:
  2.4 2.7 collective-permute-start.1
  5.3 3.3 collective-permute-start.7
  11.5 1.8 fusion.29
  13.7 1.8 fusion.122
  16.6 2.6 fusion.7
  23.4 2.4 fusion.123
  30.4 8.5 %all-to-all-start = ((bf16[16,64,128]{2,1,0:T(8,128)(2,1)}), bf16[16,64,128]{2,1,0:T(8,128)(2,1)S(1)}, u32[]{:S(2)}, u32[]{:S(2)}) async-start(bf16[16,64,128]{2,1,0:T(8,128)(2,1)} %pad_maximum_fusion.6), calls=%async_computation | async-start | bytes 524288 | tf_op jit(solution)/shard_map/all_to_all | solution.py:123
  40.5 1.9 compare_reduce_fusion
  44.7 1.9 fusion.119
  48.3 2.1 collective-permute-start.4
  51.6 2.0 fusion.118
  54.2 2.7 collective-permute-start.10
  58.2 1.8 fusion.77
  62.3 1.8 fusion.79
  70.2 2.4 collective-permute-done.5
  74.3 3.3 collective-permute-done.11
  82.5 2.4 convolution_convert_fusion.1
  84.9 104.5 %all_to_all.15 = bf16[128,16,2048]{2,1,0:T(8,128)(2,1)S(1)} all-to-all(bf16[128,16,2048]{2,1,0:T(8,128)(2,1)S(1)} %bitcast.139), channel_id=1, replica_groups=mesh['req'=8,'exp'=16] {'req','exp'}, dimensions={0} | all-to-all | bytes 16777216 | tf_op jit(solution)/shard_map/all_to_all | solution.py:216
  189.4 4.5 %fusion.13 = f32[2048,512]{1,0:T(8,128)S(1)} fusion(bf16[2048,2048]{1,0:T(8,128)(2,1)S(1)} %bitcast.145, bf16[1,2048,512]{2,1,0:T(8,128)(2,1)S(1)} %copy-done.22), kind=kOutput, calls=%fused_computation.25 | convolution fusion | flops 4294967296 | bytes 14680064 | tf_op jit(solution)/shard_map/dot_general | solution.py:92
  193.9 5.2 %multiply_convert_fusion = bf16[2048,512]{1,0:T(8,128)(2,1)S(1)} fusion(f32[2048,512]{1,0:T(8,128)S(1)} %fusion.13, bf16[2048,2048]{1,0:T(8,128)(2,1)S(1)} %bitcast.146, bf16[1,2048,512]{2,1,0:T(8,128)(2,1)S(1)} %copy-done.23), kind=kOutput, calls=%fused_computation.12 | convolution fusion | flops 4301258752 | bytes 16777216 | tf_op jit(solution)/shard_map/dot_general | solution.py:93
  199.1 6.7 %convolution_convert_fusion = bf16[2048,2048]{1,0:T(8,128)(2,1)} fusion(bf16[2048,512]{1,0:T(8,128)(2,1)S(1)} %multiply_convert_fusion, bf16[1,512,2048]{2,1,0:T(8,128)(2,1)S(1)} %copy-done), kind=kOutput, calls=%fused_computation.4 | convolution fusion | flops 4299161600 | bytes 12582912 | tf_op jit(solution)/shard_map/dot_general | solution.py:95
  205.8 9.0 %all-to-all-start.2 = ((bf16[128,16,2048]{2,1,0:T(8,128)(2,1)}), bf16[128,16,2048]{2,1,0:T(8,128)(2,1)}, u32[]{:S(2)}, u32[]{:S(2)}) async-start(bf16[128,16,2048]{2,1,0:T(8,128)(2,1)} %bitcast.144), calls=%async_computation.2 | async-start | bytes 16777216 | tf_op jit(solution)/shard_map/all_to_all | solution.py:220
  221.0 104.4 %all-to-all-done.2 = bf16[128,16,2048]{2,1,0:T(8,128)(2,1)} async-done(((bf16[128,16,2048]{2,1,0:T(8,128)(2,1)}), bf16[128,16,2048]{2,1,0:T(8,128)(2,1)}, u32[]{:S(2)}, u32[]{:S(2)}) %all-to-all-start.2) | async-done | bytes 8388640 | tf_op jit(solution)/shard_map/all_to_all | solution.py:220
  325.4 5.5 %convolution_reduce_fusion = f32[64,2048]{1,0:T(8,128)S(1)} fusion(bf16[3,64,2048]{2,1,0:T(8,128)(2,1)} %bitcast.147, bf16[2048,2048,1]{1,0,2:T(8,128)(2,1)} %bitcast.45), kind=kOutput, calls=%fused_computation.33 | convolution fusion | flops 1610874880 | bytes 9699328 | tf_op jit(solution)/shard_map/dot_general | solution.py:228
  (141 shorter events, 44.5 us)
Async XLA Ops:
  0.6 198.5 %copy-start = (bf16[1,512,2048]{2,1,0:T(8,128)(2,1)S(1)}, bf16[1,512,2048]{2,1,0:T(8,128)(2,1)}, u32[]{:S(2)}) copy-start(bf16[1,512,2048]{2,1,0:T(8,128)(2,1)} %param.39) | copy-start | bytes 6291460
  0.7 15.8 %copy-start.18 = (s32[15]{0:T(128)S(1)}, s32[15]{0:T(128)}, u32[]{:S(2)}) copy-start(s32[15]{0:T(128)} %param.29) | copy-start | bytes 184
  1.8 40.6 %copy-start.7 = (bf16[128,512]{1,0:T(8,128)(2,1)}, bf16[128,512]{1,0:T(8,128)(2,1)S(1)}, u32[]{:S(2)}) copy-start(bf16[128,512]{1,0:T(8,128)(2,1)S(1)} %get-tuple-element.11) | copy-start | bytes 393220
  1.8 40.6 %collective-permute-start = (bf16[128,512]{1,0:T(8,128)(2,1)S(1)}, bf16[128,512]{1,0:T(8,128)(2,1)S(1)}, u32[]{:S(2)}, u32[]{:S(2)}) collective-permute-start(bf16[128,512]{1,0:T(8,128)(2,1)S(1)} %get-tuple-element.10), channel_id=1, source_target_pairs={{0,3},{1,0},{2,1},{3,2},{4,7},{5,4},{6,5},{7,6},{8,11},{9,8},{10,9... | collective-permute-start | bytes 393224 | tf_op jit(solution)/shard_map/ppermute | solution.py:99
  2.4 41.5 %collective-permute-start.1 = (bf16[128,512]{1,0:T(8,128)(2,1)S(1)}, bf16[128,512]{1,0:T(8,128)(2,1)S(1)}, u32[]{:S(2)}, u32[]{:S(2)}) collective-permute-start(bf16[128,512]{1,0:T(8,128)(2,1)S(1)} %get-tuple-element.10), channel_id=1, source_target_pairs={{0,2},{1,3},{2,0},{3,1},{4,6},{5,7},{6,4},{7,5},{8,10},{9,11},{10,... | collective-permute-start | bytes 393224 | tf_op jit(solution)/shard_map/ppermute | solution.py:99
  5.2 38.8 %collective-permute-start.2 = (bf16[128,512]{1,0:T(8,128)(2,1)S(1)}, bf16[128,512]{1,0:T(8,128)(2,1)S(1)}, u32[]{:S(2)}, u32[]{:S(2)}) collective-permute-start(bf16[128,512]{1,0:T(8,128)(2,1)S(1)} %get-tuple-element.10), channel_id=1, source_target_pairs={{0,1},{1,2},{2,3},{3,0},{4,5},{5,6},{6,7},{7,4},{8,9},{9,10},{10,1... | collective-permute-start | bytes 393224 | tf_op jit(solution)/shard_map/ppermute | solution.py:99
  5.2 45.2 %collective-permute-start.6 = (bf16[128,512]{1,0:T(8,128)(2,1)S(1)}, bf16[128,512]{1,0:T(8,128)(2,1)S(1)}, u32[]{:S(2)}, u32[]{:S(2)}) collective-permute-start(bf16[128,512]{1,0:T(8,128)(2,1)S(1)} %get-tuple-element.11), channel_id=1, source_target_pairs={{0,12},{1,13},{2,14},{3,15},{4,0},{5,1},{6,2},{7,3},{8,4},{9,5},{1... | collective-permute-start | bytes 393224 | tf_op jit(solution)/shard_map/ppermute | solution.py:99
  5.3 46.3 %collective-permute-start.7 = (bf16[128,512]{1,0:T(8,128)(2,1)S(1)}, bf16[128,512]{1,0:T(8,128)(2,1)}, u32[]{:S(2)}, u32[]{:S(2)}) collective-permute-start(bf16[128,512]{1,0:T(8,128)(2,1)S(1)} %get-tuple-element.11), channel_id=1, source_target_pairs={{0,8},{1,9},{2,10},{3,11},{4,12},{5,13},{6,14},{7,15},{8,0},{9,1},... | collective-permute-start | bytes 393224 | tf_op jit(solution)/shard_map/ppermute | solution.py:99
  28.0 11.8 %copy-start.14 = (s32[64,8]{0,1:T(8,128)S(1)}, s32[64,8]{0,1:T(8,128)}, u32[]{:S(2)}) copy-start(s32[64,8]{0,1:T(8,128)} %param.35) | copy-start | bytes 6148
  30.4 26.4 %all-to-all-start = ((bf16[16,64,128]{2,1,0:T(8,128)(2,1)}), bf16[16,64,128]{2,1,0:T(8,128)(2,1)S(1)}, u32[]{:S(2)}, u32[]{:S(2)}) async-start(bf16[16,64,128]{2,1,0:T(8,128)(2,1)} %pad_maximum_fusion.6), calls=%async_computation | async-start | bytes 524288 | tf_op jit(solution)/shard_map/all_to_all | solution.py:123
  40.5 11.1 %copy-start.8 = (s32[64,8]{1,0:T(8,128)}, s32[64,8]{1,0:T(8,128)S(1)}, u32[]{:S(2)}) copy-start(s32[64,8]{1,0:T(8,128)S(1)} %copy.58) | copy-start | bytes 6148
  42.4 9.1 %collective-permute-start.8 = (bf16[128,512]{1,0:T(8,128)(2,1)S(1)}, bf16[128,512]{1,0:T(8,128)(2,1)}, u32[]{:S(2)}, u32[]{:S(2)}) collective-permute-start(bf16[128,512]{1,0:T(8,128)(2,1)S(1)} %get-tuple-element.11), channel_id=1, source_target_pairs={{0,4},{1,5},{2,6},{3,7},{4,8},{5,9},{6,10},{7,11},{8,12},{9,13},{1... | collective-permute-start | bytes 393224 | tf_op jit(solution)/shard_map/ppermute | solution.py:99
  46.6 14.9 %collective-permute-start.3 = (bf16[4,128,512]{2,1,0:T(8,128)(2,1)}, bf16[4,128,512]{2,1,0:T(8,128)(2,1)}, u32[]{:S(2)}, u32[]{:S(2)}) collective-permute-start(bf16[4,128,512]{2,1,0:T(8,128)(2,1)} %get-tuple-element.9), channel_id=1, source_target_pairs={{0,12},{1,13},{2,14},{3,15},{4,0},{5,1},{6,2},{7,3},{8,4},{9,5},{1... | collective-permute-start | bytes 1572872 | tf_op jit(solution)/shard_map/ppermute | solution.py:99
  48.3 21.8 %collective-permute-start.4 = (bf16[4,128,512]{2,1,0:T(8,128)(2,1)}, bf16[4,128,512]{2,1,0:T(8,128)(2,1)}, u32[]{:S(2)}, u32[]{:S(2)}) collective-permute-start(bf16[4,128,512]{2,1,0:T(8,128)(2,1)} %get-tuple-element.9), channel_id=1, source_target_pairs={{0,8},{1,9},{2,10},{3,11},{4,12},{5,13},{6,14},{7,15},{8,0},{9,1},... | collective-permute-start | bytes 1572872 | tf_op jit(solution)/shard_map/ppermute | solution.py:99
  50.4 22.2 %collective-permute-start.5 = (bf16[4,128,512]{2,1,0:T(8,128)(2,1)}, bf16[4,128,512]{2,1,0:T(8,128)(2,1)}, u32[]{:S(2)}, u32[]{:S(2)}) collective-permute-start(bf16[4,128,512]{2,1,0:T(8,128)(2,1)} %get-tuple-element.9), channel_id=1, source_target_pairs={{0,4},{1,5},{2,6},{3,7},{4,8},{5,9},{6,10},{7,11},{8,12},{9,13},{1... | collective-permute-start | bytes 1572872 | tf_op jit(solution)/shard_map/ppermute | solution.py:99
  53.6 20.7 %collective-permute-start.9 = (bf16[4,128,512]{2,1,0:T(8,128)(2,1)}, bf16[4,128,512]{2,1,0:T(8,128)(2,1)}, u32[]{:S(2)}, u32[]{:S(2)}) collective-permute-start(bf16[4,128,512]{2,1,0:T(8,128)(2,1)} %get-tuple-element.13), channel_id=1, source_target_pairs={{0,3},{1,0},{2,1},{3,2},{4,7},{5,4},{6,5},{7,6},{8,11},{9,8},{10,9... | collective-permute-start | bytes 1572872 | tf_op jit(solution)/shard_map/ppermute | solution.py:99
  54.2 20.1 %collective-permute-start.10 = (bf16[4,128,512]{2,1,0:T(8,128)(2,1)}, bf16[4,128,512]{2,1,0:T(8,128)(2,1)}, u32[]{:S(2)}, u32[]{:S(2)}) collective-permute-start(bf16[4,128,512]{2,1,0:T(8,128)(2,1)} %get-tuple-element.13), channel_id=1, source_target_pairs={{0,2},{1,3},{2,0},{3,1},{4,6},{5,7},{6,4},{7,5},{8,10},{9,11},{10,... | collective-permute-start | bytes 1572872 | tf_op jit(solution)/shard_map/ppermute | solution.py:99
  61.5 16.0 %collective-permute-start.11 = (bf16[4,128,512]{2,1,0:T(8,128)(2,1)}, bf16[4,128,512]{2,1,0:T(8,128)(2,1)}, u32[]{:S(2)}, u32[]{:S(2)}) collective-permute-start(bf16[4,128,512]{2,1,0:T(8,128)(2,1)} %get-tuple-element.13), channel_id=1, source_target_pairs={{0,1},{1,2},{2,3},{3,0},{4,5},{5,6},{6,7},{7,4},{8,9},{9,10},{10,1... | collective-permute-start | bytes 1572872 | tf_op jit(solution)/shard_map/ppermute | solution.py:99
  70.2 9.5 %collective-permute-start.12 = (bf16[2,64,2048]{2,1,0:T(8,128)(2,1)S(1)}, bf16[2,64,2048]{2,1,0:T(8,128)(2,1)S(1)}, u32[]{:S(2)}, u32[]{:S(2)}) collective-permute-start(bf16[2,64,2048]{2,1,0:T(8,128)(2,1)S(1)} %pad_maximum_fusion.5), channel_id=1, source_target_pairs={{0,16},{16,0},{32,48},{48,32},{64,80},{80,64},{96,112},{112,96},{1... | collective-permute-start | bytes 1572872 | tf_op jit(solution)/shard_map/ppermute | solution.py:134
  80.7 1.6 collective-permute-start.13
  84.9 104.5 %copy-start.22 = (bf16[1,2048,512]{2,1,0:T(8,128)(2,1)S(1)}, bf16[1,2048,512]{2,1,0:T(8,128)(2,1)}, u32[]{:S(2)}) copy-start(bf16[1,2048,512]{2,1,0:T(8,128)(2,1)} %param.37) | copy-start | bytes 6291460
  205.8 10.5 %copy-start.19 = (s32[16]{0:T(128)S(1)}, s32[16]{0:T(128)}, u32[]{:S(2)}) copy-start(s32[16]{0:T(128)} %param.31) | copy-start | bytes 196
  205.8 11.8 %copy-start.17 = (bf16[16,64,128]{2,1,0:T(8,128)(2,1)S(1)}, bf16[16,64,128]{2,1,0:T(8,128)(2,1)}, u32[]{:S(2)}) copy-start(bf16[16,64,128]{2,1,0:T(8,128)(2,1)} %param.22) | copy-start | bytes 786436
  205.8 119.6 %all-to-all-start.2 = ((bf16[128,16,2048]{2,1,0:T(8,128)(2,1)}), bf16[128,16,2048]{2,1,0:T(8,128)(2,1)}, u32[]{:S(2)}, u32[]{:S(2)}) async-start(bf16[128,16,2048]{2,1,0:T(8,128)(2,1)} %bitcast.144), calls=%async_computation.2 | async-start | bytes 16777216 | tf_op jit(solution)/shard_map/all_to_all | solution.py:220
  (17 other events, 53.7 us)

commit v5 on v3

--- a/solution.py
+++ b/solution.py
@@ -125,6 +125,7 @@
     second = jnp.take(blocks, z_major, axis=0).reshape(n_exp * rows, -1)
     second = jnp.dot(second, out_weight[:, split:], preferred_element_type=jnp.float32)
     second = second.astype(jnp.bfloat16).reshape(side, side * rows, split)
+    first, second = lax.optimization_barrier((first, second))
     first = ring_sum(first, x_shifts)
     second = ring_sum(second, z_shifts)
     first = ring_sum(first.astype(jnp.bfloat16).reshape(side, rows, split), z_shifts)

time: 318 us -> 314 us (0.987)
  transfers between devices with their start and end apart: 13 -> 13, of which waited for: 7 -> 7; matrix products, arithmetic and copies ran while one was open for 5% -> 4% of each run, Pallas kernels for 0% -> 0%
where the time goes in v5:
time: 314 us
  waiting for transfers between devices  125 us (40%)
  blocking collectives  102 us (32%)
  matrix products  40.3 us (13%)
  starting transfers between devices  24 us (8%)
  other arithmetic  11.8 us (4%)
  local copies, waits for them, and re-layouts  8.8 us (3%)
    all_to_all x1, waiting for transfers between devices, per_device(): lax.all_to_all(produced, ('req', 'exp'), split_axis=0, concat_axis=0, til...  104 us
    all_to_all x1, blocking collectives, per_device(): lax.all_to_all(outgoing, ('req', 'exp'), split_axis=0, concat_axis=0, til...  102 us
    ppermute x12, waiting for transfers between devices, ring_sum(): total = total + lax.ppermute(blocks[step], 'exp', pairs).astype(jnp.float32)  21.1 us
    ppermute x12, starting transfers between devices, ring_sum(): total = total + lax.ppermute(blocks[step], 'exp', pairs).astype(jnp.float32)  15 us
    all_to_all x1, starting transfers between devices, per_device(): lax.all_to_all(produced, ('req', 'exp'), split_axis=0, concat_axis=0, til...  9.02 us
    dot_general x1, matrix products, expert_rows(): jnp.dot(activation, expert_down, preferred_element_type=jnp.float32)  6.71 us
  transfers between devices with their start and end apart: 13, of which 7 were waited for; matrix products, arithmetic and copies ran while one was open for 4% of the time, Pallas kernels for 0%

profile of v5, /device:TPU:60, one launch (start us, length us, event | category | flops | bytes accessed | tf_op | source)
XLA Modules:
  0.0 313.9 jit_solution(17521814023646065030)
XLA Ops:
  0.7 1.8 fusion.25
  5.2 3.7 %fusion.7 = (f32[15,64]{1,0:T(8,128)S(1)}, f32[15,64,1024]{2,1,0:T(8,128)S(1)}) fusion(pred[15,1024]{1,0:T(8,128)(4,1)S(1)} %iota_compare_fusion.5, bf16[16,64,128]{2,1,0:T(8,128)(2,1)S(1)} %copy-done.11, bf16[15,1024,128]{2,1,0:T(8,128)(2,1)} %param.27), kind=kOutput, calls=%fused_computation.18 | convolution fusion | flops 254606400 | bytes 8145664 | tf_op jit(solution)/shard_map/bthe,blhe->bhtl/dot_general | solution.py:51
  13.3 1.7 fusion.117
  27.4 1.9 collective-permute-start.6
  31.2 1.9 compare_reduce_fusion
  33.0 5.0 %collective-permute-done = bf16[256,1024]{1,0:T(8,128)(2,1)S(1)} collective-permute-done((bf16[256,1024]{1,0:T(8,128)(2,1)}, bf16[256,1024]{1,0:T(8,128)(2,1)S(1)}, u32[]{:S(2)}, u32[]{:S(2)}) %collective-permute-start) | collective-permute-done | bytes 524320 | tf_op jit(solution)/shard_map/ppermute | solution.py:101
  39.0 9.2 %collective-permute-done.1 = bf16[256,1024]{1,0:T(8,128)(2,1)} collective-permute-done((bf16[256,1024]{1,0:T(8,128)(2,1)}, bf16[256,1024]{1,0:T(8,128)(2,1)}, u32[]{:S(2)}, u32[]{:S(2)}) %collective-permute-start.1) | collective-permute-done | bytes 524320 | tf_op jit(solution)/shard_map/ppermute | solution.py:101
  48.2 1.8 collective-permute-done.2
  50.1 1.9 fusion.41
  52.0 2.0 collective-permute-start.3
  55.1 2.5 collective-permute-start.5
  57.7 1.6 fusion.38
  60.2 1.7 collective-permute-start.11
  62.4 3.6 %collective-permute-done.10 = bf16[64,1024]{1,0:T(8,128)(2,1)S(1)} collective-permute-done((bf16[64,1024]{1,0:T(8,128)(2,1)S(1)}, bf16[64,1024]{1,0:T(8,128)(2,1)S(1)}, u32[]{:S(2)}, u32[]{:S(2)}) %collective-permute-start.10) | collective-permute-done | bytes 131104 | tf_op jit(solution)/shard_map/ppermute | solution.py:101
  67.6 2.4 convolution_convert_fusion.1
  70.0 101.5 %all_to_all.10 = bf16[128,16,2048]{2,1,0:T(8,128)(2,1)S(1)} all-to-all(bf16[128,16,2048]{2,1,0:T(8,128)(2,1)S(1)} %bitcast.119), channel_id=1, replica_groups=mesh['req'=8,'exp'=16] {'req','exp'}, dimensions={0} | all-to-all | bytes 16777216 | tf_op jit(solution)/shard_map/all_to_all | solution.py:204
  171.5 4.5 %fusion.13 = f32[2048,512]{1,0:T(8,128)S(1)} fusion(bf16[2048,2048]{1,0:T(8,128)(2,1)S(1)} %bitcast.125, bf16[1,2048,512]{2,1,0:T(8,128)(2,1)S(1)} %copy-done.17), kind=kOutput, calls=%fused_computation.23 | convolution fusion | flops 4294967296 | bytes 14680064 | tf_op jit(solution)/shard_map/dot_general | solution.py:92
  176.1 5.2 %multiply_convert_fusion = bf16[2048,512]{1,0:T(8,128)(2,1)S(1)} fusion(f32[2048,512]{1,0:T(8,128)S(1)} %fusion.13, bf16[2048,2048]{1,0:T(8,128)(2,1)S(1)} %bitcast.126, bf16[1,2048,512]{2,1,0:T(8,128)(2,1)S(1)} %copy-done.18), kind=kOutput, calls=%fused_computation.12 | convolution fusion | flops 4301258752 | bytes 16777216 | tf_op jit(solution)/shard_map/dot_general | solution.py:93
  181.3 6.7 %convolution_convert_fusion = bf16[2048,2048]{1,0:T(8,128)(2,1)} fusion(bf16[2048,512]{1,0:T(8,128)(2,1)S(1)} %multiply_convert_fusion, bf16[1,512,2048]{2,1,0:T(8,128)(2,1)S(1)} %copy-done), kind=kOutput, calls=%fused_computation.4 | convolution fusion | flops 4299161600 | bytes 12582912 | tf_op jit(solution)/shard_map/dot_general | solution.py:95
  188.0 9.0 %all-to-all-start.1 = ((bf16[128,16,2048]{2,1,0:T(8,128)(2,1)}), bf16[128,16,2048]{2,1,0:T(8,128)(2,1)}, u32[]{:S(2)}, u32[]{:S(2)}) async-start(bf16[128,16,2048]{2,1,0:T(8,128)(2,1)} %bitcast.124), calls=%async_computation.1 | async-start | bytes 16777216 | tf_op jit(solution)/shard_map/all_to_all | solution.py:208
  197.1 1.3 fusion.1
  199.8 1.4 convolution_convert_fusion.4
  203.2 104.4 %all-to-all-done.1 = bf16[128,16,2048]{2,1,0:T(8,128)(2,1)} async-done(((bf16[128,16,2048]{2,1,0:T(8,128)(2,1)}), bf16[128,16,2048]{2,1,0:T(8,128)(2,1)}, u32[]{:S(2)}, u32[]{:S(2)}) %all-to-all-start.1) | async-done | bytes 8388640 | tf_op jit(solution)/shard_map/all_to_all | solution.py:208
  307.6 5.5 %convolution_reduce_fusion = f32[64,2048]{1,0:T(8,128)S(1)} fusion(bf16[3,64,2048]{2,1,0:T(8,128)(2,1)} %bitcast.129, bf16[2048,2048,1]{1,0,2:T(8,128)(2,1)} %bitcast.35), kind=kOutput, calls=%fused_computation.33 | convolution fusion | flops 1610874880 | bytes 9699328 | tf_op jit(solution)/shard_map/dot_general | solution.py:216
  (120 shorter events, 29.6 us)
Async XLA Ops:
  0.6 180.6 %copy-start = (bf16[1,512,2048]{2,1,0:T(8,128)(2,1)S(1)}, bf16[1,512,2048]{2,1,0:T(8,128)(2,1)}, u32[]{:S(2)}) copy-start(bf16[1,512,2048]{2,1,0:T(8,128)(2,1)} %param.39) | copy-start | bytes 6291460
  0.7 4.5 %copy-start.14 = (s32[15]{0:T(128)S(1)}, s32[15]{0:T(128)}, u32[]{:S(2)}) copy-start(s32[15]{0:T(128)} %param.29) | copy-start | bytes 184
  20.9 6.5 %copy-start.1 = (bf16[1024,1024]{1,0:T(8,128)(2,1)}, bf16[1024,1024]{1,0:T(8,128)(2,1)S(1)}, u32[]{:S(2)}) copy-start(bf16[1024,1024]{1,0:T(8,128)(2,1)S(1)} %convolution_convert_fusion.2) | copy-start | bytes 6291460
  21.0 9.4 %copy-start.9 = (s32[64,8]{0,1:T(8,128)S(1)}, s32[64,8]{0,1:T(8,128)}, u32[]{:S(2)}) copy-start(s32[64,8]{0,1:T(8,128)} %param.35) | copy-start | bytes 6148
  21.7 5.7 %copy-start.2 = (bf16[1024,1024]{1,0:T(8,128)(2,1)}, bf16[1024,1024]{1,0:T(8,128)(2,1)S(1)}, u32[]{:S(2)}) copy-start(bf16[1024,1024]{1,0:T(8,128)(2,1)S(1)} %convolution_convert_fusion.3) | copy-start | bytes 6291460
  23.0 15.0 %collective-permute-start = (bf16[256,1024]{1,0:T(8,128)(2,1)}, bf16[256,1024]{1,0:T(8,128)(2,1)S(1)}, u32[]{:S(2)}, u32[]{:S(2)}) collective-permute-start(bf16[256,1024]{1,0:T(8,128)(2,1)} %get-tuple-element.8), channel_id=1, source_target_pairs={{0,1},{1,2},{2,3},{3,0},{4,5},{5,6},{6,7},{7,4},{8,9},{9,10},{10,1... | collective-permute-start | bytes 1572872 | tf_op jit(solution)/shard_map/ppermute | solution.py:101
  24.2 24.0 %collective-permute-start.1 = (bf16[256,1024]{1,0:T(8,128)(2,1)}, bf16[256,1024]{1,0:T(8,128)(2,1)}, u32[]{:S(2)}, u32[]{:S(2)}) collective-permute-start(bf16[256,1024]{1,0:T(8,128)(2,1)} %get-tuple-element.10), channel_id=1, source_target_pairs={{0,2},{1,3},{2,0},{3,1},{4,6},{5,7},{6,4},{7,5},{8,10},{9,11},{10,... | collective-permute-start | bytes 1572872 | tf_op jit(solution)/shard_map/ppermute | solution.py:101
  25.0 25.0 %collective-permute-start.2 = (bf16[256,1024]{1,0:T(8,128)(2,1)}, bf16[256,1024]{1,0:T(8,128)(2,1)}, u32[]{:S(2)}, u32[]{:S(2)}) collective-permute-start(bf16[256,1024]{1,0:T(8,128)(2,1)} %get-tuple-element.9), channel_id=1, source_target_pairs={{0,3},{1,0},{2,1},{3,2},{4,7},{5,4},{6,5},{7,6},{8,11},{9,8},{10,9... | collective-permute-start | bytes 1572872 | tf_op jit(solution)/shard_map/ppermute | solution.py:101
  27.4 27.8 %collective-permute-start.6 = (bf16[256,1024]{1,0:T(8,128)(2,1)}, bf16[256,1024]{1,0:T(8,128)(2,1)S(1)}, u32[]{:S(2)}, u32[]{:S(2)}) collective-permute-start(bf16[256,1024]{1,0:T(8,128)(2,1)} %get-tuple-element.11), channel_id=1, source_target_pairs={{0,4},{1,5},{2,6},{3,7},{4,8},{5,9},{6,10},{7,11},{8,12},{9,13},{1... | collective-permute-start | bytes 1572872 | tf_op jit(solution)/shard_map/ppermute | solution.py:101
  29.3 28.4 %collective-permute-start.7 = (bf16[256,1024]{1,0:T(8,128)(2,1)}, bf16[256,1024]{1,0:T(8,128)(2,1)}, u32[]{:S(2)}, u32[]{:S(2)}) collective-permute-start(bf16[256,1024]{1,0:T(8,128)(2,1)} %get-tuple-element.13), channel_id=1, source_target_pairs={{0,8},{1,9},{2,10},{3,11},{4,12},{5,13},{6,14},{7,15},{8,0},{9,1},... | collective-permute-start | bytes 1572872 | tf_op jit(solution)/shard_map/ppermute | solution.py:101
  38.9 28.5 %copy-start.3 = (f32[64,2048]{1,0:T(8,128)S(1)}, f32[64,2048]{1,0:T(8,128)}, u32[]{:S(2)}) copy-start(f32[64,2048]{1,0:T(8,128)} %param.32) | copy-start | bytes 1572868
  38.9 18.8 %collective-permute-start.8 = (bf16[256,1024]{1,0:T(8,128)(2,1)}, bf16[256,1024]{1,0:T(8,128)(2,1)S(1)}, u32[]{:S(2)}, u32[]{:S(2)}) collective-permute-start(bf16[256,1024]{1,0:T(8,128)(2,1)} %get-tuple-element.12), channel_id=1, source_target_pairs={{0,12},{1,13},{2,14},{3,15},{4,0},{5,1},{6,2},{7,3},{8,4},{9,5},{1... | collective-permute-start | bytes 1572872 | tf_op jit(solution)/shard_map/ppermute | solution.py:101
  52.0 15.6 %copy-start.10 = (f32[2048]{0:T(1024)S(1)}, f32[2048]{0:T(1024)}, u32[]{:S(2)}) copy-start(f32[2048]{0:T(1024)} %param.34) | copy-start | bytes 24580
  52.0 9.9 %collective-permute-start.3 = (bf16[64,1024]{1,0:T(8,128)(2,1)S(1)}, bf16[64,1024]{1,0:T(8,128)(2,1)S(1)}, u32[]{:S(2)}, u32[]{:S(2)}) collective-permute-start(bf16[64,1024]{1,0:T(8,128)(2,1)S(1)} %get-tuple-element.16), channel_id=1, source_target_pairs={{0,4},{1,5},{2,6},{3,7},{4,8},{5,9},{6,10},{7,11},{8,12},{9,13},{1... | collective-permute-start | bytes 393224 | tf_op jit(solution)/shard_map/ppermute | solution.py:101
  54.0 8.3 %collective-permute-start.4 = (bf16[64,1024]{1,0:T(8,128)(2,1)S(1)}, bf16[64,1024]{1,0:T(8,128)(2,1)S(1)}, u32[]{:S(2)}, u32[]{:S(2)}) collective-permute-start(bf16[64,1024]{1,0:T(8,128)(2,1)S(1)} %get-tuple-element.18), channel_id=1, source_target_pairs={{0,8},{1,9},{2,10},{3,11},{4,12},{5,13},{6,14},{7,15},{8,0},{9,1},... | collective-permute-start | bytes 393224 | tf_op jit(solution)/shard_map/ppermute | solution.py:101
  55.1 7.1 %collective-permute-start.5 = (bf16[64,1024]{1,0:T(8,128)(2,1)S(1)}, bf16[64,1024]{1,0:T(8,128)(2,1)S(1)}, u32[]{:S(2)}, u32[]{:S(2)}) collective-permute-start(bf16[64,1024]{1,0:T(8,128)(2,1)S(1)} %get-tuple-element.17), channel_id=1, source_target_pairs={{0,12},{1,13},{2,14},{3,15},{4,0},{5,1},{6,2},{7,3},{8,4},{9,5},{1... | collective-permute-start | bytes 393224 | tf_op jit(solution)/shard_map/ppermute | solution.py:101
  59.3 6.7 %collective-permute-start.10 = (bf16[64,1024]{1,0:T(8,128)(2,1)S(1)}, bf16[64,1024]{1,0:T(8,128)(2,1)S(1)}, u32[]{:S(2)}, u32[]{:S(2)}) collective-permute-start(bf16[64,1024]{1,0:T(8,128)(2,1)S(1)} %get-tuple-element.21), channel_id=1, source_target_pairs={{0,2},{1,3},{2,0},{3,1},{4,6},{5,7},{6,4},{7,5},{8,10},{9,11},{10,... | collective-permute-start | bytes 393224 | tf_op jit(solution)/shard_map/ppermute | solution.py:101
  60.2 6.7 %collective-permute-start.11 = (bf16[64,1024]{1,0:T(8,128)(2,1)S(1)}, bf16[64,1024]{1,0:T(8,128)(2,1)S(1)}, u32[]{:S(2)}, u32[]{:S(2)}) collective-permute-start(bf16[64,1024]{1,0:T(8,128)(2,1)S(1)} %get-tuple-element.20), channel_id=1, source_target_pairs={{0,3},{1,0},{2,1},{3,2},{4,7},{5,4},{6,5},{7,6},{8,11},{9,8},{10,9... | collective-permute-start | bytes 393224 | tf_op jit(solution)/shard_map/ppermute | solution.py:101
  61.9 5.4 %collective-permute-start.9 = (bf16[64,1024]{1,0:T(8,128)(2,1)S(1)}, bf16[64,1024]{1,0:T(8,128)(2,1)S(1)}, u32[]{:S(2)}, u32[]{:S(2)}) collective-permute-start(bf16[64,1024]{1,0:T(8,128)(2,1)S(1)} %get-tuple-element.19), channel_id=1, source_target_pairs={{0,1},{1,2},{2,3},{3,0},{4,5},{5,6},{6,7},{7,4},{8,9},{9,10},{10,1... | collective-permute-start | bytes 393224 | tf_op jit(solution)/shard_map/ppermute | solution.py:101
  70.0 101.5 %copy-start.17 = (bf16[1,2048,512]{2,1,0:T(8,128)(2,1)S(1)}, bf16[1,2048,512]{2,1,0:T(8,128)(2,1)}, u32[]{:S(2)}) copy-start(bf16[1,2048,512]{2,1,0:T(8,128)(2,1)} %param.37) | copy-start | bytes 6291460
  171.5 4.5 %copy-start.18 = (bf16[1,2048,512]{2,1,0:T(8,128)(2,1)S(1)}, bf16[1,2048,512]{2,1,0:T(8,128)(2,1)}, u32[]{:S(2)}) copy-start(bf16[1,2048,512]{2,1,0:T(8,128)(2,1)} %param.38) | copy-start | bytes 6291460
  188.0 9.0 %copy-start.12 = (f32[64,8]{0,1:T(8,128)S(1)}, f32[64,8]{0,1:T(8,128)}, u32[]{:S(2)}) copy-start(f32[64,8]{0,1:T(8,128)} %param.36) | copy-start | bytes 6148
  188.0 10.5 %copy-start.15 = (s32[16]{0:T(128)S(1)}, s32[16]{0:T(128)}, u32[]{:S(2)}) copy-start(s32[16]{0:T(128)} %param.31) | copy-start | bytes 196
  188.0 119.6 %all-to-all-start.1 = ((bf16[128,16,2048]{2,1,0:T(8,128)(2,1)}), bf16[128,16,2048]{2,1,0:T(8,128)(2,1)}, u32[]{:S(2)}, u32[]{:S(2)}) async-start(bf16[128,16,2048]{2,1,0:T(8,128)(2,1)} %bitcast.124), calls=%async_computation.1 | async-start | bytes 16777216 | tf_op jit(solution)/shard_map/all_to_all | solution.py:208
  (9 other events, 17.5 us)

commit v6 on v3

--- a/solution.py
+++ b/solution.py
@@ -45,6 +45,7 @@
     heads = width // HEAD
     scale = HEAD ** (-0.5)
     shape_q = (batch, tokens_per, heads, HEAD)
+    shape_n = (batch, new_keys.shape[1], heads, HEAD)
     shape_c = (batch, cache_keys.shape[1], heads, HEAD)
     query_four = queries.reshape(shape_q)
     cache_scores = (
@@ -62,7 +63,7 @@
         jnp.einsum(
             "bthe,bshe->bhts",
             query_four,
-            new_keys.reshape(shape_q),
+            new_keys.reshape(shape_n),
             preferred_element_type=jnp.float32,
         )
         * scale
@@ -81,7 +82,7 @@
     mixed = mixed + jnp.einsum(
         "bhts,bshe->bthe",
         draft_probs.astype(jnp.bfloat16),
-        new_values.reshape(shape_q),
+        new_values.reshape(shape_n),
         preferred_element_type=jnp.float32,
     )
     mixed = mixed / jnp.transpose(totals, (0, 2, 1))[..., None]
@@ -102,7 +103,7 @@
     return total
 
 
-def ring_reduce_scatter(attended, out_weight, n_exp):
+def half_reduce_scatter(attended, out_weight, n_exp, x_first):
     side = 4
     assert n_exp == side * side
     index = lax.axis_index("exp")
@@ -112,24 +113,20 @@
     z_shifts = [[(z * side + x, ((z + k) % side) * side + x) for z, x in cells] for k in range(1, side)]
     rows = attended.shape[0] // n_exp
     width = out_weight.shape[1]
-    split = width // 2
     blocks = attended.reshape(n_exp, rows, -1)
     near = jnp.arange(side, dtype=jnp.int32)
     z_of = (z_pos + near) % side
     x_of = (x_pos + near) % side
-    x_major = (x_of[:, None] + z_of[None, :] * side).reshape(-1)
-    z_major = (z_of[:, None] * side + x_of[None, :]).reshape(-1)
-    first = jnp.take(blocks, x_major, axis=0).reshape(n_exp * rows, -1)
-    first = jnp.dot(first, out_weight[:, :split], preferred_element_type=jnp.float32)
-    first = first.astype(jnp.bfloat16).reshape(side, side * rows, split)
-    second = jnp.take(blocks, z_major, axis=0).reshape(n_exp * rows, -1)
-    second = jnp.dot(second, out_weight[:, split:], preferred_element_type=jnp.float32)
-    second = second.astype(jnp.bfloat16).reshape(side, side * rows, split)
-    first = ring_sum(first, x_shifts)
-    second = ring_sum(second, z_shifts)
-    first = ring_sum(first.astype(jnp.bfloat16).reshape(side, rows, split), z_shifts)
-    second = ring_sum(second.astype(jnp.bfloat16).reshape(side, rows, split), x_shifts)
-    return jnp.concatenate([first, second], axis=1)
+    if x_first:
+        order = (x_of[:, None] + z_of[None, :] * side).reshape(-1)
+        first_shifts, second_shifts = x_shifts, z_shifts
+    else:
+        order = (z_of[:, None] * side + x_of[None, :]).reshape(-1)
+        first_shifts, second_shifts = z_shifts, x_shifts
+    part = jnp.take(blocks, order, axis=0).reshape(n_exp * rows, -1)
+    part = jnp.dot(part, out_weight, preferred_element_type=jnp.float32)
+    part = ring_sum(part.astype(jnp.bfloat16).reshape(side, side * rows, width), first_shifts)
+    return ring_sum(part.astype(jnp.bfloat16).reshape(side, rows, width), second_shifts)
 
 
 def per_device(
@@ -159,22 +156,34 @@
     compacted = compact_path(reached, accepted, stacked)
     accepted_keys = compacted[:, :, :head_width]
     accepted_values = compacted[:, :, head_width:]
-    long_out = attend(
-        queries[:1], long_keys, long_values, long_lengths, new_keys[:1], new_values[:1], reached[:1]
-    )
-    short_out = attend(
-        queries[1:],
-        short_keys,
-        short_values,
-        short_lengths,
-        new_keys[1:],
-        new_values[1:],
-        reached[1:],
-    )
-    attended = jnp.concatenate([long_out, short_out], axis=0).reshape(-1, head_width)
     n_exp = lax.axis_size("exp")
+    halves = 2
+    q_rows = queries.shape[1] // halves
+    reduced = []
+    for half in range(halves):
+        rows = slice(half * q_rows, (half + 1) * q_rows)
+        long_out = attend(
+            queries[:1, rows],
+            long_keys,
+            long_values,
+            long_lengths,
+            new_keys[:1],
+            new_values[:1],
+            reached[:1, rows],
+        )
+        short_out = attend(
+            queries[1:, rows],
+            short_keys,
+            short_values,
+            short_lengths,
+            new_keys[1:],
+            new_values[1:],
+            reached[1:, rows],
+        )
+        attended = jnp.concatenate([long_out, short_out], axis=0).reshape(-1, head_width)
+        reduced.append(half_reduce_scatter(attended, out_weight, n_exp, half == 0))
+    attn_proj = jnp.concatenate(reduced, axis=0)
     model_width = out_weight.shape[1]
-    attn_proj = ring_reduce_scatter(attended, out_weight, n_exp)
     middle = residual + attn_proj
     normed = (
         middle * lax.rsqrt(jnp.mean(middle * middle, axis=1, keepdims=True) + 1e-05) * norm_gain

time: 318 us -> 335 us (1.053)
  matrix products: 40.3 us -> 54.2 us
  other arithmetic: 11.8 us -> 16.4 us
    dot_general x2 -> x4, matrix products: 5.38 us -> 11.9 us  [attend(): jnp.einsum('bthe,blhe->bhtl', query_four, cache_keys.reshape(shape_c), pr...]
    dot_general x2 -> x4, matrix products: 2.23 us -> 6.65 us  [attend(): jnp.einsum('bhtl,blhe->bthe', cache_probs.astype(jnp.bfloat16), cache_val...]
  transfers between devices with their start and end apart: 13 -> 13, of which waited for: 7 -> 5; matrix products, arithmetic and copies ran while one was open for 5% -> 8% of each run, Pallas kernels for 0% -> 0%
where the time goes in v6:
time: 335 us; the launch traced here: 334 us
  waiting for transfers between devices  125 us (37%)
  blocking collectives  102 us (30%)
  matrix products  54.2 us (16%)
  starting transfers between devices  26.2 us (8%)
  other arithmetic  16.4 us (5%)
  local copies, waits for them, and re-layouts  9.07 us (3%)
    all_to_all x1, waiting for transfers between devices, per_device(): lax.all_to_all(produced, ('req', 'exp'), split_axis=0, concat_axis=0, til...  105 us
    all_to_all x1, blocking collectives, per_device(): lax.all_to_all(outgoing, ('req', 'exp'), split_axis=0, concat_axis=0, til...  102 us
    ppermute x12, waiting for transfers between devices, ring_sum(): total = total + lax.ppermute(blocks[step], 'exp', pairs).astype(jnp.float32)  19.9 us
    ppermute x12, starting transfers between devices, ring_sum(): total = total + lax.ppermute(blocks[step], 'exp', pairs).astype(jnp.float32)  17.2 us
    dot_general x4, matrix products, attend(): jnp.einsum('bthe,blhe->bhtl', query_four, cache_keys.reshape(shape_c), pr...  11.9 us
    all_to_all x1, starting transfers between devices, per_device(): lax.all_to_all(produced, ('req', 'exp'), split_axis=0, concat_axis=0, til...  9.05 us
    dot_general x1, matrix products, expert_rows(): jnp.dot(activation, expert_down, preferred_element_type=jnp.float32)  6.86 us
  transfers between devices with their start and end apart: 13, of which 5 were waited for; matrix products, arithmetic and copies ran while one was open for 8% of the time, Pallas kernels for 0%

profile of v6, /device:TPU:60, one launch (start us, length us, event | category | flops | bytes accessed | tf_op | source)
XLA Modules:
  0.0 334.4 jit_solution(14897968656193712992)
XLA Ops:
  7.0 3.8 %fusion.17 = (f32[15,32]{1,0:T(8,128)S(1)}, f32[15,32,1024]{2,1,0:T(8,128)S(1)}) fusion(pred[15,1024]{1,0:T(8,128)(4,1)S(1)} %iota_compare_fusion.5, bf16[15,1024,128]{2,1,0:T(8,128)(2,1)} %param.27, bf16[16,64,128]{2,1,0:T(8,128)(2,1)S(1)} %copy-done.16), kind=kOutput, calls=%fused_computation.34 | convolution fusion | flops 127303200 | bytes 6039424 | tf_op jit(solution)/shard_map/bthe,blhe->bhtl/dot_general | solution.py:52
  10.8 3.6 %fusion.19 = (f32[15,32]{1,0:T(8,128)S(1)}, f32[15,32]{1,0:T(8,128)}, f32[15,32,1024]{2,1,0:T(8,128)}) fusion(f32[15,32,1024]{2,1,0:T(8,128)S(1)} %get-tuple-element.26, f32[15,32]{1,0:T(8,128)S(1)} %max.47, pred[15,1024]{1,0:T(8,128)(4,1)S(1)} %iota_compare_fusion.5, bf16[15,1024,128]{2,1,0:T(8,128)(2,1)S(1)} %copy-done.6, ...), kind=kOutput, calls=%fused_computation.36 | convolution fusion | flops 129268800 | bytes 8015616 | tf_op jit(solution)/shard_map/bthe,blhe->bhtl/dot_general | solution.py:52
  32.1 2.9 fusion.190
  36.6 2.2 fusion.15
  40.1 3.1 fusion.60
  47.2 1.9 collective-permute-start.6
  50.9 1.9 compare_reduce_fusion
  52.8 2.7 collective-permute-start.8
  55.5 1.9 add_convert_fusion.1
  57.5 3.1 collective-permute-start.4
  60.5 12.7 %collective-permute-done.6 = bf16[128,2048]{1,0:T(8,128)(2,1)S(1)} collective-permute-done((bf16[128,2048]{1,0:T(8,128)(2,1)}, bf16[128,2048]{1,0:T(8,128)(2,1)S(1)}, u32[]{:S(2)}, u32[]{:S(2)}) %collective-permute-start.6) | collective-permute-done | bytes 524320 | tf_op jit(solution)/shard_map/ppermute | solution.py:102
  74.2 1.9 collective-permute-done.8
  77.8 3.1 collective-permute-start.10
  80.9 2.0 collective-permute-start.9
  83.0 1.9 collective-permute-done.10
  85.0 3.3 collective-permute-done.11
  88.5 2.4 convolution_convert_fusion.1
  91.0 101.6 %all_to_all.10 = bf16[128,16,2048]{2,1,0:T(8,128)(2,1)S(1)} all-to-all(bf16[128,16,2048]{2,1,0:T(8,128)(2,1)S(1)} %bitcast.174), channel_id=1, replica_groups=mesh['req'=8,'exp'=16] {'req','exp'}, dimensions={0} | all-to-all | bytes 16777216 | tf_op jit(solution)/shard_map/all_to_all | solution.py:212
  192.6 4.5 %fusion.11 = f32[2048,512]{1,0:T(8,128)S(1)} fusion(bf16[2048,2048]{1,0:T(8,128)(2,1)S(1)} %bitcast.176, bf16[1,2048,512]{2,1,0:T(8,128)(2,1)S(1)} %copy-done.31), kind=kOutput, calls=%fused_computation.22 | convolution fusion | flops 4294967296 | bytes 14680064 | tf_op jit(solution)/shard_map/dot_general | solution.py:93
  197.1 5.2 %multiply_convert_fusion = bf16[2048,512]{1,0:T(8,128)(2,1)S(1)} fusion(f32[2048,512]{1,0:T(8,128)S(1)} %fusion.11, bf16[2048,2048]{1,0:T(8,128)(2,1)S(1)} %bitcast.177, bf16[1,2048,512]{2,1,0:T(8,128)(2,1)S(1)} %copy-done.32), kind=kOutput, calls=%fused_computation.17 | convolution fusion | flops 4301258752 | bytes 16777216 | tf_op jit(solution)/shard_map/dot_general | solution.py:94
  202.3 6.9 %convolution_convert_fusion = bf16[2048,2048]{1,0:T(8,128)(2,1)} fusion(bf16[2048,512]{1,0:T(8,128)(2,1)S(1)} %multiply_convert_fusion, bf16[1,512,2048]{2,1,0:T(8,128)(2,1)S(1)} %copy-done), kind=kOutput, calls=%fused_computation.6 | convolution fusion | flops 4299161600 | bytes 12582912 | tf_op jit(solution)/shard_map/dot_general | solution.py:96
  209.2 9.0 %all-to-all-start.1 = ((bf16[128,16,2048]{2,1,0:T(8,128)(2,1)}), bf16[128,16,2048]{2,1,0:T(8,128)(2,1)}, u32[]{:S(2)}, u32[]{:S(2)}) async-start(bf16[128,16,2048]{2,1,0:T(8,128)(2,1)} %bitcast.175), calls=%async_computation.1 | async-start | bytes 16777216 | tf_op jit(solution)/shard_map/all_to_all | solution.py:216
  223.3 104.7 %all-to-all-done.1 = bf16[128,16,2048]{2,1,0:T(8,128)(2,1)} async-done(((bf16[128,16,2048]{2,1,0:T(8,128)(2,1)}), bf16[128,16,2048]{2,1,0:T(8,128)(2,1)}, u32[]{:S(2)}, u32[]{:S(2)}) %all-to-all-start.1) | async-done | bytes 8388640 | tf_op jit(solution)/shard_map/all_to_all | solution.py:216
  328.0 5.5 %convolution_reduce_fusion = f32[64,2048]{1,0:T(8,128)S(1)} fusion(bf16[3,64,2048]{2,1,0:T(8,128)(2,1)} %bitcast.178, bf16[2048,2048,1]{1,0,2:T(8,128)(2,1)} %bitcast.35), kind=kOutput, calls=%fused_computation.40 | convolution fusion | flops 1610874880 | bytes 9699328 | tf_op jit(solution)/shard_map/dot_general | solution.py:224
  (164 shorter events, 40.2 us)
Async XLA Ops:
  0.6 201.7 %copy-start = (bf16[1,512,2048]{2,1,0:T(8,128)(2,1)S(1)}, bf16[1,512,2048]{2,1,0:T(8,128)(2,1)}, u32[]{:S(2)}) copy-start(bf16[1,512,2048]{2,1,0:T(8,128)(2,1)} %param.39) | copy-start | bytes 6291460
  23.1 6.1 %copy-start.24 = (f32[15,32]{1,0:T(8,128)S(1)}, f32[15,32]{1,0:T(8,128)}, u32[]{:S(2)}) copy-start(f32[15,32]{1,0:T(8,128)} %get-tuple-element.5) | copy-start | bytes 5764
  23.8 5.3 %copy-start.9 = (bf16[512,2048]{1,0:T(8,128)(2,1)}, bf16[512,2048]{1,0:T(8,128)(2,1)S(1)}, u32[]{:S(2)}) copy-start(bf16[512,2048]{1,0:T(8,128)(2,1)S(1)} %convolution_convert_fusion.3) | copy-start | bytes 6291460
  23.9 6.0 %copy-start.8 = (bf16[15,1024,128]{2,1,0:T(8,128)(2,1)S(1)}, bf16[15,1024,128]{2,1,0:T(8,128)(2,1)}, u32[]{:S(2)}) copy-start(bf16[15,1024,128]{2,1,0:T(8,128)(2,1)} %param.28) | copy-start | bytes 11796484
  25.1 27.7 %collective-permute-start = (bf16[128,2048]{1,0:T(8,128)(2,1)}, bf16[128,2048]{1,0:T(8,128)(2,1)}, u32[]{:S(2)}, u32[]{:S(2)}) collective-permute-start(bf16[128,2048]{1,0:T(8,128)(2,1)} %get-tuple-element.6), channel_id=1, source_target_pairs={{0,1},{1,2},{2,3},{3,0},{4,5},{5,6},{6,7},{7,4},{8,9},{9,10},{10,1... | collective-permute-start | bytes 1572872 | tf_op jit(solution)/shard_map/ppermute | solution.py:102
  26.3 29.2 %collective-permute-start.1 = (bf16[128,2048]{1,0:T(8,128)(2,1)}, bf16[128,2048]{1,0:T(8,128)(2,1)}, u32[]{:S(2)}, u32[]{:S(2)}) collective-permute-start(bf16[128,2048]{1,0:T(8,128)(2,1)} %get-tuple-element.8), channel_id=1, source_target_pairs={{0,2},{1,3},{2,0},{3,1},{4,6},{5,7},{6,4},{7,5},{8,10},{9,11},{10,... | collective-permute-start | bytes 1572872 | tf_op jit(solution)/shard_map/ppermute | solution.py:102
  27.1 28.4 %collective-permute-start.2 = (bf16[128,2048]{1,0:T(8,128)(2,1)}, bf16[128,2048]{1,0:T(8,128)(2,1)}, u32[]{:S(2)}, u32[]{:S(2)}) collective-permute-start(bf16[128,2048]{1,0:T(8,128)(2,1)} %get-tuple-element.7), channel_id=1, source_target_pairs={{0,3},{1,0},{2,1},{3,2},{4,7},{5,4},{6,5},{7,6},{8,11},{9,8},{10,9... | collective-permute-start | bytes 1572872 | tf_op jit(solution)/shard_map/ppermute | solution.py:102
  47.2 26.1 %collective-permute-start.6 = (bf16[128,2048]{1,0:T(8,128)(2,1)}, bf16[128,2048]{1,0:T(8,128)(2,1)S(1)}, u32[]{:S(2)}, u32[]{:S(2)}) collective-permute-start(bf16[128,2048]{1,0:T(8,128)(2,1)} %get-tuple-element.9), channel_id=1, source_target_pairs={{0,4},{1,5},{2,6},{3,7},{4,8},{5,9},{6,10},{7,11},{8,12},{9,13},{1... | collective-permute-start | bytes 1572872 | tf_op jit(solution)/shard_map/ppermute | solution.py:102
  49.1 25.1 %collective-permute-start.7 = (bf16[128,2048]{1,0:T(8,128)(2,1)}, bf16[128,2048]{1,0:T(8,128)(2,1)}, u32[]{:S(2)}, u32[]{:S(2)}) collective-permute-start(bf16[128,2048]{1,0:T(8,128)(2,1)} %get-tuple-element.11), channel_id=1, source_target_pairs={{0,8},{1,9},{2,10},{3,11},{4,12},{5,13},{6,14},{7,15},{8,0},{9,1},... | collective-permute-start | bytes 1572872 | tf_op jit(solution)/shard_map/ppermute | solution.py:102
  52.8 23.3 %collective-permute-start.8 = (bf16[128,2048]{1,0:T(8,128)(2,1)}, bf16[128,2048]{1,0:T(8,128)(2,1)S(1)}, u32[]{:S(2)}, u32[]{:S(2)}) collective-permute-start(bf16[128,2048]{1,0:T(8,128)(2,1)} %get-tuple-element.10), channel_id=1, source_target_pairs={{0,12},{1,13},{2,14},{3,15},{4,0},{5,1},{6,2},{7,3},{8,4},{9,5},{1... | collective-permute-start | bytes 1572872 | tf_op jit(solution)/shard_map/ppermute | solution.py:102
  57.4 23.5 %collective-permute-start.3 = (bf16[32,2048]{1,0:T(8,128)(2,1)S(1)}, bf16[32,2048]{1,0:T(8,128)(2,1)S(1)}, u32[]{:S(2)}, u32[]{:S(2)}) collective-permute-start(bf16[32,2048]{1,0:T(8,128)(2,1)S(1)} %get-tuple-element.14), channel_id=1, source_target_pairs={{0,4},{1,5},{2,6},{3,7},{4,8},{5,9},{6,10},{7,11},{8,12},{9,13},{1... | collective-permute-start | bytes 393224 | tf_op jit(solution)/shard_map/ppermute | solution.py:102
  57.5 25.5 %collective-permute-start.4 = (bf16[32,2048]{1,0:T(8,128)(2,1)S(1)}, bf16[32,2048]{1,0:T(8,128)(2,1)S(1)}, u32[]{:S(2)}, u32[]{:S(2)}) collective-permute-start(bf16[32,2048]{1,0:T(8,128)(2,1)S(1)} %get-tuple-element.16), channel_id=1, source_target_pairs={{0,8},{1,9},{2,10},{3,11},{4,12},{5,13},{6,14},{7,15},{8,0},{9,1},... | collective-permute-start | bytes 393224 | tf_op jit(solution)/shard_map/ppermute | solution.py:102
  74.1 14.3 %copy-start.11 = (f32[64,2048]{1,0:T(8,128)S(1)}, f32[64,2048]{1,0:T(8,128)}, u32[]{:S(2)}) copy-start(f32[64,2048]{1,0:T(8,128)} %param.32) | copy-start | bytes 1572868
  74.1 8.9 %collective-permute-start.5 = (bf16[32,2048]{1,0:T(8,128)(2,1)S(1)}, bf16[32,2048]{1,0:T(8,128)(2,1)S(1)}, u32[]{:S(2)}, u32[]{:S(2)}) collective-permute-start(bf16[32,2048]{1,0:T(8,128)(2,1)S(1)} %get-tuple-element.15), channel_id=1, source_target_pairs={{0,12},{1,13},{2,14},{3,15},{4,0},{5,1},{6,2},{7,3},{8,4},{9,5},{1... | collective-permute-start | bytes 393224 | tf_op jit(solution)/shard_map/ppermute | solution.py:102
  77.7 10.8 %copy-start.26 = (f32[2048]{0:T(1024)S(1)}, f32[2048]{0:T(1024)}, u32[]{:S(2)}) copy-start(f32[2048]{0:T(1024)} %param.34) | copy-start | bytes 24580
  77.8 7.2 %collective-permute-start.10 = (bf16[32,2048]{1,0:T(8,128)(2,1)S(1)}, bf16[32,2048]{1,0:T(8,128)(2,1)S(1)}, u32[]{:S(2)}, u32[]{:S(2)}) collective-permute-start(bf16[32,2048]{1,0:T(8,128)(2,1)S(1)} %get-tuple-element.19), channel_id=1, source_target_pairs={{0,2},{1,3},{2,0},{3,1},{4,6},{5,7},{6,4},{7,5},{8,10},{9,11},{10,... | collective-permute-start | bytes 393224 | tf_op jit(solution)/shard_map/ppermute | solution.py:102
  80.9 7.3 %collective-permute-start.11 = (bf16[32,2048]{1,0:T(8,128)(2,1)S(1)}, bf16[32,2048]{1,0:T(8,128)(2,1)S(1)}, u32[]{:S(2)}, u32[]{:S(2)}) collective-permute-start(bf16[32,2048]{1,0:T(8,128)(2,1)S(1)} %get-tuple-element.18), channel_id=1, source_target_pairs={{0,3},{1,0},{2,1},{3,2},{4,7},{5,4},{6,5},{7,6},{8,11},{9,8},{10,9... | collective-permute-start | bytes 393224 | tf_op jit(solution)/shard_map/ppermute | solution.py:102
  80.9 7.3 %collective-permute-start.9 = (bf16[32,2048]{1,0:T(8,128)(2,1)S(1)}, bf16[32,2048]{1,0:T(8,128)(2,1)S(1)}, u32[]{:S(2)}, u32[]{:S(2)}) collective-permute-start(bf16[32,2048]{1,0:T(8,128)(2,1)S(1)} %get-tuple-element.17), channel_id=1, source_target_pairs={{0,1},{1,2},{2,3},{3,0},{4,5},{5,6},{6,7},{7,4},{8,9},{9,10},{10,1... | collective-permute-start | bytes 393224 | tf_op jit(solution)/shard_map/ppermute | solution.py:102
  91.0 101.6 %copy-start.31 = (bf16[1,2048,512]{2,1,0:T(8,128)(2,1)S(1)}, bf16[1,2048,512]{2,1,0:T(8,128)(2,1)}, u32[]{:S(2)}) copy-start(bf16[1,2048,512]{2,1,0:T(8,128)(2,1)} %param.37) | copy-start | bytes 6291460
  209.2 9.1 %copy-start.28 = (f32[64,8]{0,1:T(8,128)S(1)}, f32[64,8]{0,1:T(8,128)}, u32[]{:S(2)}) copy-start(f32[64,8]{0,1:T(8,128)} %param.36) | copy-start | bytes 6148
  209.2 10.5 %copy-start.30 = (s32[16]{0:T(128)S(1)}, s32[16]{0:T(128)}, u32[]{:S(2)}) copy-start(s32[16]{0:T(128)} %param.31) | copy-start | bytes 196
  209.2 10.6 %copy-start.23 = (f32[16,64]{1,0:T(8,128)S(1)}, f32[16,64]{1,0:T(8,128)}, u32[]{:S(2)}) copy-start(f32[16,64]{1,0:T(8,128)} %get-tuple-element.40) | copy-start | bytes 12292
  209.2 118.9 %all-to-all-start.1 = ((bf16[128,16,2048]{2,1,0:T(8,128)(2,1)}), bf16[128,16,2048]{2,1,0:T(8,128)(2,1)}, u32[]{:S(2)}, u32[]{:S(2)}) async-start(bf16[128,16,2048]{2,1,0:T(8,128)(2,1)} %bitcast.175), calls=%async_computation.1 | async-start | bytes 16777216 | tf_op jit(solution)/shard_map/all_to_all | solution.py:216
  328.0 5.5 %copy-start.13 = (f32[32,2048]{1,0:T(8,128)S(1)}, f32[32,2048]{1,0:T(8,128)}, u32[]{:S(2)}) copy-start(f32[32,2048]{1,0:T(8,128)} %copy-done.12) | copy-start | bytes 786436
  (23 other events, 73.6 us)

commit v7 on v5

--- a/solution.py
+++ b/solution.py
@@ -97,8 +97,8 @@
 
 def ring_sum(blocks, shifts):
     total = blocks[0].astype(jnp.float32)
-    for step, pairs in enumerate(shifts, start=1):
-        total = total + lax.ppermute(blocks[step], "exp", pairs).astype(jnp.float32)
+    for step in (2, 1, 3):
+        total = total + lax.ppermute(blocks[step], "exp", shifts[step - 1]).astype(jnp.float32)
     return total
 
 

time: 314 us -> 315 us (level)
  transfers between devices with their start and end apart: 13 -> 13, of which waited for: 7 -> 6; matrix products, arithmetic and copies ran while one was open for 4% -> 4% of each run, Pallas kernels for 0% -> 0%
where the time goes in v7:
time: 315 us
  waiting for transfers between devices  123 us (39%)
  blocking collectives  104 us (33%)
  matrix products  40.3 us (13%)
  starting transfers between devices  25 us (8%)
  other arithmetic  11.8 us (4%)
  local copies, waits for them, and re-layouts  8.8 us (3%)
    all_to_all x1, waiting for transfers between devices, per_device(): lax.all_to_all(produced, ('req', 'exp'), split_axis=0, concat_axis=0, til...  104 us
    all_to_all x1, blocking collectives, per_device(): lax.all_to_all(outgoing, ('req', 'exp'), split_axis=0, concat_axis=0, til...  104 us
    ppermute x12, waiting for transfers between devices, ring_sum(): lax.ppermute(blocks[step], 'exp', shifts[step - 1]).astype(jnp.float32)  19 us
    ppermute x12, starting transfers between devices, ring_sum(): lax.ppermute(blocks[step], 'exp', shifts[step - 1]).astype(jnp.float32)  16 us
    all_to_all x1, starting transfers between devices, per_device(): lax.all_to_all(produced, ('req', 'exp'), split_axis=0, concat_axis=0, til...  9.04 us
    dot_general x1, matrix products, expert_rows(): jnp.dot(activation, expert_down, preferred_element_type=jnp.float32)  6.71 us
  transfers between devices with their start and end apart: 13, of which 6 were waited for; matrix products, arithmetic and copies ran while one was open for 4% of the time, Pallas kernels for 0%

profile of v7, /device:TPU:60, one launch (start us, length us, event | category | flops | bytes accessed | tf_op | source)
XLA Modules:
  0.0 314.8 jit_solution(15723979219676603111)
XLA Ops:
  0.7 1.8 fusion.25
  5.2 3.7 %fusion.7 = (f32[15,64]{1,0:T(8,128)S(1)}, f32[15,64,1024]{2,1,0:T(8,128)S(1)}) fusion(pred[15,1024]{1,0:T(8,128)(4,1)S(1)} %iota_compare_fusion.5, bf16[16,64,128]{2,1,0:T(8,128)(2,1)S(1)} %copy-done.11, bf16[15,1024,128]{2,1,0:T(8,128)(2,1)} %param.27), kind=kOutput, calls=%fused_computation.18 | convolution fusion | flops 254606400 | bytes 8145664 | tf_op jit(solution)/shard_map/bthe,blhe->bhtl/dot_general | solution.py:51
  13.3 1.7 fusion.117
  23.5 2.1 collective-permute-start.1
  26.9 3.0 collective-permute-start.6
  30.6 1.9 compare_reduce_fusion
  32.5 7.1 %collective-permute-done = bf16[256,1024]{1,0:T(8,128)(2,1)S(1)} collective-permute-done((bf16[256,1024]{1,0:T(8,128)(2,1)}, bf16[256,1024]{1,0:T(8,128)(2,1)S(1)}, u32[]{:S(2)}, u32[]{:S(2)}) %collective-permute-start) | collective-permute-done | bytes 524320 | tf_op jit(solution)/shard_map/ppermute | solution.py:101
  40.5 8.4 %collective-permute-done.1 = bf16[256,1024]{1,0:T(8,128)(2,1)} collective-permute-done((bf16[256,1024]{1,0:T(8,128)(2,1)}, bf16[256,1024]{1,0:T(8,128)(2,1)}, u32[]{:S(2)}, u32[]{:S(2)}) %collective-permute-start.1) | collective-permute-done | bytes 524320 | tf_op jit(solution)/shard_map/ppermute | solution.py:101
  48.9 1.9 fusion.41
  50.8 3.1 collective-permute-start.3
  53.9 2.0 collective-permute-start.5
  55.9 1.6 fusion.38
  57.5 2.1 collective-permute-start.10
  59.6 3.0 collective-permute-start.9
  63.3 2.0 collective-permute-done.11
  66.5 2.4 convolution_convert_fusion.1
  68.9 103.5 %all_to_all.10 = bf16[128,16,2048]{2,1,0:T(8,128)(2,1)S(1)} all-to-all(bf16[128,16,2048]{2,1,0:T(8,128)(2,1)S(1)} %bitcast.119), channel_id=1, replica_groups=mesh['req'=8,'exp'=16] {'req','exp'}, dimensions={0} | all-to-all | bytes 16777216 | tf_op jit(solution)/shard_map/all_to_all | solution.py:204
  172.5 4.5 %fusion.13 = f32[2048,512]{1,0:T(8,128)S(1)} fusion(bf16[2048,2048]{1,0:T(8,128)(2,1)S(1)} %bitcast.125, bf16[1,2048,512]{2,1,0:T(8,128)(2,1)S(1)} %copy-done.17), kind=kOutput, calls=%fused_computation.23 | convolution fusion | flops 4294967296 | bytes 14680064 | tf_op jit(solution)/shard_map/dot_general | solution.py:92
  177.0 5.2 %multiply_convert_fusion = bf16[2048,512]{1,0:T(8,128)(2,1)S(1)} fusion(f32[2048,512]{1,0:T(8,128)S(1)} %fusion.13, bf16[2048,2048]{1,0:T(8,128)(2,1)S(1)} %bitcast.126, bf16[1,2048,512]{2,1,0:T(8,128)(2,1)S(1)} %copy-done.18), kind=kOutput, calls=%fused_computation.12 | convolution fusion | flops 4301258752 | bytes 16777216 | tf_op jit(solution)/shard_map/dot_general | solution.py:93
  182.2 6.7 %convolution_convert_fusion = bf16[2048,2048]{1,0:T(8,128)(2,1)} fusion(bf16[2048,512]{1,0:T(8,128)(2,1)S(1)} %multiply_convert_fusion, bf16[1,512,2048]{2,1,0:T(8,128)(2,1)S(1)} %copy-done), kind=kOutput, calls=%fused_computation.4 | convolution fusion | flops 4299161600 | bytes 12582912 | tf_op jit(solution)/shard_map/dot_general | solution.py:95
  188.9 9.0 %all-to-all-start.1 = ((bf16[128,16,2048]{2,1,0:T(8,128)(2,1)}), bf16[128,16,2048]{2,1,0:T(8,128)(2,1)}, u32[]{:S(2)}, u32[]{:S(2)}) async-start(bf16[128,16,2048]{2,1,0:T(8,128)(2,1)} %bitcast.124), calls=%async_computation.1 | async-start | bytes 16777216 | tf_op jit(solution)/shard_map/all_to_all | solution.py:208
  200.7 1.4 convolution_convert_fusion.4
  204.1 104.4 %all-to-all-done.1 = bf16[128,16,2048]{2,1,0:T(8,128)(2,1)} async-done(((bf16[128,16,2048]{2,1,0:T(8,128)(2,1)}), bf16[128,16,2048]{2,1,0:T(8,128)(2,1)}, u32[]{:S(2)}, u32[]{:S(2)}) %all-to-all-start.1) | async-done | bytes 8388640 | tf_op jit(solution)/shard_map/all_to_all | solution.py:208
  308.5 5.5 %convolution_reduce_fusion = f32[64,2048]{1,0:T(8,128)S(1)} fusion(bf16[3,64,2048]{2,1,0:T(8,128)(2,1)} %bitcast.129, bf16[2048,2048,1]{1,0,2:T(8,128)(2,1)} %bitcast.35), kind=kOutput, calls=%fused_computation.33 | convolution fusion | flops 1610874880 | bytes 9699328 | tf_op jit(solution)/shard_map/dot_general | solution.py:216
  (120 shorter events, 24.9 us)
Async XLA Ops:
  0.6 181.5 %copy-start = (bf16[1,512,2048]{2,1,0:T(8,128)(2,1)S(1)}, bf16[1,512,2048]{2,1,0:T(8,128)(2,1)}, u32[]{:S(2)}) copy-start(bf16[1,512,2048]{2,1,0:T(8,128)(2,1)} %param.39) | copy-start | bytes 6291460
  0.7 4.5 %copy-start.14 = (s32[15]{0:T(128)S(1)}, s32[15]{0:T(128)}, u32[]{:S(2)}) copy-start(s32[15]{0:T(128)} %param.29) | copy-start | bytes 184
  20.9 6.0 %copy-start.1 = (bf16[1024,1024]{1,0:T(8,128)(2,1)}, bf16[1024,1024]{1,0:T(8,128)(2,1)S(1)}, u32[]{:S(2)}) copy-start(bf16[1024,1024]{1,0:T(8,128)(2,1)S(1)} %convolution_convert_fusion.2) | copy-start | bytes 6291460
  21.0 8.9 %copy-start.9 = (s32[64,8]{0,1:T(8,128)S(1)}, s32[64,8]{0,1:T(8,128)}, u32[]{:S(2)}) copy-start(s32[64,8]{0,1:T(8,128)} %param.35) | copy-start | bytes 6148
  21.7 5.2 %copy-start.2 = (bf16[1024,1024]{1,0:T(8,128)(2,1)}, bf16[1024,1024]{1,0:T(8,128)(2,1)S(1)}, u32[]{:S(2)}) copy-start(bf16[1024,1024]{1,0:T(8,128)(2,1)S(1)} %convolution_convert_fusion.3) | copy-start | bytes 6291460
  23.0 16.5 %collective-permute-start = (bf16[256,1024]{1,0:T(8,128)(2,1)}, bf16[256,1024]{1,0:T(8,128)(2,1)S(1)}, u32[]{:S(2)}, u32[]{:S(2)}) collective-permute-start(bf16[256,1024]{1,0:T(8,128)(2,1)} %get-tuple-element.8), channel_id=1, source_target_pairs={{0,2},{1,3},{2,0},{3,1},{4,6},{5,7},{6,4},{7,5},{8,10},{9,11},{10,... | collective-permute-start | bytes 1572872 | tf_op jit(solution)/shard_map/ppermute | solution.py:101
  23.5 25.3 %collective-permute-start.1 = (bf16[256,1024]{1,0:T(8,128)(2,1)}, bf16[256,1024]{1,0:T(8,128)(2,1)}, u32[]{:S(2)}, u32[]{:S(2)}) collective-permute-start(bf16[256,1024]{1,0:T(8,128)(2,1)} %get-tuple-element.10), channel_id=1, source_target_pairs={{0,1},{1,2},{2,3},{3,0},{4,5},{5,6},{6,7},{7,4},{8,9},{9,10},{10,1... | collective-permute-start | bytes 1572872 | tf_op jit(solution)/shard_map/ppermute | solution.py:101
  25.6 23.3 %collective-permute-start.2 = (bf16[256,1024]{1,0:T(8,128)(2,1)}, bf16[256,1024]{1,0:T(8,128)(2,1)}, u32[]{:S(2)}, u32[]{:S(2)}) collective-permute-start(bf16[256,1024]{1,0:T(8,128)(2,1)} %get-tuple-element.9), channel_id=1, source_target_pairs={{0,3},{1,0},{2,1},{3,2},{4,7},{5,4},{6,5},{7,6},{8,11},{9,8},{10,9... | collective-permute-start | bytes 1572872 | tf_op jit(solution)/shard_map/ppermute | solution.py:101
  26.9 27.0 %collective-permute-start.6 = (bf16[256,1024]{1,0:T(8,128)(2,1)}, bf16[256,1024]{1,0:T(8,128)(2,1)S(1)}, u32[]{:S(2)}, u32[]{:S(2)}) collective-permute-start(bf16[256,1024]{1,0:T(8,128)(2,1)} %get-tuple-element.11), channel_id=1, source_target_pairs={{0,8},{1,9},{2,10},{3,11},{4,12},{5,13},{6,14},{7,15},{8,0},{9,1},... | collective-permute-start | bytes 1572872 | tf_op jit(solution)/shard_map/ppermute | solution.py:101
  29.9 26.0 %collective-permute-start.7 = (bf16[256,1024]{1,0:T(8,128)(2,1)}, bf16[256,1024]{1,0:T(8,128)(2,1)}, u32[]{:S(2)}, u32[]{:S(2)}) collective-permute-start(bf16[256,1024]{1,0:T(8,128)(2,1)} %get-tuple-element.13), channel_id=1, source_target_pairs={{0,4},{1,5},{2,6},{3,7},{4,8},{5,9},{6,10},{7,11},{8,12},{9,13},{1... | collective-permute-start | bytes 1572872 | tf_op jit(solution)/shard_map/ppermute | solution.py:101
  40.4 25.9 %copy-start.3 = (f32[64,2048]{1,0:T(8,128)S(1)}, f32[64,2048]{1,0:T(8,128)}, u32[]{:S(2)}) copy-start(f32[64,2048]{1,0:T(8,128)} %param.32) | copy-start | bytes 1572868
  40.4 15.5 %collective-permute-start.8 = (bf16[256,1024]{1,0:T(8,128)(2,1)}, bf16[256,1024]{1,0:T(8,128)(2,1)S(1)}, u32[]{:S(2)}, u32[]{:S(2)}) collective-permute-start(bf16[256,1024]{1,0:T(8,128)(2,1)} %get-tuple-element.12), channel_id=1, source_target_pairs={{0,12},{1,13},{2,14},{3,15},{4,0},{5,1},{6,2},{7,3},{8,4},{9,5},{1... | collective-permute-start | bytes 1572872 | tf_op jit(solution)/shard_map/ppermute | solution.py:101
  50.8 15.8 %copy-start.10 = (f32[2048]{0:T(1024)S(1)}, f32[2048]{0:T(1024)}, u32[]{:S(2)}) copy-start(f32[2048]{0:T(1024)} %param.34) | copy-start | bytes 24580
  50.8 8.8 %collective-permute-start.3 = (bf16[64,1024]{1,0:T(8,128)(2,1)S(1)}, bf16[64,1024]{1,0:T(8,128)(2,1)S(1)}, u32[]{:S(2)}, u32[]{:S(2)}) collective-permute-start(bf16[64,1024]{1,0:T(8,128)(2,1)S(1)} %get-tuple-element.16), channel_id=1, source_target_pairs={{0,8},{1,9},{2,10},{3,11},{4,12},{5,13},{6,14},{7,15},{8,0},{9,1},... | collective-permute-start | bytes 393224 | tf_op jit(solution)/shard_map/ppermute | solution.py:101
  53.9 8.8 %collective-permute-start.4 = (bf16[64,1024]{1,0:T(8,128)(2,1)S(1)}, bf16[64,1024]{1,0:T(8,128)(2,1)S(1)}, u32[]{:S(2)}, u32[]{:S(2)}) collective-permute-start(bf16[64,1024]{1,0:T(8,128)(2,1)S(1)} %get-tuple-element.18), channel_id=1, source_target_pairs={{0,4},{1,5},{2,6},{3,7},{4,8},{5,9},{6,10},{7,11},{8,12},{9,13},{1... | collective-permute-start | bytes 393224 | tf_op jit(solution)/shard_map/ppermute | solution.py:101
  53.9 8.8 %collective-permute-start.5 = (bf16[64,1024]{1,0:T(8,128)(2,1)S(1)}, bf16[64,1024]{1,0:T(8,128)(2,1)S(1)}, u32[]{:S(2)}, u32[]{:S(2)}) collective-permute-start(bf16[64,1024]{1,0:T(8,128)(2,1)S(1)} %get-tuple-element.17), channel_id=1, source_target_pairs={{0,12},{1,13},{2,14},{3,15},{4,0},{5,1},{6,2},{7,3},{8,4},{9,5},{1... | collective-permute-start | bytes 393224 | tf_op jit(solution)/shard_map/ppermute | solution.py:101
  57.5 5.8 %collective-permute-start.10 = (bf16[64,1024]{1,0:T(8,128)(2,1)S(1)}, bf16[64,1024]{1,0:T(8,128)(2,1)S(1)}, u32[]{:S(2)}, u32[]{:S(2)}) collective-permute-start(bf16[64,1024]{1,0:T(8,128)(2,1)S(1)} %get-tuple-element.21), channel_id=1, source_target_pairs={{0,1},{1,2},{2,3},{3,0},{4,5},{5,6},{6,7},{7,4},{8,9},{9,10},{10,1... | collective-permute-start | bytes 393224 | tf_op jit(solution)/shard_map/ppermute | solution.py:101
  59.6 5.7 %collective-permute-start.11 = (bf16[64,1024]{1,0:T(8,128)(2,1)S(1)}, bf16[64,1024]{1,0:T(8,128)(2,1)S(1)}, u32[]{:S(2)}, u32[]{:S(2)}) collective-permute-start(bf16[64,1024]{1,0:T(8,128)(2,1)S(1)} %get-tuple-element.20), channel_id=1, source_target_pairs={{0,3},{1,0},{2,1},{3,2},{4,7},{5,4},{6,5},{7,6},{8,11},{9,8},{10,9... | collective-permute-start | bytes 393224 | tf_op jit(solution)/shard_map/ppermute | solution.py:101
  59.6 6.6 %collective-permute-start.9 = (bf16[64,1024]{1,0:T(8,128)(2,1)S(1)}, bf16[64,1024]{1,0:T(8,128)(2,1)S(1)}, u32[]{:S(2)}, u32[]{:S(2)}) collective-permute-start(bf16[64,1024]{1,0:T(8,128)(2,1)S(1)} %get-tuple-element.19), channel_id=1, source_target_pairs={{0,2},{1,3},{2,0},{3,1},{4,6},{5,7},{6,4},{7,5},{8,10},{9,11},{10,... | collective-permute-start | bytes 393224 | tf_op jit(solution)/shard_map/ppermute | solution.py:101
  68.9 103.5 %copy-start.17 = (bf16[1,2048,512]{2,1,0:T(8,128)(2,1)S(1)}, bf16[1,2048,512]{2,1,0:T(8,128)(2,1)}, u32[]{:S(2)}) copy-start(bf16[1,2048,512]{2,1,0:T(8,128)(2,1)} %param.37) | copy-start | bytes 6291460
  172.5 4.5 %copy-start.18 = (bf16[1,2048,512]{2,1,0:T(8,128)(2,1)S(1)}, bf16[1,2048,512]{2,1,0:T(8,128)(2,1)}, u32[]{:S(2)}) copy-start(bf16[1,2048,512]{2,1,0:T(8,128)(2,1)} %param.38) | copy-start | bytes 6291460
  188.9 9.1 %copy-start.12 = (f32[64,8]{0,1:T(8,128)S(1)}, f32[64,8]{0,1:T(8,128)}, u32[]{:S(2)}) copy-start(f32[64,8]{0,1:T(8,128)} %param.36) | copy-start | bytes 6148
  188.9 10.5 %copy-start.15 = (s32[16]{0:T(128)S(1)}, s32[16]{0:T(128)}, u32[]{:S(2)}) copy-start(s32[16]{0:T(128)} %param.31) | copy-start | bytes 196
  188.9 119.6 %all-to-all-start.1 = ((bf16[128,16,2048]{2,1,0:T(8,128)(2,1)}), bf16[128,16,2048]{2,1,0:T(8,128)(2,1)}, u32[]{:S(2)}, u32[]{:S(2)}) async-start(bf16[128,16,2048]{2,1,0:T(8,128)(2,1)} %bitcast.124), calls=%async_computation.1 | async-start | bytes 16777216 | tf_op jit(solution)/shard_map/all_to_all | solution.py:208
  (9 other events, 17.5 us)

commit v8 on v5

--- a/solution.py
+++ b/solution.py
@@ -133,6 +133,18 @@
     return jnp.concatenate([first, second], axis=1)
 
 
+def slot_of(routes):
+    tok_rows, top_count = routes.shape
+    flat_routes = routes.reshape(-1)
+    flat_count = flat_routes.shape[0]
+    expert_ids = jnp.arange(EXPERTS, dtype=jnp.int32)
+    onehot = (flat_routes[:, None] == expert_ids[None, :]).astype(jnp.float32)
+    flat_ids = jnp.arange(flat_count, dtype=jnp.int32)
+    earlier = (flat_ids[:, None] > flat_ids[None, :]).astype(jnp.float32)
+    before = jnp.dot(earlier, onehot, precision=lax.Precision.HIGHEST)
+    return jnp.sum(before * onehot, axis=1).astype(jnp.int32).reshape(tok_rows, top_count)
+
+
 def per_device(
     queries,
     new_keys,
@@ -155,6 +167,24 @@
     expert_down,
 ):
     reached = ancestors(parents)
+    slot_index = slot_of(routes)
+    tok_rows, top_count = routes.shape
+    devices = lax.axis_size("req") * lax.axis_size("exp")
+    pieces = max(1, devices // EXPERTS)
+    capacity = 2 * tok_rows * top_count // EXPERTS
+    target = routes * capacity + slot_index
+    columns = jnp.arange(EXPERTS * pieces * capacity, dtype=jnp.int32)
+    column_target = (columns // (pieces * capacity)) * capacity + columns % capacity
+    hits = target[:, :, None] == column_target[None, None, :]
+    placement = jnp.any(hits, axis=1).astype(jnp.bfloat16)
+    weighing = jnp.sum(jnp.where(hits, route_weights[:, :, None], 0.0), axis=1)
+    terms = []
+    for _ in range(3):
+        term = weighing.astype(jnp.bfloat16)
+        terms.append(term)
+        weighing = weighing - term.astype(jnp.float32)
+    terms = jnp.concatenate(terms, axis=0)
+    reached, placement, terms = lax.optimization_barrier((reached, placement, terms))
     head_width = new_keys.shape[2]
     stacked = jnp.concatenate([new_keys, new_values], axis=2)
     compacted = compact_path(reached, accepted, stacked)
@@ -180,23 +210,6 @@
     normed = (
         middle * lax.rsqrt(jnp.mean(middle * middle, axis=1, keepdims=True) + 1e-05) * norm_gain
     ).astype(jnp.bfloat16)
-    tok_rows, top_count = routes.shape
-    devices = lax.axis_size("req") * lax.axis_size("exp")
-    pieces = max(1, devices // EXPERTS)
-    capacity = 2 * tok_rows * top_count // EXPERTS
-    flat_routes = routes.reshape(-1)
-    flat_count = flat_routes.shape[0]
-    expert_ids = jnp.arange(EXPERTS, dtype=jnp.int32)
-    onehot = (flat_routes[:, None] == expert_ids[None, :]).astype(jnp.float32)
-    flat_ids = jnp.arange(flat_count, dtype=jnp.int32)
-    earlier = (flat_ids[:, None] > flat_ids[None, :]).astype(jnp.float32)
-    before = jnp.dot(earlier, onehot, precision=lax.Precision.HIGHEST)
-    slot_index = jnp.sum(before * onehot, axis=1).astype(jnp.int32).reshape(tok_rows, top_count)
-    target = routes * capacity + slot_index
-    columns = jnp.arange(EXPERTS * pieces * capacity, dtype=jnp.int32)
-    column_target = (columns // (pieces * capacity)) * capacity + columns % capacity
-    hits = target[:, :, None] == column_target[None, None, :]
-    placement = jnp.any(hits, axis=1).astype(jnp.bfloat16)
     packed = jnp.einsum("tc,td->cd", placement, normed, preferred_element_type=jnp.float32).astype(
         jnp.bfloat16
     )
@@ -206,13 +219,6 @@
         received.reshape(-1, model_width), expert_gate[0], expert_up[0], expert_down[0]
     ).reshape(devices, capacity, model_width)
     returned = lax.all_to_all(produced, ("req", "exp"), split_axis=0, concat_axis=0, tiled=True)
-    weighing = jnp.sum(jnp.where(hits, route_weights[:, :, None], 0.0), axis=1)
-    terms = []
-    for _ in range(3):
-        term = weighing.astype(jnp.bfloat16)
-        terms.append(term)
-        weighing = weighing - term.astype(jnp.float32)
-    terms = jnp.concatenate(terms, axis=0)
     moe = jnp.dot(terms, returned.reshape(-1, model_width), preferred_element_type=jnp.float32)
     moe = jnp.sum(moe.reshape(3, tok_rows, model_width), axis=0)
     hidden_out = (middle + moe).astype(jnp.bfloat16)

time: 314 us -> 321 us (1.022)
  waiting for transfers between devices: 125 us -> 129 us
  starting transfers between devices: 24 us -> 27.7 us
    ppermute x12, starting transfers between devices: 15 us -> 18.7 us  [ring_sum(): total = total + lax.ppermute(blocks[step], 'exp', pairs).astype(jnp.float32)]
    all_to_all x1, waiting for transfers between devices: 104 us -> 108 us  [per_device(): lax.all_to_all(produced, ('req', 'exp'), split_axis=0, concat_axis=0, til...]
  transfers between devices with their start and end apart: 13 -> 13, of which waited for: 7 -> 7; matrix products, arithmetic and copies ran while one was open for 4% -> 1% of each run, Pallas kernels for 0% -> 0%
where the time goes in v8:
time: 321 us; the launch traced here: 320 us
  waiting for transfers between devices  129 us (40%)
  blocking collectives  102 us (32%)
  matrix products  41.3 us (13%)
  starting transfers between devices  27.7 us (9%)
  other arithmetic  10.8 us (3%)
  local copies, waits for them, and re-layouts  7.58 us (2%)
    all_to_all x1, waiting for transfers between devices, per_device(): lax.all_to_all(produced, ('req', 'exp'), split_axis=0, concat_axis=0, til...  108 us
    all_to_all x1, blocking collectives, per_device(): lax.all_to_all(outgoing, ('req', 'exp'), split_axis=0, concat_axis=0, til...  102 us
    ppermute x12, waiting for transfers between devices, ring_sum(): total = total + lax.ppermute(blocks[step], 'exp', pairs).astype(jnp.float32)  21 us
    ppermute x12, starting transfers between devices, ring_sum(): total = total + lax.ppermute(blocks[step], 'exp', pairs).astype(jnp.float32)  18.7 us
    all_to_all x1, starting transfers between devices, per_device(): lax.all_to_all(produced, ('req', 'exp'), split_axis=0, concat_axis=0, til...  9.05 us
    dot_general x1, matrix products, expert_rows(): jnp.dot(activation, expert_down, preferred_element_type=jnp.float32)  6.73 us
  transfers between devices with their start and end apart: 13, of which 7 were waited for; matrix products, arithmetic and copies ran while one was open for 1% of the time, Pallas kernels for 0%

profile of v8, /device:TPU:60, one launch (start us, length us, event | category | flops | bytes accessed | tf_op | source)
XLA Modules:
  0.0 320.0 jit_solution(15662053711789160815)
XLA Ops:
  4.1 1.9 compare_reduce_fusion
  6.7 1.8 fusion.25
  9.6 1.9 fusion.29
  15.6 1.6 fusion.7
  21.6 1.7 fusion.117
  28.7 1.6 convolution_convert_fusion.3
  30.4 1.6 convolution_convert_fusion.2
  34.3 1.7 collective-permute-start.1
  36.1 2.0 collective-permute-start.6
  38.2 8.9 %collective-permute-done = bf16[256,1024]{1,0:T(8,128)(2,1)S(1)} collective-permute-done((bf16[256,1024]{1,0:T(8,128)(2,1)S(1)}, bf16[256,1024]{1,0:T(8,128)(2,1)S(1)}, u32[]{:S(2)}, u32[]{:S(2)}) %collective-permute-start) | collective-permute-done | bytes 524320 | tf_op jit(solution)/shard_map/ppermute | solution.py:101
  47.1 3.0 collective-permute-start.7
  50.0 7.1 %collective-permute-done.1 = bf16[256,1024]{1,0:T(8,128)(2,1)S(1)} collective-permute-done((bf16[256,1024]{1,0:T(8,128)(2,1)S(1)}, bf16[256,1024]{1,0:T(8,128)(2,1)S(1)}, u32[]{:S(2)}, u32[]{:S(2)}) %collective-permute-start.1) | collective-permute-done | bytes 524320 | tf_op jit(solution)/shard_map/ppermute | solution.py:101
  57.6 2.0 collective-permute-start.3
  59.7 3.0 collective-permute-start.4
  66.4 2.6 collective-permute-start.10
  70.7 2.2 collective-permute-done.10
  73.2 2.4 convolution_convert_fusion.1
  75.6 101.9 %all_to_all.10 = bf16[128,16,2048]{2,1,0:T(8,128)(2,1)S(1)} all-to-all(bf16[128,16,2048]{2,1,0:T(8,128)(2,1)S(1)} %bitcast.119), channel_id=1, replica_groups=mesh['req'=8,'exp'=16] {'req','exp'}, dimensions={0} | all-to-all | bytes 16777216 | tf_op jit(solution)/shard_map/all_to_all | solution.py:217
  177.6 4.5 %fusion.13 = f32[2048,512]{1,0:T(8,128)S(1)} fusion(bf16[2048,2048]{1,0:T(8,128)(2,1)S(1)} %bitcast.125, bf16[1,2048,512]{2,1,0:T(8,128)(2,1)S(1)} %copy-done.15), kind=kOutput, calls=%fused_computation.23 | convolution fusion | flops 4294967296 | bytes 14680064 | tf_op jit(solution)/shard_map/dot_general | solution.py:92
  182.1 5.2 %multiply_convert_fusion = bf16[2048,512]{1,0:T(8,128)(2,1)S(1)} fusion(f32[2048,512]{1,0:T(8,128)S(1)} %fusion.13, bf16[2048,2048]{1,0:T(8,128)(2,1)S(1)} %bitcast.126, bf16[1,2048,512]{2,1,0:T(8,128)(2,1)S(1)} %copy-done.16), kind=kOutput, calls=%fused_computation.12 | convolution fusion | flops 4301258752 | bytes 16777216 | tf_op jit(solution)/shard_map/dot_general | solution.py:93
  187.3 6.7 %convolution_convert_fusion = bf16[2048,2048]{1,0:T(8,128)(2,1)} fusion(bf16[2048,512]{1,0:T(8,128)(2,1)S(1)} %multiply_convert_fusion, bf16[1,512,2048]{2,1,0:T(8,128)(2,1)S(1)} %copy-done), kind=kOutput, calls=%fused_computation.4 | convolution fusion | flops 4299161600 | bytes 12582912 | tf_op jit(solution)/shard_map/dot_general | solution.py:95
  194.0 9.0 %all-to-all-start.1 = ((bf16[128,16,2048]{2,1,0:T(8,128)(2,1)}), bf16[128,16,2048]{2,1,0:T(8,128)(2,1)}, u32[]{:S(2)}, u32[]{:S(2)}) async-start(bf16[128,16,2048]{2,1,0:T(8,128)(2,1)} %bitcast.124), calls=%async_computation.1 | async-start | bytes 16777216 | tf_op jit(solution)/shard_map/all_to_all | solution.py:221
  205.9 107.7 %all-to-all-done.1 = bf16[128,16,2048]{2,1,0:T(8,128)(2,1)} async-done(((bf16[128,16,2048]{2,1,0:T(8,128)(2,1)}), bf16[128,16,2048]{2,1,0:T(8,128)(2,1)}, u32[]{:S(2)}, u32[]{:S(2)}) %all-to-all-start.1) | async-done | bytes 8388640 | tf_op jit(solution)/shard_map/all_to_all | solution.py:221
  313.6 5.5 %convolution_reduce_fusion = f32[64,2048]{1,0:T(8,128)S(1)} fusion(bf16[3,64,2048]{2,1,0:T(8,128)(2,1)} %bitcast.129, bf16[2048,2048,1]{1,0,2:T(8,128)(2,1)} %bitcast.35), kind=kOutput, calls=%fused_computation.33 | convolution fusion | flops 1610874880 | bytes 9699328 | tf_op jit(solution)/shard_map/dot_general | solution.py:222
  (118 shorter events, 30.5 us)
Async XLA Ops:
  0.6 186.7 %copy-start = (bf16[1,512,2048]{2,1,0:T(8,128)(2,1)S(1)}, bf16[1,512,2048]{2,1,0:T(8,128)(2,1)}, u32[]{:S(2)}) copy-start(bf16[1,512,2048]{2,1,0:T(8,128)(2,1)} %param.39) | copy-start | bytes 6291460
  6.0 8.2 %copy-start.8 = (bf16[16,64,128]{2,1,0:T(8,128)(2,1)S(1)}, bf16[16,64,128]{2,1,0:T(8,128)(2,1)}, u32[]{:S(2)}) copy-start(bf16[16,64,128]{2,1,0:T(8,128)(2,1)} %param.21) | copy-start | bytes 786436
  6.0 8.2 %copy-start.10 = (bf16[16,64,128]{2,1,0:T(8,128)(2,1)S(1)}, bf16[16,64,128]{2,1,0:T(8,128)(2,1)}, u32[]{:S(2)}) copy-start(bf16[16,64,128]{2,1,0:T(8,128)(2,1)} %param.22) | copy-start | bytes 786436
  11.5 4.1 %copy-start.9 = (bf16[16,64,128]{2,1,0:T(8,128)(2,1)S(1)}, bf16[16,64,128]{2,1,0:T(8,128)(2,1)}, u32[]{:S(2)}) copy-start(bf16[16,64,128]{2,1,0:T(8,128)(2,1)} %param.21) | copy-start | bytes 786436
  32.2 14.9 %collective-permute-start = (bf16[256,1024]{1,0:T(8,128)(2,1)S(1)}, bf16[256,1024]{1,0:T(8,128)(2,1)S(1)}, u32[]{:S(2)}, u32[]{:S(2)}) collective-permute-start(bf16[256,1024]{1,0:T(8,128)(2,1)S(1)} %get-tuple-element.14), channel_id=1, source_target_pairs={{0,1},{1,2},{2,3},{3,0},{4,5},{5,6},{6,7},{7,4},{8,9},{9,10},{10,1... | collective-permute-start | bytes 1572872 | tf_op jit(solution)/shard_map/ppermute | solution.py:101
  33.4 16.6 %collective-permute-start.2 = (bf16[256,1024]{1,0:T(8,128)(2,1)S(1)}, bf16[256,1024]{1,0:T(8,128)(2,1)S(1)}, u32[]{:S(2)}, u32[]{:S(2)}) collective-permute-start(bf16[256,1024]{1,0:T(8,128)(2,1)S(1)} %get-tuple-element.15), channel_id=1, source_target_pairs={{0,3},{1,0},{2,1},{3,2},{4,7},{5,4},{6,5},{7,6},{8,11},{9,8},{10,9... | collective-permute-start | bytes 1572872 | tf_op jit(solution)/shard_map/ppermute | solution.py:101
  34.3 22.9 %collective-permute-start.1 = (bf16[256,1024]{1,0:T(8,128)(2,1)S(1)}, bf16[256,1024]{1,0:T(8,128)(2,1)S(1)}, u32[]{:S(2)}, u32[]{:S(2)}) collective-permute-start(bf16[256,1024]{1,0:T(8,128)(2,1)S(1)} %get-tuple-element.16), channel_id=1, source_target_pairs={{0,2},{1,3},{2,0},{3,1},{4,6},{5,7},{6,4},{7,5},{8,10},{9,11},{10,... | collective-permute-start | bytes 1572872 | tf_op jit(solution)/shard_map/ppermute | solution.py:101
  36.1 23.6 %collective-permute-start.6 = (bf16[256,1024]{1,0:T(8,128)(2,1)S(1)}, bf16[256,1024]{1,0:T(8,128)(2,1)S(1)}, u32[]{:S(2)}, u32[]{:S(2)}) collective-permute-start(bf16[256,1024]{1,0:T(8,128)(2,1)S(1)} %get-tuple-element.17), channel_id=1, source_target_pairs={{0,4},{1,5},{2,6},{3,7},{4,8},{5,9},{6,10},{7,11},{8,12},{9,13},{1... | collective-permute-start | bytes 1572872 | tf_op jit(solution)/shard_map/ppermute | solution.py:101
  38.1 24.6 %collective-permute-start.8 = (bf16[256,1024]{1,0:T(8,128)(2,1)S(1)}, bf16[256,1024]{1,0:T(8,128)(2,1)S(1)}, u32[]{:S(2)}, u32[]{:S(2)}) collective-permute-start(bf16[256,1024]{1,0:T(8,128)(2,1)S(1)} %get-tuple-element.18), channel_id=1, source_target_pairs={{0,12},{1,13},{2,14},{3,15},{4,0},{5,1},{6,2},{7,3},{8,4},{9,5},{1... | collective-permute-start | bytes 1572872 | tf_op jit(solution)/shard_map/ppermute | solution.py:101
  47.1 25.9 %copy-start.1 = (f32[64,2048]{1,0:T(8,128)S(1)}, f32[64,2048]{1,0:T(8,128)}, u32[]{:S(2)}) copy-start(f32[64,2048]{1,0:T(8,128)} %param.32) | copy-start | bytes 1572868
  47.1 16.9 %collective-permute-start.7 = (bf16[256,1024]{1,0:T(8,128)(2,1)S(1)}, bf16[256,1024]{1,0:T(8,128)(2,1)S(1)}, u32[]{:S(2)}, u32[]{:S(2)}) collective-permute-start(bf16[256,1024]{1,0:T(8,128)(2,1)S(1)} %get-tuple-element.19), channel_id=1, source_target_pairs={{0,8},{1,9},{2,10},{3,11},{4,12},{5,13},{6,14},{7,15},{8,0},{9,1},... | collective-permute-start | bytes 1572872 | tf_op jit(solution)/shard_map/ppermute | solution.py:101
  57.5 15.7 %copy-start.6 = (bf16[64,2048]{1,0:T(8,128)(2,1)S(1)}, bf16[64,2048]{1,0:T(8,128)(2,1)}, u32[]{:S(2)}) copy-start(bf16[64,2048]{1,0:T(8,128)(2,1)} %convert_element_type.216) | copy-start | bytes 786436
  57.5 15.7 %copy-start.7 = (f32[2048]{0:T(1024)S(1)}, f32[2048]{0:T(1024)}, u32[]{:S(2)}) copy-start(f32[2048]{0:T(1024)} %param.34) | copy-start | bytes 24580
  57.6 8.9 %collective-permute-start.3 = (bf16[64,1024]{1,0:T(8,128)(2,1)S(1)}, bf16[64,1024]{1,0:T(8,128)(2,1)S(1)}, u32[]{:S(2)}, u32[]{:S(2)}) collective-permute-start(bf16[64,1024]{1,0:T(8,128)(2,1)S(1)} %get-tuple-element.22), channel_id=1, source_target_pairs={{0,4},{1,5},{2,6},{3,7},{4,8},{5,9},{6,10},{7,11},{8,12},{9,13},{1... | collective-permute-start | bytes 393224 | tf_op jit(solution)/shard_map/ppermute | solution.py:101
  59.6 9.5 %collective-permute-start.5 = (bf16[64,1024]{1,0:T(8,128)(2,1)S(1)}, bf16[64,1024]{1,0:T(8,128)(2,1)S(1)}, u32[]{:S(2)}, u32[]{:S(2)}) collective-permute-start(bf16[64,1024]{1,0:T(8,128)(2,1)S(1)} %get-tuple-element.23), channel_id=1, source_target_pairs={{0,12},{1,13},{2,14},{3,15},{4,0},{5,1},{6,2},{7,3},{8,4},{9,5},{1... | collective-permute-start | bytes 393224 | tf_op jit(solution)/shard_map/ppermute | solution.py:101
  59.7 9.4 %collective-permute-start.4 = (bf16[64,1024]{1,0:T(8,128)(2,1)S(1)}, bf16[64,1024]{1,0:T(8,128)(2,1)S(1)}, u32[]{:S(2)}, u32[]{:S(2)}) collective-permute-start(bf16[64,1024]{1,0:T(8,128)(2,1)S(1)} %get-tuple-element.24), channel_id=1, source_target_pairs={{0,8},{1,9},{2,10},{3,11},{4,12},{5,13},{6,14},{7,15},{8,0},{9,1},... | collective-permute-start | bytes 393224 | tf_op jit(solution)/shard_map/ppermute | solution.py:101
  64.3 5.9 %collective-permute-start.9 = (bf16[64,1024]{1,0:T(8,128)(2,1)S(1)}, bf16[64,1024]{1,0:T(8,128)(2,1)S(1)}, u32[]{:S(2)}, u32[]{:S(2)}) collective-permute-start(bf16[64,1024]{1,0:T(8,128)(2,1)S(1)} %get-tuple-element.25), channel_id=1, source_target_pairs={{0,1},{1,2},{2,3},{3,0},{4,5},{5,6},{6,7},{7,4},{8,9},{9,10},{10,1... | collective-permute-start | bytes 393224 | tf_op jit(solution)/shard_map/ppermute | solution.py:101
  65.7 5.0 %collective-permute-start.11 = (bf16[64,1024]{1,0:T(8,128)(2,1)S(1)}, bf16[64,1024]{1,0:T(8,128)(2,1)S(1)}, u32[]{:S(2)}, u32[]{:S(2)}) collective-permute-start(bf16[64,1024]{1,0:T(8,128)(2,1)S(1)} %get-tuple-element.26), channel_id=1, source_target_pairs={{0,3},{1,0},{2,1},{3,2},{4,7},{5,4},{6,5},{7,6},{8,11},{9,8},{10,9... | collective-permute-start | bytes 393224 | tf_op jit(solution)/shard_map/ppermute | solution.py:101
  66.4 6.5 %collective-permute-start.10 = (bf16[64,1024]{1,0:T(8,128)(2,1)S(1)}, bf16[64,1024]{1,0:T(8,128)(2,1)S(1)}, u32[]{:S(2)}, u32[]{:S(2)}) collective-permute-start(bf16[64,1024]{1,0:T(8,128)(2,1)S(1)} %get-tuple-element.27), channel_id=1, source_target_pairs={{0,2},{1,3},{2,0},{3,1},{4,6},{5,7},{6,4},{7,5},{8,10},{9,11},{10,... | collective-permute-start | bytes 393224 | tf_op jit(solution)/shard_map/ppermute | solution.py:101
  75.6 101.9 %copy-start.15 = (bf16[1,2048,512]{2,1,0:T(8,128)(2,1)S(1)}, bf16[1,2048,512]{2,1,0:T(8,128)(2,1)}, u32[]{:S(2)}) copy-start(bf16[1,2048,512]{2,1,0:T(8,128)(2,1)} %param.37) | copy-start | bytes 6291460
  177.6 4.5 %copy-start.16 = (bf16[1,2048,512]{2,1,0:T(8,128)(2,1)S(1)}, bf16[1,2048,512]{2,1,0:T(8,128)(2,1)}, u32[]{:S(2)}) copy-start(bf16[1,2048,512]{2,1,0:T(8,128)(2,1)} %param.38) | copy-start | bytes 6291460
  194.0 9.3 %copy-start.12 = (s32[16]{0:T(128)S(1)}, s32[16]{0:T(128)}, u32[]{:S(2)}) copy-start(s32[16]{0:T(128)} %param.31) | copy-start | bytes 196
  194.0 119.6 %all-to-all-start.1 = ((bf16[128,16,2048]{2,1,0:T(8,128)(2,1)}), bf16[128,16,2048]{2,1,0:T(8,128)(2,1)}, u32[]{:S(2)}, u32[]{:S(2)}) async-start(bf16[128,16,2048]{2,1,0:T(8,128)(2,1)} %bitcast.124), calls=%async_computation.1 | async-start | bytes 16777216 | tf_op jit(solution)/shard_map/all_to_all | solution.py:221
  313.6 5.5 %copy-start.3 = (f32[64,1024]{1,0:T(8,128)S(1)}, f32[64,1024]{1,0:T(8,128)}, u32[]{:S(2)}) copy-start(f32[64,1024]{1,0:T(8,128)} %copy-done.2) | copy-start | bytes 786436
  (7 other events, 18.5 us)

commit v9 on v5

--- a/solution.py
+++ b/solution.py
@@ -119,12 +119,16 @@
     x_of = (x_pos + near) % side
     x_major = (x_of[:, None] + z_of[None, :] * side).reshape(-1)
     z_major = (z_of[:, None] * side + x_of[None, :]).reshape(-1)
-    first = jnp.take(blocks, x_major, axis=0).reshape(n_exp * rows, -1)
-    first = jnp.dot(first, out_weight[:, :split], preferred_element_type=jnp.float32)
-    first = first.astype(jnp.bfloat16).reshape(side, side * rows, split)
-    second = jnp.take(blocks, z_major, axis=0).reshape(n_exp * rows, -1)
-    second = jnp.dot(second, out_weight[:, split:], preferred_element_type=jnp.float32)
-    second = second.astype(jnp.bfloat16).reshape(side, side * rows, split)
+    def offset_blocks(order, weight):
+        parts = []
+        for step in range(side):
+            picked = jnp.take(blocks, order[step * side:(step + 1) * side], axis=0)
+            part = jnp.dot(picked.reshape(side * rows, -1), weight, preferred_element_type=jnp.float32)
+            parts.append(part.astype(jnp.bfloat16))
+        return parts
+
+    first = offset_blocks(x_major, out_weight[:, :split])
+    second = offset_blocks(z_major, out_weight[:, split:])
     first, second = lax.optimization_barrier((first, second))
     first = ring_sum(first, x_shifts)
     second = ring_sum(second, z_shifts)

time: 314 us -> 337 us (1.073)
  matrix products: 40.3 us -> 54.7 us
  local copies, waits for them, and re-layouts: 8.8 us -> 13.9 us
    dot_general x2 -> x8, matrix products: 1.39 us -> 14.5 us  [offset_blocks(): jnp.dot(picked.reshape(side * rows, -1), weight, preferred_element_type=j...]
    gather x2 -> x8, local copies, waits for them, and re-layouts: 1.19 us -> 10.2 us  [offset_blocks(): picked = jnp.take(blocks, order[step * side:(step + 1) * side], axis=0)]
where the time goes in v9:
time: 337 us; the launch traced here: 336 us
  waiting for transfers between devices  128 us (38%)
  blocking collectives  102 us (30%)
  matrix products  54.7 us (16%)
  starting transfers between devices  23.9 us (7%)
  local copies, waits for them, and re-layouts  13.9 us (4%)
  other arithmetic  12.3 us (4%)
    all_to_all x1, waiting for transfers between devices, per_device(): lax.all_to_all(produced, ('req', 'exp'), split_axis=0, concat_axis=0, til...  104 us
    all_to_all x1, blocking collectives, per_device(): lax.all_to_all(outgoing, ('req', 'exp'), split_axis=0, concat_axis=0, til...  102 us
    ppermute x12, waiting for transfers between devices, ring_sum(): total = total + lax.ppermute(blocks[step], 'exp', pairs).astype(jnp.float32)  23.2 us
    ppermute x12, starting transfers between devices, ring_sum(): total = total + lax.ppermute(blocks[step], 'exp', pairs).astype(jnp.float32)  14.9 us
    dot_general x8, matrix products, offset_blocks(): jnp.dot(picked.reshape(side * rows, -1), weight, preferred_element_type=j...  14.5 us
    gather x8, local copies, waits for them, and re-layouts, offset_blocks(): picked = jnp.take(blocks, order[step * side:(step + 1) * side], axis=0)  10.2 us
    all_to_all x1, starting transfers between devices, per_device(): lax.all_to_all(produced, ('req', 'exp'), split_axis=0, concat_axis=0, til...  9.03 us
  transfers between devices with their start and end apart: 13, of which 7 were waited for; matrix products, arithmetic and copies ran while one was open for 4% of the time, Pallas kernels for 0%

profile of v9, /device:TPU:60, one launch (start us, length us, event | category | flops | bytes accessed | tf_op | source)
XLA Modules:
  0.0 335.8 jit_solution(3355889583572434930)
XLA Ops:
  5.9 3.7 %fusion.7 = (f32[15,64]{1,0:T(8,128)S(1)}, f32[15,64,1024]{2,1,0:T(8,128)S(1)}) fusion(pred[15,1024]{1,0:T(8,128)(4,1)S(1)} %iota_compare_fusion.5, bf16[16,64,128]{2,1,0:T(8,128)(2,1)S(1)} %copy-done.9, bf16[15,1024,128]{2,1,0:T(8,128)(2,1)} %param.27), kind=kOutput, calls=%fused_computation.24 | convolution fusion | flops 254606400 | bytes 8145664 | tf_op jit(solution)/shard_map/bthe,blhe->bhtl/dot_general | solution.py:51
  21.9 2.0 convolution_convert_fusion.4
  25.5 2.0 convolution_convert_fusion.5
  32.0 2.0 convolution_convert_fusion.7
  35.7 2.0 convolution_convert_fusion.8
  39.3 2.0 convolution_convert_fusion.9
  42.9 2.0 convolution_convert_fusion.10
  48.1 1.9 collective-permute-start.6
  51.8 1.9 compare_reduce_fusion
  53.8 6.4 %collective-permute-done = bf16[256,1024]{1,0:T(8,128)(2,1)} collective-permute-done((bf16[256,1024]{1,0:T(8,128)(2,1)}, bf16[256,1024]{1,0:T(8,128)(2,1)}, u32[]{:S(2)}, u32[]{:S(2)}) %collective-permute-start) | collective-permute-done | bytes 524320 | tf_op jit(solution)/shard_map/ppermute | solution.py:101
  60.2 10.0 %collective-permute-done.1 = bf16[256,1024]{1,0:T(8,128)(2,1)} collective-permute-done((bf16[256,1024]{1,0:T(8,128)(2,1)}, bf16[256,1024]{1,0:T(8,128)(2,1)}, u32[]{:S(2)}, u32[]{:S(2)}) %collective-permute-start.1) | collective-permute-done | bytes 524320 | tf_op jit(solution)/shard_map/ppermute | solution.py:101
  70.2 1.8 collective-permute-done.2
  72.0 1.9 add_convert_fusion.1
  74.0 2.0 collective-permute-start.3
  77.1 2.5 collective-permute-start.5
  84.3 3.6 %collective-permute-done.10 = bf16[64,1024]{1,0:T(8,128)(2,1)S(1)} collective-permute-done((bf16[64,1024]{1,0:T(8,128)(2,1)S(1)}, bf16[64,1024]{1,0:T(8,128)(2,1)S(1)}, u32[]{:S(2)}, u32[]{:S(2)}) %collective-permute-start.10) | collective-permute-done | bytes 131104 | tf_op jit(solution)/shard_map/ppermute | solution.py:101
  89.5 2.4 convolution_convert_fusion.1
  91.9 101.5 %all_to_all.10 = bf16[128,16,2048]{2,1,0:T(8,128)(2,1)S(1)} all-to-all(bf16[128,16,2048]{2,1,0:T(8,128)(2,1)S(1)} %bitcast.135), channel_id=1, replica_groups=mesh['req'=8,'exp'=16] {'req','exp'}, dimensions={0} | all-to-all | bytes 16777216 | tf_op jit(solution)/shard_map/all_to_all | solution.py:208
  193.5 4.5 %fusion.13 = f32[2048,512]{1,0:T(8,128)S(1)} fusion(bf16[2048,2048]{1,0:T(8,128)(2,1)S(1)} %bitcast.137, bf16[1,2048,512]{2,1,0:T(8,128)(2,1)S(1)} %copy-done.15), kind=kOutput, calls=%fused_computation.29 | convolution fusion | flops 4294967296 | bytes 14680064 | tf_op jit(solution)/shard_map/dot_general | solution.py:92
  198.0 5.2 %multiply_convert_fusion = bf16[2048,512]{1,0:T(8,128)(2,1)S(1)} fusion(f32[2048,512]{1,0:T(8,128)S(1)} %fusion.13, bf16[2048,2048]{1,0:T(8,128)(2,1)S(1)} %bitcast.138, bf16[1,2048,512]{2,1,0:T(8,128)(2,1)S(1)} %copy-done.16), kind=kOutput, calls=%fused_computation.18 | convolution fusion | flops 4301258752 | bytes 16777216 | tf_op jit(solution)/shard_map/dot_general | solution.py:93
  203.2 6.7 %convolution_convert_fusion = bf16[2048,2048]{1,0:T(8,128)(2,1)} fusion(bf16[2048,512]{1,0:T(8,128)(2,1)S(1)} %multiply_convert_fusion, bf16[1,512,2048]{2,1,0:T(8,128)(2,1)S(1)} %copy-done), kind=kOutput, calls=%fused_computation.10 | convolution fusion | flops 4299161600 | bytes 12582912 | tf_op jit(solution)/shard_map/dot_general | solution.py:95
  210.0 9.0 %all-to-all-start.1 = ((bf16[128,16,2048]{2,1,0:T(8,128)(2,1)}), bf16[128,16,2048]{2,1,0:T(8,128)(2,1)}, u32[]{:S(2)}, u32[]{:S(2)}) async-start(bf16[128,16,2048]{2,1,0:T(8,128)(2,1)} %bitcast.136), calls=%async_computation.1 | async-start | bytes 16777216 | tf_op jit(solution)/shard_map/all_to_all | solution.py:212
  225.0 104.5 %all-to-all-done.1 = bf16[128,16,2048]{2,1,0:T(8,128)(2,1)} async-done(((bf16[128,16,2048]{2,1,0:T(8,128)(2,1)}), bf16[128,16,2048]{2,1,0:T(8,128)(2,1)}, u32[]{:S(2)}, u32[]{:S(2)}) %all-to-all-start.1) | async-done | bytes 8388640 | tf_op jit(solution)/shard_map/all_to_all | solution.py:212
  329.5 5.5 %convolution_reduce_fusion = f32[64,2048]{1,0:T(8,128)S(1)} fusion(bf16[3,64,2048]{2,1,0:T(8,128)(2,1)} %bitcast.139, bf16[2048,2048,1]{1,0,2:T(8,128)(2,1)} %bitcast.39), kind=kOutput, calls=%fused_computation.37 | convolution fusion | flops 1610874880 | bytes 9699328 | tf_op jit(solution)/shard_map/dot_general | solution.py:220
  (134 shorter events, 46.6 us)
Async XLA Ops:
  0.6 202.6 %copy-start = (bf16[1,512,2048]{2,1,0:T(8,128)(2,1)S(1)}, bf16[1,512,2048]{2,1,0:T(8,128)(2,1)}, u32[]{:S(2)}) copy-start(bf16[1,512,2048]{2,1,0:T(8,128)(2,1)} %param.39) | copy-start | bytes 6291460
  0.6 4.8 %copy-start.9 = (bf16[16,64,128]{2,1,0:T(8,128)(2,1)S(1)}, bf16[16,64,128]{2,1,0:T(8,128)(2,1)}, u32[]{:S(2)}) copy-start(bf16[16,64,128]{2,1,0:T(8,128)(2,1)} %param.21) | copy-start | bytes 786436
  0.7 4.8 %copy-start.11 = (bf16[16,64,128]{2,1,0:T(8,128)(2,1)S(1)}, bf16[16,64,128]{2,1,0:T(8,128)(2,1)}, u32[]{:S(2)}) copy-start(bf16[16,64,128]{2,1,0:T(8,128)(2,1)} %param.22) | copy-start | bytes 786436
  0.7 5.2 %copy-start.12 = (s32[15]{0:T(128)S(1)}, s32[15]{0:T(128)}, u32[]{:S(2)}) copy-start(s32[15]{0:T(128)} %param.29) | copy-start | bytes 184
  20.8 30.4 %copy-start.7 = (s32[64,8]{0,1:T(8,128)S(1)}, s32[64,8]{0,1:T(8,128)}, u32[]{:S(2)}) copy-start(s32[64,8]{0,1:T(8,128)} %param.35) | copy-start | bytes 6148
  45.0 15.1 %collective-permute-start = (bf16[256,1024]{1,0:T(8,128)(2,1)}, bf16[256,1024]{1,0:T(8,128)(2,1)}, u32[]{:S(2)}, u32[]{:S(2)}) collective-permute-start(bf16[256,1024]{1,0:T(8,128)(2,1)} %convolution_convert_fusion.9), channel_id=1, source_target_pairs={{0,1},{1,2},{2,3},{3,0},{4,5},{5,6},{6,7},{7,4},{8,9},{9,10},{10,1... | collective-permute-start | bytes 1572872 | tf_op jit(solution)/shard_map/ppermute | solution.py:101
  46.2 24.0 %collective-permute-start.1 = (bf16[256,1024]{1,0:T(8,128)(2,1)}, bf16[256,1024]{1,0:T(8,128)(2,1)}, u32[]{:S(2)}, u32[]{:S(2)}) collective-permute-start(bf16[256,1024]{1,0:T(8,128)(2,1)} %convolution_convert_fusion.8), channel_id=1, source_target_pairs={{0,2},{1,3},{2,0},{3,1},{4,6},{5,7},{6,4},{7,5},{8,10},{9,11},{10,... | collective-permute-start | bytes 1572872 | tf_op jit(solution)/shard_map/ppermute | solution.py:101
  47.0 25.1 %collective-permute-start.2 = (bf16[256,1024]{1,0:T(8,128)(2,1)}, bf16[256,1024]{1,0:T(8,128)(2,1)}, u32[]{:S(2)}, u32[]{:S(2)}) collective-permute-start(bf16[256,1024]{1,0:T(8,128)(2,1)} %convolution_convert_fusion.7), channel_id=1, source_target_pairs={{0,3},{1,0},{2,1},{3,2},{4,7},{5,4},{6,5},{7,6},{8,11},{9,8},{10,9... | collective-permute-start | bytes 1572872 | tf_op jit(solution)/shard_map/ppermute | solution.py:101
  48.1 29.0 %collective-permute-start.6 = (bf16[256,1024]{1,0:T(8,128)(2,1)}, bf16[256,1024]{1,0:T(8,128)(2,1)}, u32[]{:S(2)}, u32[]{:S(2)}) collective-permute-start(bf16[256,1024]{1,0:T(8,128)(2,1)} %convolution_convert_fusion.5), channel_id=1, source_target_pairs={{0,4},{1,5},{2,6},{3,7},{4,8},{5,9},{6,10},{7,11},{8,12},{9,13},{1... | collective-permute-start | bytes 1572872 | tf_op jit(solution)/shard_map/ppermute | solution.py:101
  50.0 29.6 %collective-permute-start.7 = (bf16[256,1024]{1,0:T(8,128)(2,1)}, bf16[256,1024]{1,0:T(8,128)(2,1)}, u32[]{:S(2)}, u32[]{:S(2)}) collective-permute-start(bf16[256,1024]{1,0:T(8,128)(2,1)} %convolution_convert_fusion.4), channel_id=1, source_target_pairs={{0,8},{1,9},{2,10},{3,11},{4,12},{5,13},{6,14},{7,15},{8,0},{9,1},... | collective-permute-start | bytes 1572872 | tf_op jit(solution)/shard_map/ppermute | solution.py:101
  53.7 35.6 %copy-start.2 = (f32[64,2048]{1,0:T(8,128)S(1)}, f32[64,2048]{1,0:T(8,128)}, u32[]{:S(2)}) copy-start(f32[64,2048]{1,0:T(8,128)} %param.32) | copy-start | bytes 1572868
  53.7 35.8 %copy-start.8 = (f32[2048]{0:T(1024)S(1)}, f32[2048]{0:T(1024)}, u32[]{:S(2)}) copy-start(f32[2048]{0:T(1024)} %param.34) | copy-start | bytes 24580
  60.1 19.5 %collective-permute-start.8 = (bf16[256,1024]{1,0:T(8,128)(2,1)}, bf16[256,1024]{1,0:T(8,128)(2,1)S(1)}, u32[]{:S(2)}, u32[]{:S(2)}) collective-permute-start(bf16[256,1024]{1,0:T(8,128)(2,1)} %convolution_convert_fusion.3), channel_id=1, source_target_pairs={{0,12},{1,13},{2,14},{3,15},{4,0},{5,1},{6,2},{7,3},{8,4},{9,5},{1... | collective-permute-start | bytes 1572872 | tf_op jit(solution)/shard_map/ppermute | solution.py:101
  74.0 9.9 %collective-permute-start.3 = (bf16[64,1024]{1,0:T(8,128)(2,1)S(1)}, bf16[64,1024]{1,0:T(8,128)(2,1)S(1)}, u32[]{:S(2)}, u32[]{:S(2)}) collective-permute-start(bf16[64,1024]{1,0:T(8,128)(2,1)S(1)} %get-tuple-element.38), channel_id=1, source_target_pairs={{0,4},{1,5},{2,6},{3,7},{4,8},{5,9},{6,10},{7,11},{8,12},{9,13},{1... | collective-permute-start | bytes 393224 | tf_op jit(solution)/shard_map/ppermute | solution.py:101
  75.9 8.3 %collective-permute-start.4 = (bf16[64,1024]{1,0:T(8,128)(2,1)S(1)}, bf16[64,1024]{1,0:T(8,128)(2,1)S(1)}, u32[]{:S(2)}, u32[]{:S(2)}) collective-permute-start(bf16[64,1024]{1,0:T(8,128)(2,1)S(1)} %get-tuple-element.40), channel_id=1, source_target_pairs={{0,8},{1,9},{2,10},{3,11},{4,12},{5,13},{6,14},{7,15},{8,0},{9,1},... | collective-permute-start | bytes 393224 | tf_op jit(solution)/shard_map/ppermute | solution.py:101
  77.1 7.1 %collective-permute-start.5 = (bf16[64,1024]{1,0:T(8,128)(2,1)S(1)}, bf16[64,1024]{1,0:T(8,128)(2,1)S(1)}, u32[]{:S(2)}, u32[]{:S(2)}) collective-permute-start(bf16[64,1024]{1,0:T(8,128)(2,1)S(1)} %get-tuple-element.39), channel_id=1, source_target_pairs={{0,12},{1,13},{2,14},{3,15},{4,0},{5,1},{6,2},{7,3},{8,4},{9,5},{1... | collective-permute-start | bytes 393224 | tf_op jit(solution)/shard_map/ppermute | solution.py:101
  81.2 6.7 %collective-permute-start.10 = (bf16[64,1024]{1,0:T(8,128)(2,1)S(1)}, bf16[64,1024]{1,0:T(8,128)(2,1)S(1)}, u32[]{:S(2)}, u32[]{:S(2)}) collective-permute-start(bf16[64,1024]{1,0:T(8,128)(2,1)S(1)} %get-tuple-element.43), channel_id=1, source_target_pairs={{0,2},{1,3},{2,0},{3,1},{4,6},{5,7},{6,4},{7,5},{8,10},{9,11},{10,... | collective-permute-start | bytes 393224 | tf_op jit(solution)/shard_map/ppermute | solution.py:101
  82.2 6.6 %collective-permute-start.11 = (bf16[64,1024]{1,0:T(8,128)(2,1)S(1)}, bf16[64,1024]{1,0:T(8,128)(2,1)S(1)}, u32[]{:S(2)}, u32[]{:S(2)}) collective-permute-start(bf16[64,1024]{1,0:T(8,128)(2,1)S(1)} %get-tuple-element.42), channel_id=1, source_target_pairs={{0,3},{1,0},{2,1},{3,2},{4,7},{5,4},{6,5},{7,6},{8,11},{9,8},{10,9... | collective-permute-start | bytes 393224 | tf_op jit(solution)/shard_map/ppermute | solution.py:101
  83.8 5.4 %collective-permute-start.9 = (bf16[64,1024]{1,0:T(8,128)(2,1)S(1)}, bf16[64,1024]{1,0:T(8,128)(2,1)S(1)}, u32[]{:S(2)}, u32[]{:S(2)}) collective-permute-start(bf16[64,1024]{1,0:T(8,128)(2,1)S(1)} %get-tuple-element.41), channel_id=1, source_target_pairs={{0,1},{1,2},{2,3},{3,0},{4,5},{5,6},{6,7},{7,4},{8,9},{9,10},{10,1... | collective-permute-start | bytes 393224 | tf_op jit(solution)/shard_map/ppermute | solution.py:101
  91.9 101.5 %copy-start.15 = (bf16[1,2048,512]{2,1,0:T(8,128)(2,1)S(1)}, bf16[1,2048,512]{2,1,0:T(8,128)(2,1)}, u32[]{:S(2)}) copy-start(bf16[1,2048,512]{2,1,0:T(8,128)(2,1)} %param.37) | copy-start | bytes 6291460
  193.5 4.5 %copy-start.16 = (bf16[1,2048,512]{2,1,0:T(8,128)(2,1)S(1)}, bf16[1,2048,512]{2,1,0:T(8,128)(2,1)}, u32[]{:S(2)}) copy-start(bf16[1,2048,512]{2,1,0:T(8,128)(2,1)} %param.38) | copy-start | bytes 6291460
  209.9 9.0 %copy-start.10 = (f32[64,8]{0,1:T(8,128)S(1)}, f32[64,8]{0,1:T(8,128)}, u32[]{:S(2)}) copy-start(f32[64,8]{0,1:T(8,128)} %param.36) | copy-start | bytes 6148
  209.9 10.5 %copy-start.13 = (s32[16]{0:T(128)S(1)}, s32[16]{0:T(128)}, u32[]{:S(2)}) copy-start(s32[16]{0:T(128)} %param.31) | copy-start | bytes 196
  210.0 119.6 %all-to-all-start.1 = ((bf16[128,16,2048]{2,1,0:T(8,128)(2,1)}), bf16[128,16,2048]{2,1,0:T(8,128)(2,1)}, u32[]{:S(2)}, u32[]{:S(2)}) async-start(bf16[128,16,2048]{2,1,0:T(8,128)(2,1)} %bitcast.136), calls=%async_computation.1 | async-start | bytes 16777216 | tf_op jit(solution)/shard_map/all_to_all | solution.py:212
  (7 other events, 16.6 us)

commit v10 on v5

--- a/solution.py
+++ b/solution.py
@@ -89,8 +89,10 @@
 
 
 def expert_rows(rows, expert_gate, expert_up, expert_down):
-    gate_part = jnp.dot(rows, expert_gate, preferred_element_type=jnp.float32)
-    up_part = jnp.dot(rows, expert_up, preferred_element_type=jnp.float32)
+    both = jnp.dot(
+        rows, jnp.concatenate([expert_gate, expert_up], axis=1), preferred_element_type=jnp.float32
+    )
+    gate_part, up_part = jnp.split(both, 2, axis=1)
     activation = (jax.nn.silu(gate_part) * up_part).astype(jnp.bfloat16)
     return jnp.dot(activation, expert_down, preferred_element_type=jnp.float32).astype(jnp.bfloat16)
 

time: 314 us -> 321 us (1.022)
  matrix products: 40.3 us -> 47.8 us
    dot_general x1, matrix products: 6.71 us -> 10.5 us  [expert_rows(): jnp.dot(activation, expert_down, preferred_element_type=jnp.float32)]
    dot_general x2 -> x1, matrix products: 9.7 us -> 11.5 us  [expert_rows(): jnp.dot(rows, jnp.concatenate([expert_gate, expert_up], axis=1), preferre...]
where the time goes in v10:
time: 321 us
  waiting for transfers between devices  125 us (39%)
  blocking collectives  102 us (32%)
  matrix products  47.8 us (15%)
  starting transfers between devices  24 us (7%)
  other arithmetic  11.8 us (4%)
  local copies, waits for them, and re-layouts  8.38 us (3%)
    all_to_all x1, waiting for transfers between devices, per_device(): lax.all_to_all(produced, ('req', 'exp'), split_axis=0, concat_axis=0, til...  104 us
    all_to_all x1, blocking collectives, per_device(): lax.all_to_all(outgoing, ('req', 'exp'), split_axis=0, concat_axis=0, til...  102 us
    ppermute x12, waiting for transfers between devices, ring_sum(): total = total + lax.ppermute(blocks[step], 'exp', pairs).astype(jnp.float32)  21.1 us
    ppermute x12, starting transfers between devices, ring_sum(): total = total + lax.ppermute(blocks[step], 'exp', pairs).astype(jnp.float32)  15 us
    dot_general x1, matrix products, expert_rows(): jnp.dot(rows, jnp.concatenate([expert_gate, expert_up], axis=1), preferre...  11.5 us
    dot_general x1, matrix products, expert_rows(): jnp.dot(activation, expert_down, preferred_element_type=jnp.float32)  10.5 us
    all_to_all x1, starting transfers between devices, per_device(): lax.all_to_all(produced, ('req', 'exp'), split_axis=0, concat_axis=0, til...  9.03 us
  transfers between devices with their start and end apart: 13, of which 7 were waited for; matrix products, arithmetic and copies ran while one was open for 4% of the time, Pallas kernels for 0%

profile of v10, /device:TPU:60, one launch (start us, length us, event | category | flops | bytes accessed | tf_op | source)
XLA Modules:
  0.0 320.9 jit_solution(15160982772355242529)
XLA Ops:
  0.7 1.8 fusion.29
  3.8 1.6 fusion.122
  6.8 3.7 %fusion.12 = (f32[15,64]{1,0:T(8,128)S(1)}, f32[15,64,1024]{2,1,0:T(8,128)S(1)}) fusion(pred[15,1024]{1,0:T(8,128)(4,1)S(1)} %iota_compare_fusion.5, bf16[16,64,128]{2,1,0:T(8,128)(2,1)S(1)} %copy-done.11, bf16[15,1024,128]{2,1,0:T(8,128)(2,1)} %param.27), kind=kOutput, calls=%fused_computation.23 | convolution fusion | flops 254606400 | bytes 8145664 | tf_op jit(solution)/shard_map/bthe,blhe->bhtl/dot_general | solution.py:51
  14.8 1.7 fusion.123
  28.9 1.9 collective-permute-start.6
  32.7 1.9 compare_reduce_fusion
  34.6 5.0 %collective-permute-done = bf16[256,1024]{1,0:T(8,128)(2,1)S(1)} collective-permute-done((bf16[256,1024]{1,0:T(8,128)(2,1)}, bf16[256,1024]{1,0:T(8,128)(2,1)S(1)}, u32[]{:S(2)}, u32[]{:S(2)}) %collective-permute-start) | collective-permute-done | bytes 524320 | tf_op jit(solution)/shard_map/ppermute | solution.py:103
  40.6 9.2 %collective-permute-done.1 = bf16[256,1024]{1,0:T(8,128)(2,1)} collective-permute-done((bf16[256,1024]{1,0:T(8,128)(2,1)}, bf16[256,1024]{1,0:T(8,128)(2,1)}, u32[]{:S(2)}, u32[]{:S(2)}) %collective-permute-start.1) | collective-permute-done | bytes 524320 | tf_op jit(solution)/shard_map/ppermute | solution.py:103
  49.8 1.8 collective-permute-done.2
  51.6 1.9 fusion.45
  53.5 2.0 collective-permute-start.3
  56.7 2.5 collective-permute-start.5
  59.2 1.6 fusion.42
  61.8 1.7 collective-permute-start.11
  63.9 3.6 %collective-permute-done.10 = bf16[64,1024]{1,0:T(8,128)(2,1)S(1)} collective-permute-done((bf16[64,1024]{1,0:T(8,128)(2,1)S(1)}, bf16[64,1024]{1,0:T(8,128)(2,1)S(1)}, u32[]{:S(2)}, u32[]{:S(2)}) %collective-permute-start.10) | collective-permute-done | bytes 131104 | tf_op jit(solution)/shard_map/ppermute | solution.py:103
  69.1 2.4 convolution_convert_fusion.1
  71.5 101.5 %all_to_all.10 = bf16[128,16,2048]{2,1,0:T(8,128)(2,1)S(1)} all-to-all(bf16[128,16,2048]{2,1,0:T(8,128)(2,1)S(1)} %bitcast.113), channel_id=1, replica_groups=mesh['req'=8,'exp'=16] {'req','exp'}, dimensions={0} | all-to-all | bytes 16777216 | tf_op jit(solution)/shard_map/all_to_all | solution.py:206
  173.1 11.5 %fusion.3 = f32[2048,1024]{1,0:T(8,128)} fusion(bf16[2048,2048]{1,0:T(8,128)(2,1)S(1)} %bitcast.119, bf16[2048,512]{1,0:T(8,128)(2,1)S(1)} %bitcast.124, bf16[2048,512]{1,0:T(8,128)(2,1)S(1)} %bitcast.125), kind=kOutput, calls=%fused_computation.11 | convolution fusion | flops 8598323200 | bytes 20971520 | tf_op jit(solution)/shard_map/dot_general | solution.py:92
  184.6 10.5 %convolution_convert_fusion = bf16[2048,2048]{1,0:T(8,128)(2,1)} fusion(f32[2048,1024]{1,0:T(8,128)} %fusion.3, bf16[1,512,2048]{2,1,0:T(8,128)(2,1)S(1)} %copy-done), kind=kOutput, calls=%fused_computation.4 | convolution fusion | flops 4305453056 | bytes 18874368 | tf_op jit(solution)/shard_map/dot_general | solution.py:97
  195.1 9.0 %all-to-all-start.1 = ((bf16[128,16,2048]{2,1,0:T(8,128)(2,1)}), bf16[128,16,2048]{2,1,0:T(8,128)(2,1)}, u32[]{:S(2)}, u32[]{:S(2)}) async-start(bf16[128,16,2048]{2,1,0:T(8,128)(2,1)} %bitcast.118), calls=%async_computation.1 | async-start | bytes 16777216 | tf_op jit(solution)/shard_map/all_to_all | solution.py:210
  204.2 1.3 fusion.1
  206.8 1.4 convolution_convert_fusion.4
  210.2 104.4 %all-to-all-done.1 = bf16[128,16,2048]{2,1,0:T(8,128)(2,1)} async-done(((bf16[128,16,2048]{2,1,0:T(8,128)(2,1)}), bf16[128,16,2048]{2,1,0:T(8,128)(2,1)}, u32[]{:S(2)}, u32[]{:S(2)}) %all-to-all-start.1) | async-done | bytes 8388640 | tf_op jit(solution)/shard_map/all_to_all | solution.py:210
  314.6 5.5 %convolution_reduce_fusion = f32[64,2048]{1,0:T(8,128)S(1)} fusion(bf16[3,64,2048]{2,1,0:T(8,128)(2,1)} %bitcast.122, bf16[2048,2048,1]{1,0,2:T(8,128)(2,1)} %bitcast.35), kind=kOutput, calls=%fused_computation.36 | convolution fusion | flops 1610874880 | bytes 9699328 | tf_op jit(solution)/shard_map/dot_general | solution.py:218
  (117 shorter events, 29.5 us)
Async XLA Ops:
  0.6 183.9 %copy-start = (bf16[1,512,2048]{2,1,0:T(8,128)(2,1)S(1)}, bf16[1,512,2048]{2,1,0:T(8,128)(2,1)}, u32[]{:S(2)}) copy-start(bf16[1,512,2048]{2,1,0:T(8,128)(2,1)} %param.39) | copy-start | bytes 6291460
  0.7 6.0 %copy-start.13 = (s32[15]{0:T(128)S(1)}, s32[15]{0:T(128)}, u32[]{:S(2)}) copy-start(s32[15]{0:T(128)} %param.29) | copy-start | bytes 184
  22.4 6.5 %copy-start.1 = (bf16[1024,1024]{1,0:T(8,128)(2,1)}, bf16[1024,1024]{1,0:T(8,128)(2,1)S(1)}, u32[]{:S(2)}) copy-start(bf16[1024,1024]{1,0:T(8,128)(2,1)S(1)} %convolution_convert_fusion.2) | copy-start | bytes 6291460
  22.5 9.4 %copy-start.9 = (s32[64,8]{0,1:T(8,128)S(1)}, s32[64,8]{0,1:T(8,128)}, u32[]{:S(2)}) copy-start(s32[64,8]{0,1:T(8,128)} %param.35) | copy-start | bytes 6148
  23.2 5.7 %copy-start.2 = (bf16[1024,1024]{1,0:T(8,128)(2,1)}, bf16[1024,1024]{1,0:T(8,128)(2,1)S(1)}, u32[]{:S(2)}) copy-start(bf16[1024,1024]{1,0:T(8,128)(2,1)S(1)} %convolution_convert_fusion.3) | copy-start | bytes 6291460
  24.6 15.0 %collective-permute-start = (bf16[256,1024]{1,0:T(8,128)(2,1)}, bf16[256,1024]{1,0:T(8,128)(2,1)S(1)}, u32[]{:S(2)}, u32[]{:S(2)}) collective-permute-start(bf16[256,1024]{1,0:T(8,128)(2,1)} %get-tuple-element.8), channel_id=1, source_target_pairs={{0,1},{1,2},{2,3},{3,0},{4,5},{5,6},{6,7},{7,4},{8,9},{9,10},{10,1... | collective-permute-start | bytes 1572872 | tf_op jit(solution)/shard_map/ppermute | solution.py:103
  25.8 24.0 %collective-permute-start.1 = (bf16[256,1024]{1,0:T(8,128)(2,1)}, bf16[256,1024]{1,0:T(8,128)(2,1)}, u32[]{:S(2)}, u32[]{:S(2)}) collective-permute-start(bf16[256,1024]{1,0:T(8,128)(2,1)} %get-tuple-element.10), channel_id=1, source_target_pairs={{0,2},{1,3},{2,0},{3,1},{4,6},{5,7},{6,4},{7,5},{8,10},{9,11},{10,... | collective-permute-start | bytes 1572872 | tf_op jit(solution)/shard_map/ppermute | solution.py:103
  26.6 25.0 %collective-permute-start.2 = (bf16[256,1024]{1,0:T(8,128)(2,1)}, bf16[256,1024]{1,0:T(8,128)(2,1)}, u32[]{:S(2)}, u32[]{:S(2)}) collective-permute-start(bf16[256,1024]{1,0:T(8,128)(2,1)} %get-tuple-element.9), channel_id=1, source_target_pairs={{0,3},{1,0},{2,1},{3,2},{4,7},{5,4},{6,5},{7,6},{8,11},{9,8},{10,9... | collective-permute-start | bytes 1572872 | tf_op jit(solution)/shard_map/ppermute | solution.py:103
  28.9 27.8 %collective-permute-start.6 = (bf16[256,1024]{1,0:T(8,128)(2,1)}, bf16[256,1024]{1,0:T(8,128)(2,1)S(1)}, u32[]{:S(2)}, u32[]{:S(2)}) collective-permute-start(bf16[256,1024]{1,0:T(8,128)(2,1)} %get-tuple-element.11), channel_id=1, source_target_pairs={{0,4},{1,5},{2,6},{3,7},{4,8},{5,9},{6,10},{7,11},{8,12},{9,13},{1... | collective-permute-start | bytes 1572872 | tf_op jit(solution)/shard_map/ppermute | solution.py:103
  30.8 28.4 %collective-permute-start.7 = (bf16[256,1024]{1,0:T(8,128)(2,1)}, bf16[256,1024]{1,0:T(8,128)(2,1)}, u32[]{:S(2)}, u32[]{:S(2)}) collective-permute-start(bf16[256,1024]{1,0:T(8,128)(2,1)} %get-tuple-element.13), channel_id=1, source_target_pairs={{0,8},{1,9},{2,10},{3,11},{4,12},{5,13},{6,14},{7,15},{8,0},{9,1},... | collective-permute-start | bytes 1572872 | tf_op jit(solution)/shard_map/ppermute | solution.py:103
  40.5 28.5 %copy-start.3 = (f32[64,2048]{1,0:T(8,128)S(1)}, f32[64,2048]{1,0:T(8,128)}, u32[]{:S(2)}) copy-start(f32[64,2048]{1,0:T(8,128)} %param.32) | copy-start | bytes 1572868
  40.5 28.6 %copy-start.10 = (f32[2048]{0:T(1024)S(1)}, f32[2048]{0:T(1024)}, u32[]{:S(2)}) copy-start(f32[2048]{0:T(1024)} %param.34) | copy-start | bytes 24580
  40.5 18.8 %collective-permute-start.8 = (bf16[256,1024]{1,0:T(8,128)(2,1)}, bf16[256,1024]{1,0:T(8,128)(2,1)S(1)}, u32[]{:S(2)}, u32[]{:S(2)}) collective-permute-start(bf16[256,1024]{1,0:T(8,128)(2,1)} %get-tuple-element.12), channel_id=1, source_target_pairs={{0,12},{1,13},{2,14},{3,15},{4,0},{5,1},{6,2},{7,3},{8,4},{9,5},{1... | collective-permute-start | bytes 1572872 | tf_op jit(solution)/shard_map/ppermute | solution.py:103
  53.5 9.9 %collective-permute-start.3 = (bf16[64,1024]{1,0:T(8,128)(2,1)S(1)}, bf16[64,1024]{1,0:T(8,128)(2,1)S(1)}, u32[]{:S(2)}, u32[]{:S(2)}) collective-permute-start(bf16[64,1024]{1,0:T(8,128)(2,1)S(1)} %get-tuple-element.16), channel_id=1, source_target_pairs={{0,4},{1,5},{2,6},{3,7},{4,8},{5,9},{6,10},{7,11},{8,12},{9,13},{1... | collective-permute-start | bytes 393224 | tf_op jit(solution)/shard_map/ppermute | solution.py:103
  55.5 8.3 %collective-permute-start.4 = (bf16[64,1024]{1,0:T(8,128)(2,1)S(1)}, bf16[64,1024]{1,0:T(8,128)(2,1)S(1)}, u32[]{:S(2)}, u32[]{:S(2)}) collective-permute-start(bf16[64,1024]{1,0:T(8,128)(2,1)S(1)} %get-tuple-element.18), channel_id=1, source_target_pairs={{0,8},{1,9},{2,10},{3,11},{4,12},{5,13},{6,14},{7,15},{8,0},{9,1},... | collective-permute-start | bytes 393224 | tf_op jit(solution)/shard_map/ppermute | solution.py:103
  56.7 7.1 %collective-permute-start.5 = (bf16[64,1024]{1,0:T(8,128)(2,1)S(1)}, bf16[64,1024]{1,0:T(8,128)(2,1)S(1)}, u32[]{:S(2)}, u32[]{:S(2)}) collective-permute-start(bf16[64,1024]{1,0:T(8,128)(2,1)S(1)} %get-tuple-element.17), channel_id=1, source_target_pairs={{0,12},{1,13},{2,14},{3,15},{4,0},{5,1},{6,2},{7,3},{8,4},{9,5},{1... | collective-permute-start | bytes 393224 | tf_op jit(solution)/shard_map/ppermute | solution.py:103
  60.8 6.7 %collective-permute-start.10 = (bf16[64,1024]{1,0:T(8,128)(2,1)S(1)}, bf16[64,1024]{1,0:T(8,128)(2,1)S(1)}, u32[]{:S(2)}, u32[]{:S(2)}) collective-permute-start(bf16[64,1024]{1,0:T(8,128)(2,1)S(1)} %get-tuple-element.21), channel_id=1, source_target_pairs={{0,2},{1,3},{2,0},{3,1},{4,6},{5,7},{6,4},{7,5},{8,10},{9,11},{10,... | collective-permute-start | bytes 393224 | tf_op jit(solution)/shard_map/ppermute | solution.py:103
  61.8 6.7 %collective-permute-start.11 = (bf16[64,1024]{1,0:T(8,128)(2,1)S(1)}, bf16[64,1024]{1,0:T(8,128)(2,1)S(1)}, u32[]{:S(2)}, u32[]{:S(2)}) collective-permute-start(bf16[64,1024]{1,0:T(8,128)(2,1)S(1)} %get-tuple-element.20), channel_id=1, source_target_pairs={{0,3},{1,0},{2,1},{3,2},{4,7},{5,4},{6,5},{7,6},{8,11},{9,8},{10,9... | collective-permute-start | bytes 393224 | tf_op jit(solution)/shard_map/ppermute | solution.py:103
  63.4 5.4 %collective-permute-start.9 = (bf16[64,1024]{1,0:T(8,128)(2,1)S(1)}, bf16[64,1024]{1,0:T(8,128)(2,1)S(1)}, u32[]{:S(2)}, u32[]{:S(2)}) collective-permute-start(bf16[64,1024]{1,0:T(8,128)(2,1)S(1)} %get-tuple-element.19), channel_id=1, source_target_pairs={{0,1},{1,2},{2,3},{3,0},{4,5},{5,6},{6,7},{7,4},{8,9},{9,10},{10,1... | collective-permute-start | bytes 393224 | tf_op jit(solution)/shard_map/ppermute | solution.py:103
  71.5 101.6 %copy-start.16 = (bf16[1,2048,512]{2,1,0:T(8,128)(2,1)S(1)}, bf16[1,2048,512]{2,1,0:T(8,128)(2,1)}, u32[]{:S(2)}) copy-start(bf16[1,2048,512]{2,1,0:T(8,128)(2,1)} %param.38) | copy-start | bytes 6291460
  71.5 101.6 %copy-start.17 = (bf16[1,2048,512]{2,1,0:T(8,128)(2,1)S(1)}, bf16[1,2048,512]{2,1,0:T(8,128)(2,1)}, u32[]{:S(2)}) copy-start(bf16[1,2048,512]{2,1,0:T(8,128)(2,1)} %param.37) | copy-start | bytes 6291460
  195.1 9.0 %copy-start.12 = (f32[64,8]{0,1:T(8,128)S(1)}, f32[64,8]{0,1:T(8,128)}, u32[]{:S(2)}) copy-start(f32[64,8]{0,1:T(8,128)} %param.36) | copy-start | bytes 6148
  195.1 10.5 %copy-start.14 = (s32[16]{0:T(128)S(1)}, s32[16]{0:T(128)}, u32[]{:S(2)}) copy-start(s32[16]{0:T(128)} %param.31) | copy-start | bytes 196
  195.1 119.6 %all-to-all-start.1 = ((bf16[128,16,2048]{2,1,0:T(8,128)(2,1)}), bf16[128,16,2048]{2,1,0:T(8,128)(2,1)}, u32[]{:S(2)}, u32[]{:S(2)}) async-start(bf16[128,16,2048]{2,1,0:T(8,128)(2,1)} %bitcast.118), calls=%async_computation.1 | async-start | bytes 16777216 | tf_op jit(solution)/shard_map/all_to_all | solution.py:210
  (8 other events, 16.8 us)

commit v11 on v5

--- a/solution.py
+++ b/solution.py
@@ -208,13 +208,13 @@
     returned = lax.all_to_all(produced, ("req", "exp"), split_axis=0, concat_axis=0, tiled=True)
     weighing = jnp.sum(jnp.where(hits, route_weights[:, :, None], 0.0), axis=1)
     terms = []
-    for _ in range(3):
+    for _ in range(2):
         term = weighing.astype(jnp.bfloat16)
         terms.append(term)
         weighing = weighing - term.astype(jnp.float32)
     terms = jnp.concatenate(terms, axis=0)
     moe = jnp.dot(terms, returned.reshape(-1, model_width), preferred_element_type=jnp.float32)
-    moe = jnp.sum(moe.reshape(3, tok_rows, model_width), axis=0)
+    moe = jnp.sum(moe.reshape(2, tok_rows, model_width), axis=0)
     hidden_out = (middle + moe).astype(jnp.bfloat16)
     return (hidden_out, accepted_keys, accepted_values)
 

time: 314 us -> 315 us (level)
  no operation moved by 1% of the time
where the time goes in v11:
time: 315 us
  waiting for transfers between devices  126 us (40%)
  blocking collectives  102 us (32%)
  matrix products  41.7 us (13%)
  starting transfers between devices  24 us (8%)
  other arithmetic  11.6 us (4%)
  local copies, waits for them, and re-layouts  8.37 us (3%)
    all_to_all x1, waiting for transfers between devices, per_device(): lax.all_to_all(produced, ('req', 'exp'), split_axis=0, concat_axis=0, til...  105 us
    all_to_all x1, blocking collectives, per_device(): lax.all_to_all(outgoing, ('req', 'exp'), split_axis=0, concat_axis=0, til...  102 us
    ppermute x12, waiting for transfers between devices, ring_sum(): total = total + lax.ppermute(blocks[step], 'exp', pairs).astype(jnp.float32)  21.1 us
    ppermute x12, starting transfers between devices, ring_sum(): total = total + lax.ppermute(blocks[step], 'exp', pairs).astype(jnp.float32)  15 us
    all_to_all x1, starting transfers between devices, per_device(): lax.all_to_all(produced, ('req', 'exp'), split_axis=0, concat_axis=0, til...  9.02 us
    dot_general x1, matrix products, expert_rows(): jnp.dot(activation, expert_down, preferred_element_type=jnp.float32)  6.73 us
  transfers between devices with their start and end apart: 13, of which 7 were waited for; matrix products, arithmetic and copies ran while one was open for 4% of the time, Pallas kernels for 0%

profile of v11, /device:TPU:60, one launch (start us, length us, event | category | flops | bytes accessed | tf_op | source)
XLA Modules:
  0.0 314.8 jit_solution(17229959407404589592)
XLA Ops:
  0.7 1.8 fusion.25
  3.8 1.6 fusion.114
  6.8 3.7 %fusion.7 = (f32[15,64]{1,0:T(8,128)S(1)}, f32[15,64,1024]{2,1,0:T(8,128)S(1)}) fusion(pred[15,1024]{1,0:T(8,128)(4,1)S(1)} %iota_compare_fusion.5, bf16[16,64,128]{2,1,0:T(8,128)(2,1)S(1)} %copy-done.11, bf16[15,1024,128]{2,1,0:T(8,128)(2,1)} %param.27), kind=kOutput, calls=%fused_computation.18 | convolution fusion | flops 254606400 | bytes 8145664 | tf_op jit(solution)/shard_map/bthe,blhe->bhtl/dot_general | solution.py:51
  14.8 1.7 fusion.115
  28.9 1.9 collective-permute-start.6
  32.7 1.9 compare_reduce_fusion
  34.6 5.0 %collective-permute-done = bf16[256,1024]{1,0:T(8,128)(2,1)S(1)} collective-permute-done((bf16[256,1024]{1,0:T(8,128)(2,1)}, bf16[256,1024]{1,0:T(8,128)(2,1)S(1)}, u32[]{:S(2)}, u32[]{:S(2)}) %collective-permute-start) | collective-permute-done | bytes 524320 | tf_op jit(solution)/shard_map/ppermute | solution.py:101
  40.6 9.2 %collective-permute-done.1 = bf16[256,1024]{1,0:T(8,128)(2,1)} collective-permute-done((bf16[256,1024]{1,0:T(8,128)(2,1)}, bf16[256,1024]{1,0:T(8,128)(2,1)}, u32[]{:S(2)}, u32[]{:S(2)}) %collective-permute-start.1) | collective-permute-done | bytes 524320 | tf_op jit(solution)/shard_map/ppermute | solution.py:101
  49.8 1.8 collective-permute-done.2
  51.6 1.9 fusion.41
  53.5 2.0 collective-permute-start.3
  56.7 2.5 collective-permute-start.5
  59.2 1.6 fusion.38
  61.8 1.7 collective-permute-start.11
  63.9 3.6 %collective-permute-done.10 = bf16[64,1024]{1,0:T(8,128)(2,1)S(1)} collective-permute-done((bf16[64,1024]{1,0:T(8,128)(2,1)S(1)}, bf16[64,1024]{1,0:T(8,128)(2,1)S(1)}, u32[]{:S(2)}, u32[]{:S(2)}) %collective-permute-start.10) | collective-permute-done | bytes 131104 | tf_op jit(solution)/shard_map/ppermute | solution.py:101
  69.1 2.4 convolution_convert_fusion.1
  71.5 101.5 %all_to_all.10 = bf16[128,16,2048]{2,1,0:T(8,128)(2,1)S(1)} all-to-all(bf16[128,16,2048]{2,1,0:T(8,128)(2,1)S(1)} %bitcast.119), channel_id=1, replica_groups=mesh['req'=8,'exp'=16] {'req','exp'}, dimensions={0} | all-to-all | bytes 16777216 | tf_op jit(solution)/shard_map/all_to_all | solution.py:204
  173.1 4.5 %fusion.13 = f32[2048,512]{1,0:T(8,128)S(1)} fusion(bf16[2048,2048]{1,0:T(8,128)(2,1)S(1)} %bitcast.125, bf16[1,2048,512]{2,1,0:T(8,128)(2,1)S(1)} %copy-done.16), kind=kOutput, calls=%fused_computation.23 | convolution fusion | flops 4294967296 | bytes 14680064 | tf_op jit(solution)/shard_map/dot_general | solution.py:92
  177.6 5.2 %multiply_convert_fusion = bf16[2048,512]{1,0:T(8,128)(2,1)S(1)} fusion(f32[2048,512]{1,0:T(8,128)S(1)} %fusion.13, bf16[2048,2048]{1,0:T(8,128)(2,1)S(1)} %bitcast.126, bf16[1,2048,512]{2,1,0:T(8,128)(2,1)S(1)} %copy-done.17), kind=kOutput, calls=%fused_computation.12 | convolution fusion | flops 4301258752 | bytes 16777216 | tf_op jit(solution)/shard_map/dot_general | solution.py:93
  182.8 6.7 %convolution_convert_fusion = bf16[2048,2048]{1,0:T(8,128)(2,1)} fusion(bf16[2048,512]{1,0:T(8,128)(2,1)S(1)} %multiply_convert_fusion, bf16[1,512,2048]{2,1,0:T(8,128)(2,1)S(1)} %copy-done), kind=kOutput, calls=%fused_computation.4 | convolution fusion | flops 4299161600 | bytes 12582912 | tf_op jit(solution)/shard_map/dot_general | solution.py:95
  189.5 9.0 %all-to-all-start.1 = ((bf16[128,16,2048]{2,1,0:T(8,128)(2,1)}), bf16[128,16,2048]{2,1,0:T(8,128)(2,1)}, u32[]{:S(2)}, u32[]{:S(2)}) async-start(bf16[128,16,2048]{2,1,0:T(8,128)(2,1)} %bitcast.124), calls=%async_computation.1 | async-start | bytes 16777216 | tf_op jit(solution)/shard_map/all_to_all | solution.py:208
  202.2 1.4 convolution_convert_fusion.4
  204.6 104.5 %all-to-all-done.1 = bf16[128,16,2048]{2,1,0:T(8,128)(2,1)} async-done(((bf16[128,16,2048]{2,1,0:T(8,128)(2,1)}), bf16[128,16,2048]{2,1,0:T(8,128)(2,1)}, u32[]{:S(2)}, u32[]{:S(2)}) %all-to-all-start.1) | async-done | bytes 8388640 | tf_op jit(solution)/shard_map/all_to_all | solution.py:208
  309.1 4.9 %convolution_reduce_fusion = f32[64,2048]{1,0:T(8,128)S(1)} fusion(bf16[2,64,2048]{2,1,0:T(8,128)(2,1)} %bitcast.127, bf16[2048,2048,1]{1,0,2:T(8,128)(2,1)} %bitcast.35), kind=kOutput, calls=%fused_computation.34 | convolution fusion | flops 1073872896 | bytes 9437184 | tf_op jit(solution)/shard_map/dot_general | solution.py:216
  (118 shorter events, 30.7 us)
Async XLA Ops:
  0.6 182.2 %copy-start = (bf16[1,512,2048]{2,1,0:T(8,128)(2,1)S(1)}, bf16[1,512,2048]{2,1,0:T(8,128)(2,1)}, u32[]{:S(2)}) copy-start(bf16[1,512,2048]{2,1,0:T(8,128)(2,1)} %param.39) | copy-start | bytes 6291460
  0.6 4.7 %copy-start.11 = (bf16[16,64,128]{2,1,0:T(8,128)(2,1)S(1)}, bf16[16,64,128]{2,1,0:T(8,128)(2,1)}, u32[]{:S(2)}) copy-start(bf16[16,64,128]{2,1,0:T(8,128)(2,1)} %param.21) | copy-start | bytes 786436
  0.7 6.0 %copy-start.13 = (s32[15]{0:T(128)S(1)}, s32[15]{0:T(128)}, u32[]{:S(2)}) copy-start(s32[15]{0:T(128)} %param.29) | copy-start | bytes 184
  22.4 6.5 %copy-start.1 = (bf16[1024,1024]{1,0:T(8,128)(2,1)}, bf16[1024,1024]{1,0:T(8,128)(2,1)S(1)}, u32[]{:S(2)}) copy-start(bf16[1024,1024]{1,0:T(8,128)(2,1)S(1)} %convolution_convert_fusion.2) | copy-start | bytes 6291460
  22.5 9.4 %copy-start.9 = (s32[64,8]{0,1:T(8,128)S(1)}, s32[64,8]{0,1:T(8,128)}, u32[]{:S(2)}) copy-start(s32[64,8]{0,1:T(8,128)} %param.35) | copy-start | bytes 6148
  23.2 5.7 %copy-start.2 = (bf16[1024,1024]{1,0:T(8,128)(2,1)}, bf16[1024,1024]{1,0:T(8,128)(2,1)S(1)}, u32[]{:S(2)}) copy-start(bf16[1024,1024]{1,0:T(8,128)(2,1)S(1)} %convolution_convert_fusion.3) | copy-start | bytes 6291460
  24.6 15.0 %collective-permute-start = (bf16[256,1024]{1,0:T(8,128)(2,1)}, bf16[256,1024]{1,0:T(8,128)(2,1)S(1)}, u32[]{:S(2)}, u32[]{:S(2)}) collective-permute-start(bf16[256,1024]{1,0:T(8,128)(2,1)} %get-tuple-element.10), channel_id=1, source_target_pairs={{0,1},{1,2},{2,3},{3,0},{4,5},{5,6},{6,7},{7,4},{8,9},{9,10},{10,1... | collective-permute-start | bytes 1572872 | tf_op jit(solution)/shard_map/ppermute | solution.py:101
  25.8 24.0 %collective-permute-start.1 = (bf16[256,1024]{1,0:T(8,128)(2,1)}, bf16[256,1024]{1,0:T(8,128)(2,1)}, u32[]{:S(2)}, u32[]{:S(2)}) collective-permute-start(bf16[256,1024]{1,0:T(8,128)(2,1)} %get-tuple-element.12), channel_id=1, source_target_pairs={{0,2},{1,3},{2,0},{3,1},{4,6},{5,7},{6,4},{7,5},{8,10},{9,11},{10,... | collective-permute-start | bytes 1572872 | tf_op jit(solution)/shard_map/ppermute | solution.py:101
  26.6 25.0 %collective-permute-start.2 = (bf16[256,1024]{1,0:T(8,128)(2,1)}, bf16[256,1024]{1,0:T(8,128)(2,1)}, u32[]{:S(2)}, u32[]{:S(2)}) collective-permute-start(bf16[256,1024]{1,0:T(8,128)(2,1)} %get-tuple-element.11), channel_id=1, source_target_pairs={{0,3},{1,0},{2,1},{3,2},{4,7},{5,4},{6,5},{7,6},{8,11},{9,8},{10,9... | collective-permute-start | bytes 1572872 | tf_op jit(solution)/shard_map/ppermute | solution.py:101
  28.9 27.8 %collective-permute-start.6 = (bf16[256,1024]{1,0:T(8,128)(2,1)}, bf16[256,1024]{1,0:T(8,128)(2,1)S(1)}, u32[]{:S(2)}, u32[]{:S(2)}) collective-permute-start(bf16[256,1024]{1,0:T(8,128)(2,1)} %get-tuple-element.13), channel_id=1, source_target_pairs={{0,4},{1,5},{2,6},{3,7},{4,8},{5,9},{6,10},{7,11},{8,12},{9,13},{1... | collective-permute-start | bytes 1572872 | tf_op jit(solution)/shard_map/ppermute | solution.py:101
  30.8 28.4 %collective-permute-start.7 = (bf16[256,1024]{1,0:T(8,128)(2,1)}, bf16[256,1024]{1,0:T(8,128)(2,1)}, u32[]{:S(2)}, u32[]{:S(2)}) collective-permute-start(bf16[256,1024]{1,0:T(8,128)(2,1)} %get-tuple-element.15), channel_id=1, source_target_pairs={{0,8},{1,9},{2,10},{3,11},{4,12},{5,13},{6,14},{7,15},{8,0},{9,1},... | collective-permute-start | bytes 1572872 | tf_op jit(solution)/shard_map/ppermute | solution.py:101
  40.5 28.5 %copy-start.3 = (f32[64,2048]{1,0:T(8,128)S(1)}, f32[64,2048]{1,0:T(8,128)}, u32[]{:S(2)}) copy-start(f32[64,2048]{1,0:T(8,128)} %param.32) | copy-start | bytes 1572868
  40.5 28.6 %copy-start.10 = (f32[2048]{0:T(1024)S(1)}, f32[2048]{0:T(1024)}, u32[]{:S(2)}) copy-start(f32[2048]{0:T(1024)} %param.34) | copy-start | bytes 24580
  40.5 18.8 %collective-permute-start.8 = (bf16[256,1024]{1,0:T(8,128)(2,1)}, bf16[256,1024]{1,0:T(8,128)(2,1)S(1)}, u32[]{:S(2)}, u32[]{:S(2)}) collective-permute-start(bf16[256,1024]{1,0:T(8,128)(2,1)} %get-tuple-element.14), channel_id=1, source_target_pairs={{0,12},{1,13},{2,14},{3,15},{4,0},{5,1},{6,2},{7,3},{8,4},{9,5},{1... | collective-permute-start | bytes 1572872 | tf_op jit(solution)/shard_map/ppermute | solution.py:101
  53.5 9.9 %collective-permute-start.3 = (bf16[64,1024]{1,0:T(8,128)(2,1)S(1)}, bf16[64,1024]{1,0:T(8,128)(2,1)S(1)}, u32[]{:S(2)}, u32[]{:S(2)}) collective-permute-start(bf16[64,1024]{1,0:T(8,128)(2,1)S(1)} %get-tuple-element.18), channel_id=1, source_target_pairs={{0,4},{1,5},{2,6},{3,7},{4,8},{5,9},{6,10},{7,11},{8,12},{9,13},{1... | collective-permute-start | bytes 393224 | tf_op jit(solution)/shard_map/ppermute | solution.py:101
  55.5 8.3 %collective-permute-start.4 = (bf16[64,1024]{1,0:T(8,128)(2,1)S(1)}, bf16[64,1024]{1,0:T(8,128)(2,1)S(1)}, u32[]{:S(2)}, u32[]{:S(2)}) collective-permute-start(bf16[64,1024]{1,0:T(8,128)(2,1)S(1)} %get-tuple-element.20), channel_id=1, source_target_pairs={{0,8},{1,9},{2,10},{3,11},{4,12},{5,13},{6,14},{7,15},{8,0},{9,1},... | collective-permute-start | bytes 393224 | tf_op jit(solution)/shard_map/ppermute | solution.py:101
  56.7 7.1 %collective-permute-start.5 = (bf16[64,1024]{1,0:T(8,128)(2,1)S(1)}, bf16[64,1024]{1,0:T(8,128)(2,1)S(1)}, u32[]{:S(2)}, u32[]{:S(2)}) collective-permute-start(bf16[64,1024]{1,0:T(8,128)(2,1)S(1)} %get-tuple-element.19), channel_id=1, source_target_pairs={{0,12},{1,13},{2,14},{3,15},{4,0},{5,1},{6,2},{7,3},{8,4},{9,5},{1... | collective-permute-start | bytes 393224 | tf_op jit(solution)/shard_map/ppermute | solution.py:101
  60.8 6.7 %collective-permute-start.10 = (bf16[64,1024]{1,0:T(8,128)(2,1)S(1)}, bf16[64,1024]{1,0:T(8,128)(2,1)S(1)}, u32[]{:S(2)}, u32[]{:S(2)}) collective-permute-start(bf16[64,1024]{1,0:T(8,128)(2,1)S(1)} %get-tuple-element.23), channel_id=1, source_target_pairs={{0,2},{1,3},{2,0},{3,1},{4,6},{5,7},{6,4},{7,5},{8,10},{9,11},{10,... | collective-permute-start | bytes 393224 | tf_op jit(solution)/shard_map/ppermute | solution.py:101
  61.8 6.7 %collective-permute-start.11 = (bf16[64,1024]{1,0:T(8,128)(2,1)S(1)}, bf16[64,1024]{1,0:T(8,128)(2,1)S(1)}, u32[]{:S(2)}, u32[]{:S(2)}) collective-permute-start(bf16[64,1024]{1,0:T(8,128)(2,1)S(1)} %get-tuple-element.22), channel_id=1, source_target_pairs={{0,3},{1,0},{2,1},{3,2},{4,7},{5,4},{6,5},{7,6},{8,11},{9,8},{10,9... | collective-permute-start | bytes 393224 | tf_op jit(solution)/shard_map/ppermute | solution.py:101
  63.4 5.4 %collective-permute-start.9 = (bf16[64,1024]{1,0:T(8,128)(2,1)S(1)}, bf16[64,1024]{1,0:T(8,128)(2,1)S(1)}, u32[]{:S(2)}, u32[]{:S(2)}) collective-permute-start(bf16[64,1024]{1,0:T(8,128)(2,1)S(1)} %get-tuple-element.21), channel_id=1, source_target_pairs={{0,1},{1,2},{2,3},{3,0},{4,5},{5,6},{6,7},{7,4},{8,9},{9,10},{10,1... | collective-permute-start | bytes 393224 | tf_op jit(solution)/shard_map/ppermute | solution.py:101
  71.5 101.5 %copy-start.16 = (bf16[1,2048,512]{2,1,0:T(8,128)(2,1)S(1)}, bf16[1,2048,512]{2,1,0:T(8,128)(2,1)}, u32[]{:S(2)}) copy-start(bf16[1,2048,512]{2,1,0:T(8,128)(2,1)} %param.37) | copy-start | bytes 6291460
  189.5 9.0 %copy-start.12 = (f32[64,8]{0,1:T(8,128)S(1)}, f32[64,8]{0,1:T(8,128)}, u32[]{:S(2)}) copy-start(f32[64,8]{0,1:T(8,128)} %param.36) | copy-start | bytes 6148
  189.5 10.5 %copy-start.14 = (s32[16]{0:T(128)S(1)}, s32[16]{0:T(128)}, u32[]{:S(2)}) copy-start(s32[16]{0:T(128)} %param.31) | copy-start | bytes 196
  189.5 119.6 %all-to-all-start.1 = ((bf16[128,16,2048]{2,1,0:T(8,128)(2,1)}), bf16[128,16,2048]{2,1,0:T(8,128)(2,1)}, u32[]{:S(2)}, u32[]{:S(2)}) async-start(bf16[128,16,2048]{2,1,0:T(8,128)(2,1)} %bitcast.124), calls=%async_computation.1 | async-start | bytes 16777216 | tf_op jit(solution)/shard_map/all_to_all | solution.py:208
  (8 other events, 16.6 us)
